TPU v7x, 128 devices: a whole 4x4x4 slice. The times are simulated.
128 devices in a mesh: expert: 32 (over y, z, core), hidden: 4 (over x).
Axes of the slice: x: 4, y: 4, z: 4, core: 2. Of those that a mesh axis runs over, the one named last changes fastest.
Arguments:
- tokens: bfloat16 [2048, 7168], P('expert'), may hold values from -6 to 6
- expert_ids: int32 [2048, 8], replicated, may hold values from 0 to 31, all different within a row; in each aligned block of 64 rows (0 to 63, 64 to 127, ...) at most 24 rows name the same one
- gate_weight: bfloat16 [32, 7168, 2048], P('expert', None, 'hidden')
- up_weight: bfloat16 [32, 7168, 2048], P('expert', None, 'hidden')
Outputs:
- expert_hidden: bfloat16 [32, 32, 24, 2048], P('expert', None, None, 'hidden')
Inputs may be any that keep to these rules, and one draw needn't show every extreme that they name: `expert_ids`: each row names 8 different experts; among the rows of one device no expert is named more than 24 times, and in every draw some expert is named exactly 24 times there.
All inputs are finite; a program needn't handle non-finite values.
Results may differ from a plain program's by a relative error of at most 0.0058.
Values may be sent and summed in bfloat16 or wider, within the bound.
No kernel may reach another device: no remote copies, remote signals or barrier semaphores. Data moves between devices by JAX's collectives and lax.ppermute only.
A program may use at most 192 MiB of HBM per device.

v0:
```python
import jax
import jax.numpy as jnp
from jax import lax
from jax.sharding import PartitionSpec as P

TOPK = 8
EXPERTS = 32
SWEEPS = 5
TOK_DEV = 64
CAP = 24
HANDOFF = 2


EPS = 1e-06


def dispatch_rows(block_ids, tokens, first_slot, slots):
    tok_local, topk = block_ids.shape
    flat_ids = block_ids.reshape(-1)
    onehot = (flat_ids[:, None] == jnp.arange(EXPERTS, dtype=jnp.int32)[None, :]).astype(jnp.int32)
    before = jnp.cumsum(onehot, axis=0) - onehot
    my_rank = jnp.sum(before * onehot, axis=1) - first_slot
    pair_ids = flat_ids.reshape(tok_local, topk)
    pair_rank = my_rank.reshape(tok_local, topk)
    hit = (pair_ids[None, None] == jnp.arange(EXPERTS, dtype=jnp.int32)[:, None, None, None]) & (
        pair_rank[None, None] == jnp.arange(slots, dtype=jnp.int32)[None, :, None, None]
    )
    select = jnp.any(hit, axis=3).astype(tokens.dtype)
    rows = jnp.einsum("est,td->esd", select, tokens, preferred_element_type=jnp.float32)
    return rows.astype(tokens.dtype)[:, None]


def hidden_sum(values):
    n = lax.axis_size("hidden")
    total = values
    for shift in range(1, n):
        total = total + lax.ppermute(values, "hidden", [(i, (i + shift) % n) for i in range(n)])
    return total


def row_terms(weight, cols_sq):
    values = weight.astype(jnp.float32)
    return jnp.sum(values * values * cols_sq[:, None, :], axis=2)


def col_terms(weight, scale_sq):
    values = weight.astype(jnp.float32)
    return jnp.sum(values * values * scale_sq[:, :, None], axis=1)


def shards(tokens, expert_ids, gate_weight, up_weight):
    exp_local = gate_weight.shape[0]
    width = gate_weight.shape[1]
    ff_local = gate_weight.shape[2]
    n_hidden = lax.axis_size("hidden")
    ff_total = ff_local * n_hidden
    my_index = lax.axis_index("expert")
    parity = lax.axis_index("hidden") % 2
    half = CAP // 2

    tok_local = tokens.shape[0]
    block_ids = lax.dynamic_slice_in_dim(expert_ids, my_index * tok_local, tok_local, 0)
    outgoing = dispatch_rows(block_ids, tokens, parity * half, half)
    mine = lax.all_to_all(outgoing, "expert", split_axis=0, concat_axis=1, tiled=True)

    def sweep(_, carry):
        gate_cols, up_cols, _ = carry
        partial_rows = row_terms(gate_weight, gate_cols * gate_cols) + row_terms(
            up_weight, up_cols * up_cols
        )
        row_sums = hidden_sum(partial_rows)
        row_scale = lax.rsqrt(width * row_sums / (2 * ff_total) + EPS)
        scale_sq = row_scale * row_scale
        gate_cols = lax.rsqrt(col_terms(gate_weight, scale_sq) + EPS)
        up_cols = lax.rsqrt(col_terms(up_weight, scale_sq) + EPS)
        return gate_cols, up_cols, row_scale

    carry = (
        jnp.ones((exp_local, ff_local), jnp.float32),
        jnp.ones((exp_local, ff_local), jnp.float32),
        jnp.ones((exp_local, width), jnp.float32),
    )
    for step in range(HANDOFF):
        carry = sweep(step, carry)
    mine, carry = lax.optimization_barrier((mine, carry))
    quarter = half // 2
    from_next = lax.ppermute(
        mine[:, :, :quarter], "hidden", [(i, (i - 1) % n_hidden) for i in range(n_hidden)]
    )
    from_prev = lax.ppermute(
        mine[:, :, quarter:], "hidden", [(i, (i + 1) % n_hidden) for i in range(n_hidden)]
    )
    other = jnp.concatenate([from_next, from_prev], axis=2)
    gate_cols, up_cols, row_scale = lax.fori_loop(HANDOFF, SWEEPS, sweep, carry)
    gate_eq = (
        gate_weight.astype(jnp.float32) * row_scale[:, :, None] * gate_cols[:, None, :]
    ).astype(jnp.bfloat16)
    up_eq = (up_weight.astype(jnp.float32) * row_scale[:, :, None] * up_cols[:, None, :]).astype(
        jnp.bfloat16
    )

    def expert_mlp(rows):
        gate_act = jnp.einsum("ensd,edf->ensf", rows, gate_eq, preferred_element_type=jnp.float32)
        up_act = jnp.einsum("ensd,edf->ensf", rows, up_eq, preferred_element_type=jnp.float32)
        return (jax.nn.silu(gate_act) * up_act).astype(jnp.bfloat16)

    res_mine = expert_mlp(mine)
    res_other = expert_mlp(other)
    low = jnp.where(parity == 0, res_mine, res_other)
    high = jnp.where(parity == 0, res_other, res_mine)
    return jnp.concatenate([low, high], axis=2)


def solution(mesh):
    in_specs = (P("expert", None), P(), P("expert", None, "hidden"), P("expert", None, "hidden"))
    out_specs = P("expert", None, None, "hidden")
    return jax.shard_map(shards, mesh=mesh, in_specs=in_specs, out_specs=out_specs, check_vma=False)
```

profile of v0, /device:TPU:48, one launch (start us, length us, event | category | flops | bytes accessed | tf_op | source)
XLA Modules:
  0.0 315.4 jit_solution(10510829208944157312)
XLA Ops:
  0.0 8.2 %fusion.3 = (f32[7168]{0:T(1024)S(1)}, f32[7168]{0:T(1024)S(1)}) fusion(bf16[1,7168,512]{2,1,0:T(8,128)(2,1)} %param.9, bf16[1,7168,512]{2,1,0:T(8,128)(2,1)} %param.8), kind=kLoop, calls=%fused_computation.14 | loop fusion | flops 22005760 | bytes 14737408 | tf_op jit(solution)/shard_map/reduce_sum | solution.py:43
  8.2 1.6 collective-permute-start.3
  9.8 2.7 collective-permute-start.4
  17.3 1.6 fusion.18
  18.9 6.1 %copy.24 = bf16[32,1,12,7168]{3,2,1,0:T(8,128)(2,1)} copy(bf16[32,1,12,7168]{3,0,2,1:T(8,128)(2,1)S(1)} %fusion.18) | data formatting | bytes 11010048 | tf_op jit(solution)/shard_map/broadcast_in_dim | solution.py:30
  25.0 8.5 %all-to-all-start = ((bf16[32,1,12,7168]{3,2,1,0:T(8,128)(2,1)}), bf16[32,1,12,7168]{3,2,1,0:T(8,128)(2,1)}, u32[]{:S(2)}, u32[]{:S(2)}) async-start(bf16[32,1,12,7168]{3,2,1,0:T(8,128)(2,1)} %copy.24), calls=%async_computation | async-start | bytes 14680064 | tf_op jit(solution)/shard_map/all_to_all | solution.py:64
  33.6 8.6 %fusion.13 = (f32[512]{0:T(512)S(1)}, f32[512]{0:T(512)S(1)}) fusion(bf16[1,7168,512]{2,1,0:T(8,128)(2,1)} %param.9, f32[7168]{0:T(1024)S(1)} %bitcast.116, bf16[1,7168,512]{2,1,0:T(8,128)(2,1)} %param.8), kind=kLoop, calls=%fused_computation.26 | loop fusion | flops 29359104 | bytes 14712832 | tf_op jit(solution)/shard_map/reduce_sum | solution.py:48
  42.3 5.1 %fusion.14 = f32[7168]{0:T(1024)S(1)} fusion(bf16[1,7168,512]{2,1,0:T(8,128)(2,1)} %param.9, f32[512]{0:T(512)S(1)} %rsqrt_multiply_fusion.1), kind=kLoop, calls=%fused_computation.27 | loop fusion | flops 14672896 | bytes 7370752 | tf_op jit(solution)/shard_map/reduce_sum | solution.py:43
  47.4 2.0 fusion.9
  51.0 1.9 collective-permute-start.8
  52.9 1.8 collective-permute-done.6
  56.4 7.6 %fusion.15 = (f32[512]{0:T(512)S(1)}, f32[512]{0:T(512)S(1)}) fusion(bf16[1,7168,512]{2,1,0:T(8,128)(2,1)} %param.9, f32[7168]{0:T(1024)S(1)} %bitcast.115, bf16[1,7168,512]{2,1,0:T(8,128)(2,1)} %param.8), kind=kLoop, calls=%fused_computation.28 | loop fusion | flops 29359104 | bytes 14712832 | tf_op jit(solution)/shard_map/reduce_sum | solution.py:48
  64.0 79.1 %all-to-all-done = bf16[32,1,12,7168]{3,2,1,0:T(8,128)(2,1)} async-done(((bf16[32,1,12,7168]{3,2,1,0:T(8,128)(2,1)}), bf16[32,1,12,7168]{3,2,1,0:T(8,128)(2,1)}, u32[]{:S(2)}, u32[]{:S(2)}) %all-to-all-start) | async-done | bytes 5505056 | tf_op jit(solution)/shard_map/all_to_all | solution.py:64
  143.1 6.1 %copy.32 = bf16[32,1,12,7168]{3,0,2,1:T(8,128)(2,1)S(1)} copy(bf16[32,1,12,7168]{3,2,1,0:T(8,128)(2,1)} %all-to-all-done) | data formatting | bytes 11010048 | tf_op jit(solution)/shard_map/all_to_all | solution.py:64
  149.3 2.4 copy-done.2
  151.6 2.8 fusion.53
  155.0 15.7 %collective-permute-start.9 = (bf16[1,32,6,7168]{3,1,2,0:T(8,128)(2,1)}, bf16[1,32,6,7168]{3,1,2,0:T(8,128)(2,1)}, u32[]{:S(2)}, u32[]{:S(2)}) collective-permute-start(bf16[1,32,6,7168]{3,1,2,0:T(8,128)(2,1)} %get-tuple-element.115), channel_id=1, source_target_pairs={{0,3},{1,0},{2,1},{3,2},{4,7},{5,4},{6,5},{7,6},{8,11},{9,8},{10,9... | collective-permute-start | bytes 8257544 | tf_op jit(solution)/shard_map/ppermute | solution.py:87
  170.8 119.5 %while.16 = (s32[]{:T(128)}, f32[1,512]{1,0:T(1,128)S(1)}, f32[1,512]{1,0:T(1,128)S(1)}, f32[1,7168]{1,0:T(1,128)}, bf16[1,7168,512]{2,1,0:T(8,128)(2,1)}, /*index=5*/bf16[1,7168,512]{2,1,0:T(8,128)(2,1)}, s32[]{:T(128)}) while((s32[]{:T(128)}, f32[1,512]{1,0:T(1,128)S(1)}, f32[1,512]{1,0:T(1,128)S(1)}, f32[1,7168]{1,0:T(1,128)}, ...), condition=%wide.region_17.18_spmd, body=%wide.region_12.17_spmd.sunk | while | flops 58757120 | bytes 30077124 | solution.py:94
  170.8 9.1 %multiply_reduce_fusion.6 = (f32[7168]{0:T(1024)S(1)}, f32[7168]{0:T(1024)S(1)}) fusion(bf16[1,7168,512]{2,1,0:T(8,128)(2,1)} %get-tuple-element.187, f32[512]{0:T(512)S(1)} %bitcast.113, f32[512]{0:T(512)S(1)} %bitcast.114, bf16[1,7168,512]{2,1,0:T(8,128)(2,1)} %get-tuple-element.186), kind=kLoop, calls=%fused_computation.2.clone.1 | loop fusion | flops 29345792 | bytes 14741504 | tf_op jit(solution)/shard_map/while/body/eval_jaxpr/reduce_sum | solution.py:43
  182.0 48.7 %collective-permute-done = f32[1,7168]{1,0:T(1,128)S(1)} collective-permute-done((f32[1,7168]{1,0:T(1,128)S(1)}, f32[1,7168]{1,0:T(1,128)S(1)}, u32[]{:S(2)}, u32[]{:S(2)}) %collective-permute-start) | collective-permute-done | bytes 28704 | tf_op jit(solution)/shard_map/while/body/eval_jaxpr/ppermute | solution.py:37
  231.4 7.6 %multiply_reduce_fusion.7 = (f32[512]{0:T(512)S(1)}, f32[512]{0:T(512)S(1)}) fusion(bf16[1,7168,512]{2,1,0:T(8,128)(2,1)} %get-tuple-element.187, f32[7168]{0:T(1024)S(1)} %bitcast.100, bf16[1,7168,512]{2,1,0:T(8,128)(2,1)} %get-tuple-element.186), kind=kLoop, calls=%fused_computation.clone.1 | loop fusion | flops 29359104 | bytes 14712832 | tf_op jit(solution)/shard_map/while/body/eval_jaxpr/reduce_sum | solution.py:48
  239.0 9.1 %multiply_reduce_fusion.6 = (f32[7168]{0:T(1024)S(1)}, f32[7168]{0:T(1024)S(1)}) fusion(bf16[1,7168,512]{2,1,0:T(8,128)(2,1)} %get-tuple-element.187, f32[512]{0:T(512)S(1)} %bitcast.113, f32[512]{0:T(512)S(1)} %bitcast.114, bf16[1,7168,512]{2,1,0:T(8,128)(2,1)} %get-tuple-element.186), kind=kLoop, calls=%fused_computation.2.clone.1 | loop fusion | flops 29345792 | bytes 14741504 | tf_op jit(solution)/shard_map/while/body/eval_jaxpr/reduce_sum | solution.py:43
  248.2 3.7 %collective-permute-start = (f32[1,7168]{1,0:T(1,128)S(1)}, f32[1,7168]{1,0:T(1,128)S(1)}, u32[]{:S(2)}, u32[]{:S(2)}) collective-permute-start(f32[1,7168]{1,0:T(1,128)S(1)} %bitcast.101), channel_id=1, source_target_pairs={{0,3},{1,0},{2,1},{3,2},{4,7},{5,4},{6,5},{7,6},{8,11},{9,8},{10,9... | collective-permute-start | bytes 86024 | tf_op jit(solution)/shard_map/while/body/eval_jaxpr/ppermute | solution.py:37
  253.4 3.8 %collective-permute-done.1 = f32[1,7168]{1,0:T(1,128)S(1)} collective-permute-done((f32[1,7168]{1,0:T(1,128)S(1)}, f32[1,7168]{1,0:T(1,128)S(1)}, u32[]{:S(2)}, u32[]{:S(2)}) %collective-permute-start.1) | collective-permute-done | bytes 28704 | tf_op jit(solution)/shard_map/while/body/eval_jaxpr/ppermute | solution.py:37
  258.0 7.6 %multiply_reduce_fusion.7 = (f32[512]{0:T(512)S(1)}, f32[512]{0:T(512)S(1)}) fusion(bf16[1,7168,512]{2,1,0:T(8,128)(2,1)} %get-tuple-element.187, f32[7168]{0:T(1024)S(1)} %bitcast.100, bf16[1,7168,512]{2,1,0:T(8,128)(2,1)} %get-tuple-element.186), kind=kLoop, calls=%fused_computation.clone.1 | loop fusion | flops 29359104 | bytes 14712832 | tf_op jit(solution)/shard_map/while/body/eval_jaxpr/reduce_sum | solution.py:48
  265.6 9.1 %multiply_reduce_fusion.6 = (f32[7168]{0:T(1024)S(1)}, f32[7168]{0:T(1024)S(1)}) fusion(bf16[1,7168,512]{2,1,0:T(8,128)(2,1)} %get-tuple-element.187, f32[512]{0:T(512)S(1)} %bitcast.113, f32[512]{0:T(512)S(1)} %bitcast.114, bf16[1,7168,512]{2,1,0:T(8,128)(2,1)} %get-tuple-element.186), kind=kLoop, calls=%fused_computation.2.clone.1 | loop fusion | flops 29345792 | bytes 14741504 | tf_op jit(solution)/shard_map/while/body/eval_jaxpr/reduce_sum | solution.py:43
  278.7 2.4 collective-permute-done.1
  282.7 7.6 %multiply_reduce_fusion.7 = (f32[512]{0:T(512)S(1)}, f32[512]{0:T(512)S(1)}) fusion(bf16[1,7168,512]{2,1,0:T(8,128)(2,1)} %get-tuple-element.187, f32[7168]{0:T(1024)S(1)} %bitcast.100, bf16[1,7168,512]{2,1,0:T(8,128)(2,1)} %get-tuple-element.186), kind=kLoop, calls=%fused_computation.clone.1 | loop fusion | flops 29359104 | bytes 14712832 | tf_op jit(solution)/shard_map/while/body/eval_jaxpr/reduce_sum | solution.py:48
  290.3 7.9 %fusion.23 = f32[32,12,512]{2,0,1:T(8,128)S(1)} fusion(bf16[1,32,12,7168]{3,1,2,0:T(8,128)(2,1)} %bitcast.98, bf16[1,7168,512]{2,1,0:T(8,128)(2,1)} %get-tuple-element.189, f32[512]{0:T(512)S(1)} %bitcast.107, f32[7168]{0:T(1024)} %bitcast.125), kind=kOutput, calls=%fused_computation.38 | convolution fusion | flops 2833252352 | bytes 13662208 | tf_op jit(solution)/shard_map/ensd,edf->ensf/dot_general | solution.py:103
  298.6 3.3 %fusion.36 = bf16[32,12,512]{2,0,1:T(8,128)(2,1)S(1)} fusion(bf16[1,7168,512]{2,1,0:T(8,128)(2,1)S(1)} %copy-done.1, f32[512]{0:T(512)S(1)} %bitcast.111, f32[7168]{0:T(1024)S(1)} %bitcast.126, bf16[1,32,12,7168]{3,1,2,0:T(8,128)(2,1)S(1)} %bitcast.99, f32[32,12,512]{2,0,1:T(8,128)S(1)} %fusion.23), kind=kOutput, calls=%fused_computation.45 | convolution fusion | flops 2834432000 | bytes 14055424 | tf_op jit(solution)/shard_map/ensd,edf->ensf/dot_general | solution.py:104
  301.9 5.9 %fusion.26 = f32[32,12,512]{2,0,1:T(8,128)S(1)} fusion(bf16[1,32,6,7168]{3,1,2,0:T(8,128)(2,1)} %collective-permute-done.10, bf16[1,32,6,7168]{3,1,2,0:T(8,128)(2,1)} %collective-permute-done.9, bf16[1,7168,512]{2,1,0:T(8,128)(2,1)S(1)} %bitcast.96, f32[512]{0:T(512)S(1)} %bitcast.108, f32[7168]{0:T(1024)S(1)} %bitcast.127), kind=kOutput, calls=%fused_computation.42 | convolution fusion | flops 2836004864 | bytes 13662208 | tf_op jit(solution)/shard_map/ensd,edf->ensf/dot_general | solution.py:103
  307.8 6.1 %select_bitcast_fusion.1 = (bf16[1,32,12,512]{3,1,2,0:T(8,128)(2,1)S(1)}, bf16[1,32,12,512]{3,1,2,0:T(8,128)(2,1)S(1)}) fusion(bf16[32,12,512]{2,0,1:T(8,128)(2,1)S(1)} %fusion.36, pred[]{:T(512)S(6)} %eq.67, bf16[1,7168,512]{2,1,0:T(8,128)(2,1)S(1)} %copy-done.1, f32[512]{0:T(512)S(1)} %bitcast.112, f32[7168]{0:T(1024)S(1)} %bitcast.128, ...), kind=kOutput, calls=%fused_computation.50 | convolution fusion | flops 2837577728 | bytes 14841857 | tf_op jit(solution)/shard_map/ensd,edf->ensf/dot_general | solution.py:104
  (88 shorter events, 21.2 us)
Async XLA Ops:
  0.0 17.3 %copy-start = (bf16[64,7168]{1,0:T(8,128)(2,1)S(1)}, bf16[64,7168]{1,0:T(8,128)(2,1)}, u32[]{:S(2)}) copy-start(bf16[64,7168]{1,0:T(8,128)(2,1)} %param.6) | copy-start | bytes 2752516
  8.2 25.2 %collective-permute-start.3 = (f32[1,7168]{1,0:T(1,128)S(1)}, f32[1,7168]{1,0:T(1,128)S(1)}, u32[]{:S(2)}, u32[]{:S(2)}) collective-permute-start(f32[1,7168]{1,0:T(1,128)S(1)} %bitcast.117), channel_id=1, source_target_pairs={{0,1},{1,2},{2,3},{3,0},{4,5},{5,6},{6,7},{7,4},{8,9},{9,10},{10,1... | collective-permute-start | bytes 86024 | tf_op jit(solution)/shard_map/ppermute | solution.py:37
  9.8 23.7 %collective-permute-start.4 = (f32[1,7168]{1,0:T(1,128)S(1)}, f32[1,7168]{1,0:T(1,128)S(1)}, u32[]{:S(2)}, u32[]{:S(2)}) collective-permute-start(f32[1,7168]{1,0:T(1,128)S(1)} %bitcast.118), channel_id=1, source_target_pairs={{0,2},{1,3},{2,0},{3,1},{4,6},{5,7},{6,4},{7,5},{8,10},{9,11},{10,... | collective-permute-start | bytes 86024 | tf_op jit(solution)/shard_map/ppermute | solution.py:37
  12.5 21.0 %collective-permute-start.5 = (f32[1,7168]{1,0:T(1,128)S(1)}, f32[1,7168]{1,0:T(1,128)S(1)}, u32[]{:S(2)}, u32[]{:S(2)}) collective-permute-start(f32[1,7168]{1,0:T(1,128)S(1)} %bitcast.119), channel_id=1, source_target_pairs={{0,3},{1,0},{2,1},{3,2},{4,7},{5,4},{6,5},{7,6},{8,11},{9,8},{10,9... | collective-permute-start | bytes 86024 | tf_op jit(solution)/shard_map/ppermute | solution.py:37
  25.0 118.1 %all-to-all-start = ((bf16[32,1,12,7168]{3,2,1,0:T(8,128)(2,1)}), bf16[32,1,12,7168]{3,2,1,0:T(8,128)(2,1)}, u32[]{:S(2)}, u32[]{:S(2)}) async-start(bf16[32,1,12,7168]{3,2,1,0:T(8,128)(2,1)} %copy.24), calls=%async_computation | async-start | bytes 14680064 | tf_op jit(solution)/shard_map/all_to_all | solution.py:64
  33.6 13.8 %slice-start = ((s8[7340032]{0:T(1024)(128)(4,1)}), s8[4194304]{0:T(1024)(128)(4,1)S(1)}, s32[]{:S(2)}) async-start(s8[7340032]{0:T(1024)(128)(4,1)} %bitcast.93), calls=%async_computation.1 | async-start | bytes 8388608
  33.6 13.8 %slice-start.1 = ((s8[7340032]{0:T(1024)(128)(4,1)}), s8[3145728]{0:T(1024)(128)(4,1)S(1)}, s32[]{:S(2)}) async-start(s8[7340032]{0:T(1024)(128)(4,1)} %bitcast.93), calls=%async_computation.2 | async-start | bytes 6291456
  49.4 5.2 %collective-permute-start.6 = (f32[1,7168]{1,0:T(1,128)S(1)}, f32[1,7168]{1,0:T(1,128)S(1)}, u32[]{:S(2)}, u32[]{:S(2)}) collective-permute-start(f32[1,7168]{1,0:T(1,128)S(1)} %bitcast.121), channel_id=1, source_target_pairs={{0,1},{1,2},{2,3},{3,0},{4,5},{5,6},{6,7},{7,4},{8,9},{9,10},{10,1... | collective-permute-start | bytes 86024 | tf_op jit(solution)/shard_map/ppermute | solution.py:37
  50.1 5.4 %collective-permute-start.7 = (f32[1,7168]{1,0:T(1,128)S(1)}, f32[1,7168]{1,0:T(1,128)S(1)}, u32[]{:S(2)}, u32[]{:S(2)}) collective-permute-start(f32[1,7168]{1,0:T(1,128)S(1)} %bitcast.122), channel_id=1, source_target_pairs={{0,2},{1,3},{2,0},{3,1},{4,6},{5,7},{6,4},{7,5},{8,10},{9,11},{10,... | collective-permute-start | bytes 86024 | tf_op jit(solution)/shard_map/ppermute | solution.py:37
  51.0 4.8 %collective-permute-start.8 = (f32[1,7168]{1,0:T(1,128)S(1)}, f32[1,7168]{1,0:T(1,128)S(1)}, u32[]{:S(2)}, u32[]{:S(2)}) collective-permute-start(f32[1,7168]{1,0:T(1,128)S(1)} %bitcast.123), channel_id=1, source_target_pairs={{0,3},{1,0},{2,1},{3,2},{4,7},{5,4},{6,5},{7,6},{8,11},{9,8},{10,9... | collective-permute-start | bytes 86024 | tf_op jit(solution)/shard_map/ppermute | solution.py:37
  149.2 2.4 copy-start.2
  154.4 147.4 %collective-permute-start.10 = (bf16[1,32,6,7168]{3,1,2,0:T(8,128)(2,1)}, bf16[1,32,6,7168]{3,1,2,0:T(8,128)(2,1)}, u32[]{:S(2)}, u32[]{:S(2)}) collective-permute-start(bf16[1,32,6,7168]{3,1,2,0:T(8,128)(2,1)} %get-tuple-element.116), channel_id=1, source_target_pairs={{0,1},{1,2},{2,3},{3,0},{4,5},{5,6},{6,7},{7,4},{8,9},{9,10},{10,1... | collective-permute-start | bytes 8257544 | tf_op jit(solution)/shard_map/ppermute | solution.py:90
  155.0 146.8 %collective-permute-start.9 = (bf16[1,32,6,7168]{3,1,2,0:T(8,128)(2,1)}, bf16[1,32,6,7168]{3,1,2,0:T(8,128)(2,1)}, u32[]{:S(2)}, u32[]{:S(2)}) collective-permute-start(bf16[1,32,6,7168]{3,1,2,0:T(8,128)(2,1)} %get-tuple-element.115), channel_id=1, source_target_pairs={{0,3},{1,0},{2,1},{3,2},{4,7},{5,4},{6,5},{7,6},{8,11},{9,8},{10,9... | collective-permute-start | bytes 8257544 | tf_op jit(solution)/shard_map/ppermute | solution.py:87
  179.9 50.8 %collective-permute-start = (f32[1,7168]{1,0:T(1,128)S(1)}, f32[1,7168]{1,0:T(1,128)S(1)}, u32[]{:S(2)}, u32[]{:S(2)}) collective-permute-start(f32[1,7168]{1,0:T(1,128)S(1)} %bitcast.101), channel_id=1, source_target_pairs={{0,3},{1,0},{2,1},{3,2},{4,7},{5,4},{6,5},{7,6},{8,11},{9,8},{10,9... | collective-permute-start | bytes 86024 | tf_op jit(solution)/shard_map/while/body/eval_jaxpr/ppermute | solution.py:37
  180.0 50.7 %collective-permute-start.1 = (f32[1,7168]{1,0:T(1,128)S(1)}, f32[1,7168]{1,0:T(1,128)S(1)}, u32[]{:S(2)}, u32[]{:S(2)}) collective-permute-start(f32[1,7168]{1,0:T(1,128)S(1)} %bitcast.102), channel_id=1, source_target_pairs={{0,2},{1,3},{2,0},{3,1},{4,6},{5,7},{6,4},{7,5},{8,10},{9,11},{10,... | collective-permute-start | bytes 86024 | tf_op jit(solution)/shard_map/while/body/eval_jaxpr/ppermute | solution.py:37
  181.4 49.3 %collective-permute-start.2 = (f32[1,7168]{1,0:T(1,128)S(1)}, f32[1,7168]{1,0:T(1,128)S(1)}, u32[]{:S(2)}, u32[]{:S(2)}) collective-permute-start(f32[1,7168]{1,0:T(1,128)S(1)} %bitcast.103), channel_id=1, source_target_pairs={{0,1},{1,2},{2,3},{3,0},{4,5},{5,6},{6,7},{7,4},{8,9},{9,10},{10,1... | collective-permute-start | bytes 86024 | tf_op jit(solution)/shard_map/while/body/eval_jaxpr/ppermute | solution.py:37
  248.2 5.3 %collective-permute-start = (f32[1,7168]{1,0:T(1,128)S(1)}, f32[1,7168]{1,0:T(1,128)S(1)}, u32[]{:S(2)}, u32[]{:S(2)}) collective-permute-start(f32[1,7168]{1,0:T(1,128)S(1)} %bitcast.101), channel_id=1, source_target_pairs={{0,3},{1,0},{2,1},{3,2},{4,7},{5,4},{6,5},{7,6},{8,11},{9,8},{10,9... | collective-permute-start | bytes 86024 | tf_op jit(solution)/shard_map/while/body/eval_jaxpr/ppermute | solution.py:37
  251.9 5.4 %collective-permute-start.1 = (f32[1,7168]{1,0:T(1,128)S(1)}, f32[1,7168]{1,0:T(1,128)S(1)}, u32[]{:S(2)}, u32[]{:S(2)}) collective-permute-start(f32[1,7168]{1,0:T(1,128)S(1)} %bitcast.102), channel_id=1, source_target_pairs={{0,2},{1,3},{2,0},{3,1},{4,6},{5,7},{6,4},{7,5},{8,10},{9,11},{10,... | collective-permute-start | bytes 86024 | tf_op jit(solution)/shard_map/while/body/eval_jaxpr/ppermute | solution.py:37
  251.9 5.4 %collective-permute-start.2 = (f32[1,7168]{1,0:T(1,128)S(1)}, f32[1,7168]{1,0:T(1,128)S(1)}, u32[]{:S(2)}, u32[]{:S(2)}) collective-permute-start(f32[1,7168]{1,0:T(1,128)S(1)} %bitcast.103), channel_id=1, source_target_pairs={{0,1},{1,2},{2,3},{3,0},{4,5},{5,6},{6,7},{7,4},{8,9},{9,10},{10,1... | collective-permute-start | bytes 86024 | tf_op jit(solution)/shard_map/while/body/eval_jaxpr/ppermute | solution.py:37
  274.7 3.9 %collective-permute-start = (f32[1,7168]{1,0:T(1,128)S(1)}, f32[1,7168]{1,0:T(1,128)S(1)}, u32[]{:S(2)}, u32[]{:S(2)}) collective-permute-start(f32[1,7168]{1,0:T(1,128)S(1)} %bitcast.101), channel_id=1, source_target_pairs={{0,3},{1,0},{2,1},{3,2},{4,7},{5,4},{6,5},{7,6},{8,11},{9,8},{10,9... | collective-permute-start | bytes 86024 | tf_op jit(solution)/shard_map/while/body/eval_jaxpr/ppermute | solution.py:37
  275.6 5.4 %collective-permute-start.1 = (f32[1,7168]{1,0:T(1,128)S(1)}, f32[1,7168]{1,0:T(1,128)S(1)}, u32[]{:S(2)}, u32[]{:S(2)}) collective-permute-start(f32[1,7168]{1,0:T(1,128)S(1)} %bitcast.102), channel_id=1, source_target_pairs={{0,2},{1,3},{2,0},{3,1},{4,6},{5,7},{6,4},{7,5},{8,10},{9,11},{10,... | collective-permute-start | bytes 86024 | tf_op jit(solution)/shard_map/while/body/eval_jaxpr/ppermute | solution.py:37
  276.9 5.1 %collective-permute-start.2 = (f32[1,7168]{1,0:T(1,128)S(1)}, f32[1,7168]{1,0:T(1,128)S(1)}, u32[]{:S(2)}, u32[]{:S(2)}) collective-permute-start(f32[1,7168]{1,0:T(1,128)S(1)} %bitcast.103), channel_id=1, source_target_pairs={{0,1},{1,2},{2,3},{3,0},{4,5},{5,6},{6,7},{7,4},{8,9},{9,10},{10,1... | collective-permute-start | bytes 86024 | tf_op jit(solution)/shard_map/while/body/eval_jaxpr/ppermute | solution.py:37
  290.3 8.0 %copy-start.1 = (bf16[1,7168,512]{2,1,0:T(8,128)(2,1)S(1)}, bf16[1,7168,512]{2,1,0:T(8,128)(2,1)}, u32[]{:S(2)}) copy-start(bf16[1,7168,512]{2,1,0:T(8,128)(2,1)} %get-tuple-element.190) | copy-start | bytes 22020100
  290.3 8.3 %copy-start.3 = (bf16[32,1,12,7168]{3,0,2,1:T(8,128)(2,1)S(1)}, bf16[32,1,12,7168]{3,0,2,1:T(8,128)(2,1)}, u32[]{:S(2)}) copy-start(bf16[32,1,12,7168]{3,0,2,1:T(8,128)(2,1)} %copy-done.2) | copy-start | bytes 16515076
  290.3 8.3 %copy-start.4 = (f32[1,7168]{1,0:T(1,128)S(1)}, f32[1,7168]{1,0:T(1,128)}, u32[]{:S(2)}) copy-start(f32[1,7168]{1,0:T(1,128)} %get-tuple-element.88) | copy-start | bytes 86020
  290.3 11.6 %slice-start.2 = ((s8[7340032]{0:T(1024)(128)(4,1)}), s8[4194304]{0:T(1024)(128)(4,1)S(1)}, s32[]{:S(2)}) async-start(s8[7340032]{0:T(1024)(128)(4,1)} %bitcast.95), calls=%async_computation.3 | async-start | bytes 8388608
  298.6 3.3 %slice-start.3 = ((s8[7340032]{0:T(1024)(128)(4,1)}), s8[3145728]{0:T(1024)(128)(4,1)S(1)}, s32[]{:S(2)}) async-start(s8[7340032]{0:T(1024)(128)(4,1)} %bitcast.95), calls=%async_computation.4 | async-start | bytes 6291456
where the time goes:
time: 317 us; the launch traced here: 315 us
  waiting for transfers between devices  139 us (44%)
  other arithmetic  86.5 us (27%)
  starting transfers between devices  44.2 us (14%)
  matrix products  24.7 us (8%)
  local copies, waits for them, and re-layouts  20.5 us (6%)
    all_to_all x1, waiting for transfers between devices, shards(): lax.all_to_all(outgoing, 'expert', split_axis=0, concat_axis=1, tiled=True)  79.1 us
    ppermute x15, waiting for transfers between devices, hidden_sum(): lax.ppermute(values, 'hidden', [(i, (i + shift) % n) for i in range(n)])  59.8 us
    reduce_sum x6, other arithmetic, row_terms(): return jnp.sum(values * values * cols_sq[:, None, :], axis=2)  42.6 us
    reduce_sum x5, other arithmetic, col_terms(): return jnp.sum(values * values * scale_sq[:, :, None], axis=1)  38.9 us
    ppermute x15, starting transfers between devices, hidden_sum(): lax.ppermute(values, 'hidden', [(i, (i + shift) % n) for i in range(n)])  19.4 us
    ppermute x1, starting transfers between devices, shards(): lax.ppermute(mine[:, :, :quarter], 'hidden', [(i, (i - 1) % n_hidden) for...  15.7 us
    dot_general x2, matrix products, expert_mlp(): jnp.einsum('ensd,edf->ensf', rows, gate_eq, preferred_element_type=jnp.fl...  13.8 us
    dot_general x2, matrix products, expert_mlp(): jnp.einsum('ensd,edf->ensf', rows, up_eq, preferred_element_type=jnp.floa...  9.31 us
  transfers between devices with their start and end apart: 18, of which 10 were waited for; matrix products, arithmetic and copies ran while one was open for 31% of the time, Pallas kernels for 0%

commit v1 on v0

v1 whole, which is shorter than its diff:
```python
import jax
import jax.numpy as jnp
from jax import lax
from jax.sharding import PartitionSpec as P

TOPK = 8
EXPERTS = 32
SWEEPS = 5
TOK_DEV = 64
CAP = 24


EPS = 1e-06


def dispatch_rows(block_ids, tokens):
    tok_local, topk = block_ids.shape
    flat_ids = block_ids.reshape(-1)
    onehot = (flat_ids[:, None] == jnp.arange(EXPERTS, dtype=jnp.int32)[None, :]).astype(jnp.int32)
    before = jnp.cumsum(onehot, axis=0) - onehot
    my_rank = jnp.sum(before * onehot, axis=1)
    pair_ids = flat_ids.reshape(tok_local, topk)
    pair_rank = my_rank.reshape(tok_local, topk)
    hit = (pair_ids[None, None] == jnp.arange(EXPERTS, dtype=jnp.int32)[:, None, None, None]) & (
        pair_rank[None, None] == jnp.arange(CAP, dtype=jnp.int32)[None, :, None, None]
    )
    select = jnp.any(hit, axis=3).astype(tokens.dtype)
    rows = jnp.einsum("est,td->esd", select, tokens, preferred_element_type=jnp.float32)
    return rows.astype(tokens.dtype)[:, None]


def hidden_sum(values):
    n = lax.axis_size("hidden")
    total = values
    for shift in range(1, n):
        total = total + lax.ppermute(values, "hidden", [(i, (i + shift) % n) for i in range(n)])
    return total


def row_terms(weight, cols_sq):
    values = weight.astype(jnp.float32)
    return jnp.sum(values * values * cols_sq[:, None, :], axis=2)


def col_terms(weight, scale_sq):
    values = weight.astype(jnp.float32)
    return jnp.sum(values * values * scale_sq[:, :, None], axis=1)


def shards(tokens, expert_ids, gate_weight, up_weight):
    exp_local = gate_weight.shape[0]
    width = gate_weight.shape[1]
    ff_local = gate_weight.shape[2]
    ff_total = ff_local * lax.axis_size("hidden")
    my_index = lax.axis_index("expert")
    tok_local = tokens.shape[0]
    block_ids = lax.dynamic_slice_in_dim(expert_ids, my_index * tok_local, tok_local, 0)
    outgoing = dispatch_rows(block_ids, tokens)
    routed = lax.all_to_all(outgoing, "expert", split_axis=0, concat_axis=1, tiled=True)
    def sweep(_, carry):
        gate_cols, up_cols, _ = carry
        partial_rows = row_terms(gate_weight, gate_cols * gate_cols) + row_terms(
            up_weight, up_cols * up_cols
        )
        row_sums = hidden_sum(partial_rows)
        row_scale = lax.rsqrt(width * row_sums / (2 * ff_total) + EPS)
        scale_sq = row_scale * row_scale
        gate_cols = lax.rsqrt(col_terms(gate_weight, scale_sq) + EPS)
        up_cols = lax.rsqrt(col_terms(up_weight, scale_sq) + EPS)
        return gate_cols, up_cols, row_scale

    carry = (
        jnp.ones((exp_local, ff_local), jnp.float32),
        jnp.ones((exp_local, ff_local), jnp.float32),
        jnp.ones((exp_local, width), jnp.float32),
    )
    gate_cols, up_cols, row_scale = lax.fori_loop(0, SWEEPS, sweep, carry)
    gate_eq = (
        gate_weight.astype(jnp.float32) * row_scale[:, :, None] * gate_cols[:, None, :]
    ).astype(jnp.bfloat16)
    up_eq = (up_weight.astype(jnp.float32) * row_scale[:, :, None] * up_cols[:, None, :]).astype(
        jnp.bfloat16
    )
    gate_act = jnp.einsum("ensd,edf->ensf", routed, gate_eq, preferred_element_type=jnp.float32)
    up_act = jnp.einsum("ensd,edf->ensf", routed, up_eq, preferred_element_type=jnp.float32)
    return (jax.nn.silu(gate_act) * up_act).astype(jnp.bfloat16)


def solution(mesh):
    in_specs = (P("expert", None), P(), P("expert", None, "hidden"), P("expert", None, "hidden"))
    out_specs = P("expert", None, None, "hidden")
    return jax.shard_map(shards, mesh=mesh, in_specs=in_specs, out_specs=out_specs, check_vma=False)
```

time: 317 us -> 213 us (0.67)
  waiting for transfers between devices: 139 us -> 68.2 us
  starting transfers between devices: 44.2 us -> 24.1 us
  local copies, waits for them, and re-layouts: 20.5 us -> 1.5 us
  matrix products: 24.7 us -> 29.2 us
    ppermute x15, waiting for transfers between devices: 59.8 us -> 22 us  [hidden_sum(): lax.ppermute(values, 'hidden', [(i, (i + shift) % n) for i in range(n)])]
    all_to_all x1, waiting for transfers between devices: 79.1 us -> 46.3 us  [shards(): lax.all_to_all(outgoing, 'expert', split_axis=0, concat_axis=1, tiled=True)]
    ppermute x2 -> x0, starting transfers between devices: 16.3 us -> none  [the longest x1 15.7 us: shards(): lax.ppermute(mine[:, :, :quarter], 'hidden', [(i, (i - 1) % n_hidden) for...]
    broadcast_in_dim x1 -> x0, local copies, waits for them, and re-layouts: 6.14 us -> none  [dispatch_rows(): return rows.astype(tokens.dtype)[:, None]]
    all_to_all x1 -> x0, local copies, waits for them, and re-layouts: 6.1 us -> none  [shards(): lax.all_to_all(outgoing, 'expert', split_axis=0, concat_axis=1, tiled=True)]
    dot_general x1, matrix products: 1.57 us -> 5.62 us  [dispatch_rows(): jnp.einsum('est,td->esd', select, tokens, preferred_element_type=jnp.floa...]
    ppermute x15, starting transfers between devices: 19.4 us -> 16.1 us  [hidden_sum(): lax.ppermute(values, 'hidden', [(i, (i + shift) % n) for i in range(n)])]
    reduce_sum x6 -> x5, other arithmetic: 42.6 us -> 45.5 us  [row_terms(): return jnp.sum(values * values * cols_sq[:, None, :], axis=2)]
  transfers between devices with their start and end apart: 18 -> 16, of which waited for: 10 -> 15; matrix products, arithmetic and copies ran while one was open for 31% -> 41% of each run, Pallas kernels for 0% -> 0%
where the time goes in v1:
time: 213 us
  other arithmetic  89.3 us (42%)
  waiting for transfers between devices  68.2 us (32%)
  matrix products  29.2 us (14%)
  starting transfers between devices  24.1 us (11%)
    all_to_all x1, waiting for transfers between devices, shards(): lax.all_to_all(outgoing, 'expert', split_axis=0, concat_axis=1, tiled=True)  46.3 us
    reduce_sum x5, other arithmetic, row_terms(): return jnp.sum(values * values * cols_sq[:, None, :], axis=2)  45.5 us
    reduce_sum x5, other arithmetic, col_terms(): return jnp.sum(values * values * scale_sq[:, :, None], axis=1)  37.9 us
    ppermute x15, waiting for transfers between devices, hidden_sum(): lax.ppermute(values, 'hidden', [(i, (i + shift) % n) for i in range(n)])  22 us
    ppermute x15, starting transfers between devices, hidden_sum(): lax.ppermute(values, 'hidden', [(i, (i + shift) % n) for i in range(n)])  16.1 us
    dot_general x1, matrix products, shards(): jnp.einsum('ensd,edf->ensf', routed, gate_eq, preferred_element_type=jnp....  12.3 us
    dot_general x1, matrix products, shards(): jnp.einsum('ensd,edf->ensf', routed, up_eq, preferred_element_type=jnp.fl...  11.3 us
    all_to_all x1, starting transfers between devices, shards(): lax.all_to_all(outgoing, 'expert', split_axis=0, concat_axis=1, tiled=True)  8.03 us
  transfers between devices with their start and end apart: 16, of which 15 were waited for; matrix products, arithmetic and copies ran while one was open for 41% of the time, Pallas kernels for 0%

profile of v1, /device:TPU:48, one launch (start us, length us, event | category | flops | bytes accessed | tf_op | source)
XLA Modules:
  0.0 213.0 jit_solution(6398732077900331420)
XLA Ops:
  1.2 1.2 reduce-window.6
  3.9 5.6 %fusion.4 = bf16[32,1,24,7168]{3,2,1,0:T(8,128)(2,1)} fusion(pred[32,24,64]{2,1,0:T(8,128)(4,1)S(1)} %and_reduce_fusion, bf16[64,7168]{1,0:T(8,128)(2,1)S(1)} %copy-done), kind=kOutput, calls=%fused_computation.16 | convolution fusion | flops 710148096 | bytes 11976704 | tf_op jit(solution)/shard_map/est,td->esd/dot_general | solution.py:28
  9.5 8.0 %all-to-all-start = ((bf16[32,1,24,7168]{3,2,1,0:T(8,128)(2,1)}), bf16[32,1,24,7168]{3,2,1,0:T(8,128)(2,1)}, u32[]{:S(2)}, u32[]{:S(2)}) async-start(bf16[32,1,24,7168]{3,2,1,0:T(8,128)(2,1)} %fusion.4), calls=%async_computation | async-start | bytes 22020096 | tf_op jit(solution)/shard_map/all_to_all | solution.py:59
  17.6 125.5 %while.16 = (s32[]{:T(128)}, f32[1,512]{1,0:T(1,128)S(1)}, f32[1,512]{1,0:T(1,128)S(1)}, f32[1,7168]{1,0:T(1,128)}, bf16[1,7168,512]{2,1,0:T(8,128)(2,1)}, /*index=5*/bf16[1,7168,512]{2,1,0:T(8,128)(2,1)}, s32[]{:T(128)}) while((s32[]{:T(128)}, f32[1,512]{1,0:T(1,128)S(1)}, f32[1,512]{1,0:T(1,128)S(1)}, f32[1,7168]{1,0:T(1,128)}, ...), condition=%wide.region_9.10_spmd, body=%wide.region_4.9_spmd.sunk | while | flops 58757120 | bytes 30077124 | solution.py:77
  17.6 9.1 %multiply_reduce_fusion.6 = (f32[7168]{0:T(1024)S(1)}, f32[7168]{0:T(1024)S(1)}) fusion(bf16[1,7168,512]{2,1,0:T(8,128)(2,1)} %get-tuple-element.167, f32[512]{0:T(512)S(1)} %bitcast.80, f32[512]{0:T(512)S(1)} %bitcast.81, bf16[1,7168,512]{2,1,0:T(8,128)(2,1)} %get-tuple-element.166), kind=kLoop, calls=%fused_computation.2.clone.1 | loop fusion | flops 29345792 | bytes 14741504 | tf_op jit(solution)/shard_map/while/body/eval_jaxpr/reduce_sum | solution.py:42
  26.7 2.8 %collective-permute-start = (f32[1,7168]{1,0:T(1,128)S(1)}, f32[1,7168]{1,0:T(1,128)S(1)}, u32[]{:S(2)}, u32[]{:S(2)}) collective-permute-start(f32[1,7168]{1,0:T(1,128)S(1)} %bitcast.72), channel_id=1, source_target_pairs={{0,3},{1,0},{2,1},{3,2},{4,7},{5,4},{6,5},{7,6},{8,11},{9,8},{10,9... | collective-permute-start | bytes 86024 | tf_op jit(solution)/shard_map/while/body/eval_jaxpr/ppermute | solution.py:36
  31.3 3.6 %collective-permute-done.1 = f32[1,7168]{1,0:T(1,128)S(1)} collective-permute-done((f32[1,7168]{1,0:T(1,128)S(1)}, f32[1,7168]{1,0:T(1,128)S(1)}, u32[]{:S(2)}, u32[]{:S(2)}) %collective-permute-start.1) | collective-permute-done | bytes 28704 | tf_op jit(solution)/shard_map/while/body/eval_jaxpr/ppermute | solution.py:36
  36.1 7.6 %multiply_reduce_fusion.7 = (f32[512]{0:T(512)S(1)}, f32[512]{0:T(512)S(1)}) fusion(bf16[1,7168,512]{2,1,0:T(8,128)(2,1)} %get-tuple-element.167, f32[7168]{0:T(1024)S(1)} %bitcast.71, bf16[1,7168,512]{2,1,0:T(8,128)(2,1)} %get-tuple-element.166), kind=kLoop, calls=%fused_computation.clone.1 | loop fusion | flops 29359104 | bytes 14712832 | tf_op jit(solution)/shard_map/while/body/eval_jaxpr/reduce_sum | solution.py:47
  43.8 9.1 %multiply_reduce_fusion.6 = (f32[7168]{0:T(1024)S(1)}, f32[7168]{0:T(1024)S(1)}) fusion(bf16[1,7168,512]{2,1,0:T(8,128)(2,1)} %get-tuple-element.167, f32[512]{0:T(512)S(1)} %bitcast.80, f32[512]{0:T(512)S(1)} %bitcast.81, bf16[1,7168,512]{2,1,0:T(8,128)(2,1)} %get-tuple-element.166), kind=kLoop, calls=%fused_computation.2.clone.1 | loop fusion | flops 29345792 | bytes 14741504 | tf_op jit(solution)/shard_map/while/body/eval_jaxpr/reduce_sum | solution.py:42
  53.3 1.4 collective-permute-start.1
  54.7 1.2 collective-permute-start.2
  56.8 1.9 collective-permute-done.1
  58.7 1.1 collective-permute-done.2
  60.5 7.6 %multiply_reduce_fusion.7 = (f32[512]{0:T(512)S(1)}, f32[512]{0:T(512)S(1)}) fusion(bf16[1,7168,512]{2,1,0:T(8,128)(2,1)} %get-tuple-element.167, f32[7168]{0:T(1024)S(1)} %bitcast.71, bf16[1,7168,512]{2,1,0:T(8,128)(2,1)} %get-tuple-element.166), kind=kLoop, calls=%fused_computation.clone.1 | loop fusion | flops 29359104 | bytes 14712832 | tf_op jit(solution)/shard_map/while/body/eval_jaxpr/reduce_sum | solution.py:47
  68.1 9.1 %multiply_reduce_fusion.6 = (f32[7168]{0:T(1024)S(1)}, f32[7168]{0:T(1024)S(1)}) fusion(bf16[1,7168,512]{2,1,0:T(8,128)(2,1)} %get-tuple-element.167, f32[512]{0:T(512)S(1)} %bitcast.80, f32[512]{0:T(512)S(1)} %bitcast.81, bf16[1,7168,512]{2,1,0:T(8,128)(2,1)} %get-tuple-element.166), kind=kLoop, calls=%fused_computation.2.clone.1 | loop fusion | flops 29345792 | bytes 14741504 | tf_op jit(solution)/shard_map/while/body/eval_jaxpr/reduce_sum | solution.py:42
  77.2 1.8 collective-permute-start
  80.0 1.2 collective-permute-done
  81.2 3.2 %collective-permute-done.1 = f32[1,7168]{1,0:T(1,128)S(1)} collective-permute-done((f32[1,7168]{1,0:T(1,128)S(1)}, f32[1,7168]{1,0:T(1,128)S(1)}, u32[]{:S(2)}, u32[]{:S(2)}) %collective-permute-start.1) | collective-permute-done | bytes 28704 | tf_op jit(solution)/shard_map/while/body/eval_jaxpr/ppermute | solution.py:36
  85.7 7.6 %multiply_reduce_fusion.7 = (f32[512]{0:T(512)S(1)}, f32[512]{0:T(512)S(1)}) fusion(bf16[1,7168,512]{2,1,0:T(8,128)(2,1)} %get-tuple-element.167, f32[7168]{0:T(1024)S(1)} %bitcast.71, bf16[1,7168,512]{2,1,0:T(8,128)(2,1)} %get-tuple-element.166), kind=kLoop, calls=%fused_computation.clone.1 | loop fusion | flops 29359104 | bytes 14712832 | tf_op jit(solution)/shard_map/while/body/eval_jaxpr/reduce_sum | solution.py:47
  93.4 9.1 %multiply_reduce_fusion.6 = (f32[7168]{0:T(1024)S(1)}, f32[7168]{0:T(1024)S(1)}) fusion(bf16[1,7168,512]{2,1,0:T(8,128)(2,1)} %get-tuple-element.167, f32[512]{0:T(512)S(1)} %bitcast.80, f32[512]{0:T(512)S(1)} %bitcast.81, bf16[1,7168,512]{2,1,0:T(8,128)(2,1)} %get-tuple-element.166), kind=kLoop, calls=%fused_computation.2.clone.1 | loop fusion | flops 29345792 | bytes 14741504 | tf_op jit(solution)/shard_map/while/body/eval_jaxpr/reduce_sum | solution.py:42
  104.3 1.1 collective-permute-start.2
  105.4 1.0 collective-permute-done
  106.4 2.3 %collective-permute-done.1 = f32[1,7168]{1,0:T(1,128)S(1)} collective-permute-done((f32[1,7168]{1,0:T(1,128)S(1)}, f32[1,7168]{1,0:T(1,128)S(1)}, u32[]{:S(2)}, u32[]{:S(2)}) %collective-permute-start.1) | collective-permute-done | bytes 28704 | tf_op jit(solution)/shard_map/while/body/eval_jaxpr/ppermute | solution.py:36
  110.1 7.6 %multiply_reduce_fusion.7 = (f32[512]{0:T(512)S(1)}, f32[512]{0:T(512)S(1)}) fusion(bf16[1,7168,512]{2,1,0:T(8,128)(2,1)} %get-tuple-element.167, f32[7168]{0:T(1024)S(1)} %bitcast.71, bf16[1,7168,512]{2,1,0:T(8,128)(2,1)} %get-tuple-element.166), kind=kLoop, calls=%fused_computation.clone.1 | loop fusion | flops 29359104 | bytes 14712832 | tf_op jit(solution)/shard_map/while/body/eval_jaxpr/reduce_sum | solution.py:47
  117.7 9.1 %multiply_reduce_fusion.6 = (f32[7168]{0:T(1024)S(1)}, f32[7168]{0:T(1024)S(1)}) fusion(bf16[1,7168,512]{2,1,0:T(8,128)(2,1)} %get-tuple-element.167, f32[512]{0:T(512)S(1)} %bitcast.80, f32[512]{0:T(512)S(1)} %bitcast.81, bf16[1,7168,512]{2,1,0:T(8,128)(2,1)} %get-tuple-element.166), kind=kLoop, calls=%fused_computation.2.clone.1 | loop fusion | flops 29345792 | bytes 14741504 | tf_op jit(solution)/shard_map/while/body/eval_jaxpr/reduce_sum | solution.py:42
  126.8 1.8 collective-permute-start
  129.7 1.0 collective-permute-done
  130.8 3.2 %collective-permute-done.1 = f32[1,7168]{1,0:T(1,128)S(1)} collective-permute-done((f32[1,7168]{1,0:T(1,128)S(1)}, f32[1,7168]{1,0:T(1,128)S(1)}, u32[]{:S(2)}, u32[]{:S(2)}) %collective-permute-start.1) | collective-permute-done | bytes 28704 | tf_op jit(solution)/shard_map/while/body/eval_jaxpr/ppermute | solution.py:36
  135.3 7.6 %multiply_reduce_fusion.7 = (f32[512]{0:T(512)S(1)}, f32[512]{0:T(512)S(1)}) fusion(bf16[1,7168,512]{2,1,0:T(8,128)(2,1)} %get-tuple-element.167, f32[7168]{0:T(1024)S(1)} %bitcast.71, bf16[1,7168,512]{2,1,0:T(8,128)(2,1)} %get-tuple-element.166), kind=kLoop, calls=%fused_computation.clone.1 | loop fusion | flops 29359104 | bytes 14712832 | tf_op jit(solution)/shard_map/while/body/eval_jaxpr/reduce_sum | solution.py:47
  143.1 46.3 %all-to-all-done = bf16[32,1,24,7168]{3,2,1,0:T(8,128)(2,1)} async-done(((bf16[32,1,24,7168]{3,2,1,0:T(8,128)(2,1)}), bf16[32,1,24,7168]{3,2,1,0:T(8,128)(2,1)}, u32[]{:S(2)}, u32[]{:S(2)}) %all-to-all-start) | async-done | bytes 11010080 | tf_op jit(solution)/shard_map/all_to_all | solution.py:59
  189.4 12.3 %fusion.2 = f32[32,24,512]{2,1,0:T(8,128)S(1)} fusion(bf16[32,1,24,7168]{3,2,1,0:T(8,128)(2,1)} %all-to-all-done, bf16[1,7168,512]{2,1,0:T(8,128)(2,1)} %get-tuple-element.169, f32[512]{0:T(512)S(1)} %bitcast.77, f32[7168]{0:T(1024)} %bitcast.82), kind=kOutput, calls=%fused_computation.14 | convolution fusion | flops 5651824640 | bytes 19953664 | tf_op jit(solution)/shard_map/ensd,edf->ensf/dot_general | solution.py:84
  201.7 11.3 %fusion.17 = bf16[1,32,24,512]{3,2,1,0:T(8,128)(2,1)} fusion(bf16[1,7168,512]{2,1,0:T(8,128)(2,1)S(1)} %copy-done.1, f32[512]{0:T(512)S(1)} %bitcast.79, f32[7168]{0:T(1024)S(1)} %bitcast.83, bf16[32,1,24,7168]{3,2,1,0:T(8,128)(2,1)} %all-to-all-done, f32[32,24,512]{2,1,0:T(8,128)S(1)} %fusion.2), kind=kOutput, calls=%fused_computation.25 | convolution fusion | flops 5654183936 | bytes 20740096 | tf_op jit(solution)/shard_map/ensd,edf->ensf/dot_general | solution.py:85
  (68 shorter events, 15.5 us)
Async XLA Ops:
  0.0 3.9 %copy-start = (bf16[64,7168]{1,0:T(8,128)(2,1)S(1)}, bf16[64,7168]{1,0:T(8,128)(2,1)}, u32[]{:S(2)}) copy-start(bf16[64,7168]{1,0:T(8,128)(2,1)} %param.6) | copy-start | bytes 2752516
  9.5 179.9 %all-to-all-start = ((bf16[32,1,24,7168]{3,2,1,0:T(8,128)(2,1)}), bf16[32,1,24,7168]{3,2,1,0:T(8,128)(2,1)}, u32[]{:S(2)}, u32[]{:S(2)}) async-start(bf16[32,1,24,7168]{3,2,1,0:T(8,128)(2,1)} %fusion.4), calls=%async_computation | async-start | bytes 22020096 | tf_op jit(solution)/shard_map/all_to_all | solution.py:59
  26.7 4.6 %collective-permute-start = (f32[1,7168]{1,0:T(1,128)S(1)}, f32[1,7168]{1,0:T(1,128)S(1)}, u32[]{:S(2)}, u32[]{:S(2)}) collective-permute-start(f32[1,7168]{1,0:T(1,128)S(1)} %bitcast.72), channel_id=1, source_target_pairs={{0,3},{1,0},{2,1},{3,2},{4,7},{5,4},{6,5},{7,6},{8,11},{9,8},{10,9... | collective-permute-start | bytes 86024 | tf_op jit(solution)/shard_map/while/body/eval_jaxpr/ppermute | solution.py:36
  29.6 5.4 %collective-permute-start.1 = (f32[1,7168]{1,0:T(1,128)S(1)}, f32[1,7168]{1,0:T(1,128)S(1)}, u32[]{:S(2)}, u32[]{:S(2)}) collective-permute-start(f32[1,7168]{1,0:T(1,128)S(1)} %bitcast.73), channel_id=1, source_target_pairs={{0,2},{1,3},{2,0},{3,1},{4,6},{5,7},{6,4},{7,5},{8,10},{9,11},{10,... | collective-permute-start | bytes 86024 | tf_op jit(solution)/shard_map/while/body/eval_jaxpr/ppermute | solution.py:36
  30.4 5.1 %collective-permute-start.2 = (f32[1,7168]{1,0:T(1,128)S(1)}, f32[1,7168]{1,0:T(1,128)S(1)}, u32[]{:S(2)}, u32[]{:S(2)}) collective-permute-start(f32[1,7168]{1,0:T(1,128)S(1)} %bitcast.74), channel_id=1, source_target_pairs={{0,1},{1,2},{2,3},{3,0},{4,5},{5,6},{6,7},{7,4},{8,9},{9,10},{10,1... | collective-permute-start | bytes 86024 | tf_op jit(solution)/shard_map/while/body/eval_jaxpr/ppermute | solution.py:36
  52.9 3.9 %collective-permute-start = (f32[1,7168]{1,0:T(1,128)S(1)}, f32[1,7168]{1,0:T(1,128)S(1)}, u32[]{:S(2)}, u32[]{:S(2)}) collective-permute-start(f32[1,7168]{1,0:T(1,128)S(1)} %bitcast.72), channel_id=1, source_target_pairs={{0,3},{1,0},{2,1},{3,2},{4,7},{5,4},{6,5},{7,6},{8,11},{9,8},{10,9... | collective-permute-start | bytes 86024 | tf_op jit(solution)/shard_map/while/body/eval_jaxpr/ppermute | solution.py:36
  53.3 5.4 %collective-permute-start.1 = (f32[1,7168]{1,0:T(1,128)S(1)}, f32[1,7168]{1,0:T(1,128)S(1)}, u32[]{:S(2)}, u32[]{:S(2)}) collective-permute-start(f32[1,7168]{1,0:T(1,128)S(1)} %bitcast.73), channel_id=1, source_target_pairs={{0,2},{1,3},{2,0},{3,1},{4,6},{5,7},{6,4},{7,5},{8,10},{9,11},{10,... | collective-permute-start | bytes 86024 | tf_op jit(solution)/shard_map/while/body/eval_jaxpr/ppermute | solution.py:36
  54.7 5.1 %collective-permute-start.2 = (f32[1,7168]{1,0:T(1,128)S(1)}, f32[1,7168]{1,0:T(1,128)S(1)}, u32[]{:S(2)}, u32[]{:S(2)}) collective-permute-start(f32[1,7168]{1,0:T(1,128)S(1)} %bitcast.74), channel_id=1, source_target_pairs={{0,1},{1,2},{2,3},{3,0},{4,5},{5,6},{6,7},{7,4},{8,9},{9,10},{10,1... | collective-permute-start | bytes 86024 | tf_op jit(solution)/shard_map/while/body/eval_jaxpr/ppermute | solution.py:36
  77.2 3.9 %collective-permute-start = (f32[1,7168]{1,0:T(1,128)S(1)}, f32[1,7168]{1,0:T(1,128)S(1)}, u32[]{:S(2)}, u32[]{:S(2)}) collective-permute-start(f32[1,7168]{1,0:T(1,128)S(1)} %bitcast.72), channel_id=1, source_target_pairs={{0,3},{1,0},{2,1},{3,2},{4,7},{5,4},{6,5},{7,6},{8,11},{9,8},{10,9... | collective-permute-start | bytes 86024 | tf_op jit(solution)/shard_map/while/body/eval_jaxpr/ppermute | solution.py:36
  79.1 5.4 %collective-permute-start.1 = (f32[1,7168]{1,0:T(1,128)S(1)}, f32[1,7168]{1,0:T(1,128)S(1)}, u32[]{:S(2)}, u32[]{:S(2)}) collective-permute-start(f32[1,7168]{1,0:T(1,128)S(1)} %bitcast.73), channel_id=1, source_target_pairs={{0,2},{1,3},{2,0},{3,1},{4,6},{5,7},{6,4},{7,5},{8,10},{9,11},{10,... | collective-permute-start | bytes 86024 | tf_op jit(solution)/shard_map/while/body/eval_jaxpr/ppermute | solution.py:36
  80.0 5.1 %collective-permute-start.2 = (f32[1,7168]{1,0:T(1,128)S(1)}, f32[1,7168]{1,0:T(1,128)S(1)}, u32[]{:S(2)}, u32[]{:S(2)}) collective-permute-start(f32[1,7168]{1,0:T(1,128)S(1)} %bitcast.74), channel_id=1, source_target_pairs={{0,1},{1,2},{2,3},{3,0},{4,5},{5,6},{6,7},{7,4},{8,9},{9,10},{10,1... | collective-permute-start | bytes 86024 | tf_op jit(solution)/shard_map/while/body/eval_jaxpr/ppermute | solution.py:36
  102.5 3.9 %collective-permute-start = (f32[1,7168]{1,0:T(1,128)S(1)}, f32[1,7168]{1,0:T(1,128)S(1)}, u32[]{:S(2)}, u32[]{:S(2)}) collective-permute-start(f32[1,7168]{1,0:T(1,128)S(1)} %bitcast.72), channel_id=1, source_target_pairs={{0,3},{1,0},{2,1},{3,2},{4,7},{5,4},{6,5},{7,6},{8,11},{9,8},{10,9... | collective-permute-start | bytes 86024 | tf_op jit(solution)/shard_map/while/body/eval_jaxpr/ppermute | solution.py:36
  103.4 5.4 %collective-permute-start.1 = (f32[1,7168]{1,0:T(1,128)S(1)}, f32[1,7168]{1,0:T(1,128)S(1)}, u32[]{:S(2)}, u32[]{:S(2)}) collective-permute-start(f32[1,7168]{1,0:T(1,128)S(1)} %bitcast.73), channel_id=1, source_target_pairs={{0,2},{1,3},{2,0},{3,1},{4,6},{5,7},{6,4},{7,5},{8,10},{9,11},{10,... | collective-permute-start | bytes 86024 | tf_op jit(solution)/shard_map/while/body/eval_jaxpr/ppermute | solution.py:36
  104.3 5.1 %collective-permute-start.2 = (f32[1,7168]{1,0:T(1,128)S(1)}, f32[1,7168]{1,0:T(1,128)S(1)}, u32[]{:S(2)}, u32[]{:S(2)}) collective-permute-start(f32[1,7168]{1,0:T(1,128)S(1)} %bitcast.74), channel_id=1, source_target_pairs={{0,1},{1,2},{2,3},{3,0},{4,5},{5,6},{6,7},{7,4},{8,9},{9,10},{10,1... | collective-permute-start | bytes 86024 | tf_op jit(solution)/shard_map/while/body/eval_jaxpr/ppermute | solution.py:36
  126.8 3.9 %collective-permute-start = (f32[1,7168]{1,0:T(1,128)S(1)}, f32[1,7168]{1,0:T(1,128)S(1)}, u32[]{:S(2)}, u32[]{:S(2)}) collective-permute-start(f32[1,7168]{1,0:T(1,128)S(1)} %bitcast.72), channel_id=1, source_target_pairs={{0,3},{1,0},{2,1},{3,2},{4,7},{5,4},{6,5},{7,6},{8,11},{9,8},{10,9... | collective-permute-start | bytes 86024 | tf_op jit(solution)/shard_map/while/body/eval_jaxpr/ppermute | solution.py:36
  128.6 5.4 %collective-permute-start.1 = (f32[1,7168]{1,0:T(1,128)S(1)}, f32[1,7168]{1,0:T(1,128)S(1)}, u32[]{:S(2)}, u32[]{:S(2)}) collective-permute-start(f32[1,7168]{1,0:T(1,128)S(1)} %bitcast.73), channel_id=1, source_target_pairs={{0,2},{1,3},{2,0},{3,1},{4,6},{5,7},{6,4},{7,5},{8,10},{9,11},{10,... | collective-permute-start | bytes 86024 | tf_op jit(solution)/shard_map/while/body/eval_jaxpr/ppermute | solution.py:36
  129.6 5.1 %collective-permute-start.2 = (f32[1,7168]{1,0:T(1,128)S(1)}, f32[1,7168]{1,0:T(1,128)S(1)}, u32[]{:S(2)}, u32[]{:S(2)}) collective-permute-start(f32[1,7168]{1,0:T(1,128)S(1)} %bitcast.74), channel_id=1, source_target_pairs={{0,1},{1,2},{2,3},{3,0},{4,5},{5,6},{6,7},{7,4},{8,9},{9,10},{10,1... | collective-permute-start | bytes 86024 | tf_op jit(solution)/shard_map/while/body/eval_jaxpr/ppermute | solution.py:36
  189.4 12.3 %copy-start.1 = (bf16[1,7168,512]{2,1,0:T(8,128)(2,1)S(1)}, bf16[1,7168,512]{2,1,0:T(8,128)(2,1)}, u32[]{:S(2)}) copy-start(bf16[1,7168,512]{2,1,0:T(8,128)(2,1)} %get-tuple-element.170) | copy-start | bytes 22020100
  189.4 12.3 %copy-start.2 = (f32[1,7168]{1,0:T(1,128)S(1)}, f32[1,7168]{1,0:T(1,128)}, u32[]{:S(2)}) copy-start(f32[1,7168]{1,0:T(1,128)} %get-tuple-element.80) | copy-start | bytes 86020

commit v2 on v1

--- a/solution.py
+++ b/solution.py
@@ -81,8 +81,10 @@
     up_eq = (up_weight.astype(jnp.float32) * row_scale[:, :, None] * up_cols[:, None, :]).astype(
         jnp.bfloat16
     )
-    gate_act = jnp.einsum("ensd,edf->ensf", routed, gate_eq, preferred_element_type=jnp.float32)
-    up_act = jnp.einsum("ensd,edf->ensf", routed, up_eq, preferred_element_type=jnp.float32)
+    both_eq = lax.optimization_barrier(jnp.concatenate([gate_eq, up_eq], axis=2))
+    act = jnp.einsum("ensd,edf->ensf", routed, both_eq, preferred_element_type=jnp.float32)
+    gate_act = act[..., :ff_local]
+    up_act = act[..., ff_local:]
     return (jax.nn.silu(gate_act) * up_act).astype(jnp.bfloat16)
 
 

time: 213 us -> 208 us (0.977)
  other arithmetic: 89.3 us -> 105 us
  waiting for transfers between devices: 68.2 us -> 54.4 us
  matrix products: 29.2 us -> 22.2 us
    all_to_all x1, waiting for transfers between devices: 46.3 us -> 32.4 us  [shards(): lax.all_to_all(outgoing, 'expert', split_axis=0, concat_axis=1, tiled=True)]
    convert_element_type x0 -> x2, other arithmetic: none -> 8.84 us  [the longest x1 7.45 us: shards(): gate_eq = (gate_weight.astype(jnp.float32) * row_scale[:, :, None] * gate...]
    dot_general x2 -> x1, matrix products: 23.6 us -> 16.5 us  [shards(): jnp.einsum('ensd,edf->ensf', routed, both_eq, preferred_element_type=jnp....]
    concatenate x0 -> x1, other arithmetic: none -> 6.5 us  [shards(): jnp.concatenate([gate_eq, up_eq], axis=2)]
  transfers between devices with their start and end apart: 16 -> 16, of which waited for: 15 -> 15; matrix products, arithmetic and copies ran while one was open for 41% -> 49% of each run, Pallas kernels for 0% -> 0%
where the time goes in v2:
time: 208 us; the launch traced here: 207 us
  other arithmetic  105 us (50%)
  waiting for transfers between devices  54.4 us (26%)
  starting transfers between devices  24.1 us (12%)
  matrix products  22.2 us (11%)
    reduce_sum x5, other arithmetic, row_terms(): return jnp.sum(values * values * cols_sq[:, None, :], axis=2)  45.5 us
    reduce_sum x5, other arithmetic, col_terms(): return jnp.sum(values * values * scale_sq[:, :, None], axis=1)  37.9 us
    all_to_all x1, waiting for transfers between devices, shards(): lax.all_to_all(outgoing, 'expert', split_axis=0, concat_axis=1, tiled=True)  32.4 us
    ppermute x15, waiting for transfers between devices, hidden_sum(): lax.ppermute(values, 'hidden', [(i, (i + shift) % n) for i in range(n)])  22 us
    dot_general x1, matrix products, shards(): jnp.einsum('ensd,edf->ensf', routed, both_eq, preferred_element_type=jnp....  16.5 us
    ppermute x15, starting transfers between devices, hidden_sum(): lax.ppermute(values, 'hidden', [(i, (i + shift) % n) for i in range(n)])  16.1 us
    all_to_all x1, starting transfers between devices, shards(): lax.all_to_all(outgoing, 'expert', split_axis=0, concat_axis=1, tiled=True)  8.03 us
    convert_element_type x1, other arithmetic, shards(): gate_eq = (gate_weight.astype(jnp.float32) * row_scale[:, :, None] * gate...  7.45 us
  transfers between devices with their start and end apart: 16, of which 15 were waited for; matrix products, arithmetic and copies ran while one was open for 49% of the time, Pallas kernels for 0%

profile of v2, /device:TPU:48, one launch (start us, length us, event | category | flops | bytes accessed | tf_op | source)
XLA Modules:
  0.0 207.4 jit_solution(6090679004832156550)
XLA Ops:
  1.2 1.2 reduce-window.6
  3.9 5.7 %fusion.3 = bf16[32,1,24,7168]{3,2,1,0:T(8,128)(2,1)} fusion(pred[32,24,64]{2,1,0:T(8,128)(4,1)S(1)} %and_reduce_fusion, bf16[64,7168]{1,0:T(8,128)(2,1)S(1)} %copy-done), kind=kOutput, calls=%fused_computation.16 | convolution fusion | flops 710148096 | bytes 11976704 | tf_op jit(solution)/shard_map/est,td->esd/dot_general | solution.py:28
  9.6 8.0 %all-to-all-start = ((bf16[32,1,24,7168]{3,2,1,0:T(8,128)(2,1)}), bf16[32,1,24,7168]{3,2,1,0:T(8,128)(2,1)}, u32[]{:S(2)}, u32[]{:S(2)}) async-start(bf16[32,1,24,7168]{3,2,1,0:T(8,128)(2,1)} %fusion.3), calls=%async_computation | async-start | bytes 22020096 | tf_op jit(solution)/shard_map/all_to_all | solution.py:59
  17.6 125.4 %while.16 = (s32[]{:T(128)}, f32[1,512]{1,0:T(1,128)S(1)}, f32[1,512]{1,0:T(1,128)S(1)}, f32[1,7168]{1,0:T(1,128)}, bf16[1,7168,512]{2,1,0:T(8,128)(2,1)}, /*index=5*/bf16[1,7168,512]{2,1,0:T(8,128)(2,1)}, s32[]{:T(128)}) while((s32[]{:T(128)}, f32[1,512]{1,0:T(1,128)S(1)}, f32[1,512]{1,0:T(1,128)S(1)}, f32[1,7168]{1,0:T(1,128)}, ...), condition=%wide.region_9.10_spmd, body=%wide.region_4.9_spmd.sunk | while | flops 58757120 | bytes 30077124 | solution.py:77
  17.7 9.1 %multiply_reduce_fusion.6 = (f32[7168]{0:T(1024)S(1)}, f32[7168]{0:T(1024)S(1)}) fusion(bf16[1,7168,512]{2,1,0:T(8,128)(2,1)} %get-tuple-element.169, f32[512]{0:T(512)S(1)} %bitcast.70, f32[512]{0:T(512)S(1)} %bitcast.71, bf16[1,7168,512]{2,1,0:T(8,128)(2,1)} %get-tuple-element.168), kind=kLoop, calls=%fused_computation.2.clone.1 | loop fusion | flops 29345792 | bytes 14741504 | tf_op jit(solution)/shard_map/while/body/eval_jaxpr/reduce_sum | solution.py:42
  26.8 2.8 %collective-permute-start = (f32[1,7168]{1,0:T(1,128)S(1)}, f32[1,7168]{1,0:T(1,128)S(1)}, u32[]{:S(2)}, u32[]{:S(2)}) collective-permute-start(f32[1,7168]{1,0:T(1,128)S(1)} %bitcast.62), channel_id=1, source_target_pairs={{0,3},{1,0},{2,1},{3,2},{4,7},{5,4},{6,5},{7,6},{8,11},{9,8},{10,9... | collective-permute-start | bytes 86024 | tf_op jit(solution)/shard_map/while/body/eval_jaxpr/ppermute | solution.py:36
  31.3 3.6 %collective-permute-done.1 = f32[1,7168]{1,0:T(1,128)S(1)} collective-permute-done((f32[1,7168]{1,0:T(1,128)S(1)}, f32[1,7168]{1,0:T(1,128)S(1)}, u32[]{:S(2)}, u32[]{:S(2)}) %collective-permute-start.1) | collective-permute-done | bytes 28704 | tf_op jit(solution)/shard_map/while/body/eval_jaxpr/ppermute | solution.py:36
  36.2 7.6 %multiply_reduce_fusion.7 = (f32[512]{0:T(512)S(1)}, f32[512]{0:T(512)S(1)}) fusion(bf16[1,7168,512]{2,1,0:T(8,128)(2,1)} %get-tuple-element.169, f32[7168]{0:T(1024)S(1)} %bitcast.61, bf16[1,7168,512]{2,1,0:T(8,128)(2,1)} %get-tuple-element.168), kind=kLoop, calls=%fused_computation.clone.1 | loop fusion | flops 29359104 | bytes 14712832 | tf_op jit(solution)/shard_map/while/body/eval_jaxpr/reduce_sum | solution.py:47
  43.8 9.1 %multiply_reduce_fusion.6 = (f32[7168]{0:T(1024)S(1)}, f32[7168]{0:T(1024)S(1)}) fusion(bf16[1,7168,512]{2,1,0:T(8,128)(2,1)} %get-tuple-element.169, f32[512]{0:T(512)S(1)} %bitcast.70, f32[512]{0:T(512)S(1)} %bitcast.71, bf16[1,7168,512]{2,1,0:T(8,128)(2,1)} %get-tuple-element.168), kind=kLoop, calls=%fused_computation.2.clone.1 | loop fusion | flops 29345792 | bytes 14741504 | tf_op jit(solution)/shard_map/while/body/eval_jaxpr/reduce_sum | solution.py:42
  53.4 1.4 collective-permute-start.1
  54.8 1.2 collective-permute-start.2
  56.9 1.9 collective-permute-done.1
  58.8 1.1 collective-permute-done.2
  60.5 7.6 %multiply_reduce_fusion.7 = (f32[512]{0:T(512)S(1)}, f32[512]{0:T(512)S(1)}) fusion(bf16[1,7168,512]{2,1,0:T(8,128)(2,1)} %get-tuple-element.169, f32[7168]{0:T(1024)S(1)} %bitcast.61, bf16[1,7168,512]{2,1,0:T(8,128)(2,1)} %get-tuple-element.168), kind=kLoop, calls=%fused_computation.clone.1 | loop fusion | flops 29359104 | bytes 14712832 | tf_op jit(solution)/shard_map/while/body/eval_jaxpr/reduce_sum | solution.py:47
  68.2 9.1 %multiply_reduce_fusion.6 = (f32[7168]{0:T(1024)S(1)}, f32[7168]{0:T(1024)S(1)}) fusion(bf16[1,7168,512]{2,1,0:T(8,128)(2,1)} %get-tuple-element.169, f32[512]{0:T(512)S(1)} %bitcast.70, f32[512]{0:T(512)S(1)} %bitcast.71, bf16[1,7168,512]{2,1,0:T(8,128)(2,1)} %get-tuple-element.168), kind=kLoop, calls=%fused_computation.2.clone.1 | loop fusion | flops 29345792 | bytes 14741504 | tf_op jit(solution)/shard_map/while/body/eval_jaxpr/reduce_sum | solution.py:42
  77.3 1.8 collective-permute-start
  80.1 1.2 collective-permute-done
  81.3 3.2 %collective-permute-done.1 = f32[1,7168]{1,0:T(1,128)S(1)} collective-permute-done((f32[1,7168]{1,0:T(1,128)S(1)}, f32[1,7168]{1,0:T(1,128)S(1)}, u32[]{:S(2)}, u32[]{:S(2)}) %collective-permute-start.1) | collective-permute-done | bytes 28704 | tf_op jit(solution)/shard_map/while/body/eval_jaxpr/ppermute | solution.py:36
  85.8 7.6 %multiply_reduce_fusion.7 = (f32[512]{0:T(512)S(1)}, f32[512]{0:T(512)S(1)}) fusion(bf16[1,7168,512]{2,1,0:T(8,128)(2,1)} %get-tuple-element.169, f32[7168]{0:T(1024)S(1)} %bitcast.61, bf16[1,7168,512]{2,1,0:T(8,128)(2,1)} %get-tuple-element.168), kind=kLoop, calls=%fused_computation.clone.1 | loop fusion | flops 29359104 | bytes 14712832 | tf_op jit(solution)/shard_map/while/body/eval_jaxpr/reduce_sum | solution.py:47
  93.5 9.1 %multiply_reduce_fusion.6 = (f32[7168]{0:T(1024)S(1)}, f32[7168]{0:T(1024)S(1)}) fusion(bf16[1,7168,512]{2,1,0:T(8,128)(2,1)} %get-tuple-element.169, f32[512]{0:T(512)S(1)} %bitcast.70, f32[512]{0:T(512)S(1)} %bitcast.71, bf16[1,7168,512]{2,1,0:T(8,128)(2,1)} %get-tuple-element.168), kind=kLoop, calls=%fused_computation.2.clone.1 | loop fusion | flops 29345792 | bytes 14741504 | tf_op jit(solution)/shard_map/while/body/eval_jaxpr/reduce_sum | solution.py:42
  104.4 1.1 collective-permute-start.2
  106.5 2.3 %collective-permute-done.1 = f32[1,7168]{1,0:T(1,128)S(1)} collective-permute-done((f32[1,7168]{1,0:T(1,128)S(1)}, f32[1,7168]{1,0:T(1,128)S(1)}, u32[]{:S(2)}, u32[]{:S(2)}) %collective-permute-start.1) | collective-permute-done | bytes 28704 | tf_op jit(solution)/shard_map/while/body/eval_jaxpr/ppermute | solution.py:36
  110.2 7.6 %multiply_reduce_fusion.7 = (f32[512]{0:T(512)S(1)}, f32[512]{0:T(512)S(1)}) fusion(bf16[1,7168,512]{2,1,0:T(8,128)(2,1)} %get-tuple-element.169, f32[7168]{0:T(1024)S(1)} %bitcast.61, bf16[1,7168,512]{2,1,0:T(8,128)(2,1)} %get-tuple-element.168), kind=kLoop, calls=%fused_computation.clone.1 | loop fusion | flops 29359104 | bytes 14712832 | tf_op jit(solution)/shard_map/while/body/eval_jaxpr/reduce_sum | solution.py:47
  117.8 9.1 %multiply_reduce_fusion.6 = (f32[7168]{0:T(1024)S(1)}, f32[7168]{0:T(1024)S(1)}) fusion(bf16[1,7168,512]{2,1,0:T(8,128)(2,1)} %get-tuple-element.169, f32[512]{0:T(512)S(1)} %bitcast.70, f32[512]{0:T(512)S(1)} %bitcast.71, bf16[1,7168,512]{2,1,0:T(8,128)(2,1)} %get-tuple-element.168), kind=kLoop, calls=%fused_computation.2.clone.1 | loop fusion | flops 29345792 | bytes 14741504 | tf_op jit(solution)/shard_map/while/body/eval_jaxpr/reduce_sum | solution.py:42
  127.0 1.8 collective-permute-start
  130.9 3.2 %collective-permute-done.1 = f32[1,7168]{1,0:T(1,128)S(1)} collective-permute-done((f32[1,7168]{1,0:T(1,128)S(1)}, f32[1,7168]{1,0:T(1,128)S(1)}, u32[]{:S(2)}, u32[]{:S(2)}) %collective-permute-start.1) | collective-permute-done | bytes 28704 | tf_op jit(solution)/shard_map/while/body/eval_jaxpr/ppermute | solution.py:36
  135.4 7.6 %multiply_reduce_fusion.7 = (f32[512]{0:T(512)S(1)}, f32[512]{0:T(512)S(1)}) fusion(bf16[1,7168,512]{2,1,0:T(8,128)(2,1)} %get-tuple-element.169, f32[7168]{0:T(1024)S(1)} %bitcast.61, bf16[1,7168,512]{2,1,0:T(8,128)(2,1)} %get-tuple-element.168), kind=kLoop, calls=%fused_computation.clone.1 | loop fusion | flops 29359104 | bytes 14712832 | tf_op jit(solution)/shard_map/while/body/eval_jaxpr/reduce_sum | solution.py:47
  143.1 7.4 %multiply_convert_fusion.1 = (bf16[1,7168,512]{2,1,0:T(8,128)(2,1)S(1)}, bf16[1,7168,512]{2,1,0:T(8,128)(2,1)S(1)}) fusion(bf16[1,7168,512]{2,1,0:T(8,128)(2,1)} %get-tuple-element.171, f32[512]{0:T(512)S(1)} %bitcast.67, f32[7168]{0:T(1024)} %bitcast.72, f32[512]{0:T(512)S(1)} %bitcast.69, bf16[1,7168,512]{2,1,0:T(8,128)(2,1)} %get-tuple-element.172), kind=kLoop, calls=%fused_computation.13 | loop fusion | flops 29360128 | bytes 29392896 | tf_op jit(solution)/shard_map/convert_element_type | solution.py:80
  150.5 6.5 %pad_maximum_fusion = bf16[1,7168,1024]{2,1,0:T(8,128)(2,1)} fusion(bf16[1,7168,512]{2,1,0:T(8,128)(2,1)S(1)} %get-tuple-element.102, bf16[1,7168,512]{2,1,0:T(8,128)(2,1)S(1)} %get-tuple-element.101), kind=kLoop, calls=%fused_computation.9 | loop fusion | flops 29360128 | bytes 29360128 | tf_op jit(solution)/shard_map/concatenate | solution.py:84
  157.0 32.4 %all-to-all-done = bf16[32,1,24,7168]{3,2,1,0:T(8,128)(2,1)} async-done(((bf16[32,1,24,7168]{3,2,1,0:T(8,128)(2,1)}), bf16[32,1,24,7168]{3,2,1,0:T(8,128)(2,1)}, u32[]{:S(2)}, u32[]{:S(2)}) %all-to-all-start) | async-done | bytes 11010080 | tf_op jit(solution)/shard_map/all_to_all | solution.py:59
  189.4 16.5 %fusion.4 = f32[1,32,24,1024]{3,2,1,0:T(8,128)S(1)} fusion(bf16[1,7168,1024]{2,1,0:T(8,128)(2,1)} %pad_maximum_fusion, bf16[32,1,24,7168]{3,2,1,0:T(8,128)(2,1)} %all-to-all-done), kind=kOutput, calls=%fused_computation.18 | convolution fusion | flops 11274289152 | bytes 28835840 | tf_op jit(solution)/shard_map/ensd,edf->ensf/dot_general | solution.py:85
  206.0 1.4 fusion.9
  (68 shorter events, 17.6 us)
Async XLA Ops:
  0.0 3.9 %copy-start = (bf16[64,7168]{1,0:T(8,128)(2,1)S(1)}, bf16[64,7168]{1,0:T(8,128)(2,1)}, u32[]{:S(2)}) copy-start(bf16[64,7168]{1,0:T(8,128)(2,1)} %param.6) | copy-start | bytes 2752516
  9.6 179.9 %all-to-all-start = ((bf16[32,1,24,7168]{3,2,1,0:T(8,128)(2,1)}), bf16[32,1,24,7168]{3,2,1,0:T(8,128)(2,1)}, u32[]{:S(2)}, u32[]{:S(2)}) async-start(bf16[32,1,24,7168]{3,2,1,0:T(8,128)(2,1)} %fusion.3), calls=%async_computation | async-start | bytes 22020096 | tf_op jit(solution)/shard_map/all_to_all | solution.py:59
  26.8 4.6 %collective-permute-start = (f32[1,7168]{1,0:T(1,128)S(1)}, f32[1,7168]{1,0:T(1,128)S(1)}, u32[]{:S(2)}, u32[]{:S(2)}) collective-permute-start(f32[1,7168]{1,0:T(1,128)S(1)} %bitcast.62), channel_id=1, source_target_pairs={{0,3},{1,0},{2,1},{3,2},{4,7},{5,4},{6,5},{7,6},{8,11},{9,8},{10,9... | collective-permute-start | bytes 86024 | tf_op jit(solution)/shard_map/while/body/eval_jaxpr/ppermute | solution.py:36
  29.6 5.4 %collective-permute-start.1 = (f32[1,7168]{1,0:T(1,128)S(1)}, f32[1,7168]{1,0:T(1,128)S(1)}, u32[]{:S(2)}, u32[]{:S(2)}) collective-permute-start(f32[1,7168]{1,0:T(1,128)S(1)} %bitcast.63), channel_id=1, source_target_pairs={{0,2},{1,3},{2,0},{3,1},{4,6},{5,7},{6,4},{7,5},{8,10},{9,11},{10,... | collective-permute-start | bytes 86024 | tf_op jit(solution)/shard_map/while/body/eval_jaxpr/ppermute | solution.py:36
  30.4 5.1 %collective-permute-start.2 = (f32[1,7168]{1,0:T(1,128)S(1)}, f32[1,7168]{1,0:T(1,128)S(1)}, u32[]{:S(2)}, u32[]{:S(2)}) collective-permute-start(f32[1,7168]{1,0:T(1,128)S(1)} %bitcast.64), channel_id=1, source_target_pairs={{0,1},{1,2},{2,3},{3,0},{4,5},{5,6},{6,7},{7,4},{8,9},{9,10},{10,1... | collective-permute-start | bytes 86024 | tf_op jit(solution)/shard_map/while/body/eval_jaxpr/ppermute | solution.py:36
  53.0 3.9 %collective-permute-start = (f32[1,7168]{1,0:T(1,128)S(1)}, f32[1,7168]{1,0:T(1,128)S(1)}, u32[]{:S(2)}, u32[]{:S(2)}) collective-permute-start(f32[1,7168]{1,0:T(1,128)S(1)} %bitcast.62), channel_id=1, source_target_pairs={{0,3},{1,0},{2,1},{3,2},{4,7},{5,4},{6,5},{7,6},{8,11},{9,8},{10,9... | collective-permute-start | bytes 86024 | tf_op jit(solution)/shard_map/while/body/eval_jaxpr/ppermute | solution.py:36
  53.4 5.4 %collective-permute-start.1 = (f32[1,7168]{1,0:T(1,128)S(1)}, f32[1,7168]{1,0:T(1,128)S(1)}, u32[]{:S(2)}, u32[]{:S(2)}) collective-permute-start(f32[1,7168]{1,0:T(1,128)S(1)} %bitcast.63), channel_id=1, source_target_pairs={{0,2},{1,3},{2,0},{3,1},{4,6},{5,7},{6,4},{7,5},{8,10},{9,11},{10,... | collective-permute-start | bytes 86024 | tf_op jit(solution)/shard_map/while/body/eval_jaxpr/ppermute | solution.py:36
  54.8 5.1 %collective-permute-start.2 = (f32[1,7168]{1,0:T(1,128)S(1)}, f32[1,7168]{1,0:T(1,128)S(1)}, u32[]{:S(2)}, u32[]{:S(2)}) collective-permute-start(f32[1,7168]{1,0:T(1,128)S(1)} %bitcast.64), channel_id=1, source_target_pairs={{0,1},{1,2},{2,3},{3,0},{4,5},{5,6},{6,7},{7,4},{8,9},{9,10},{10,1... | collective-permute-start | bytes 86024 | tf_op jit(solution)/shard_map/while/body/eval_jaxpr/ppermute | solution.py:36
  77.3 3.9 %collective-permute-start = (f32[1,7168]{1,0:T(1,128)S(1)}, f32[1,7168]{1,0:T(1,128)S(1)}, u32[]{:S(2)}, u32[]{:S(2)}) collective-permute-start(f32[1,7168]{1,0:T(1,128)S(1)} %bitcast.62), channel_id=1, source_target_pairs={{0,3},{1,0},{2,1},{3,2},{4,7},{5,4},{6,5},{7,6},{8,11},{9,8},{10,9... | collective-permute-start | bytes 86024 | tf_op jit(solution)/shard_map/while/body/eval_jaxpr/ppermute | solution.py:36
  79.1 5.4 %collective-permute-start.1 = (f32[1,7168]{1,0:T(1,128)S(1)}, f32[1,7168]{1,0:T(1,128)S(1)}, u32[]{:S(2)}, u32[]{:S(2)}) collective-permute-start(f32[1,7168]{1,0:T(1,128)S(1)} %bitcast.63), channel_id=1, source_target_pairs={{0,2},{1,3},{2,0},{3,1},{4,6},{5,7},{6,4},{7,5},{8,10},{9,11},{10,... | collective-permute-start | bytes 86024 | tf_op jit(solution)/shard_map/while/body/eval_jaxpr/ppermute | solution.py:36
  80.0 5.1 %collective-permute-start.2 = (f32[1,7168]{1,0:T(1,128)S(1)}, f32[1,7168]{1,0:T(1,128)S(1)}, u32[]{:S(2)}, u32[]{:S(2)}) collective-permute-start(f32[1,7168]{1,0:T(1,128)S(1)} %bitcast.64), channel_id=1, source_target_pairs={{0,1},{1,2},{2,3},{3,0},{4,5},{5,6},{6,7},{7,4},{8,9},{9,10},{10,1... | collective-permute-start | bytes 86024 | tf_op jit(solution)/shard_map/while/body/eval_jaxpr/ppermute | solution.py:36
  102.6 3.9 %collective-permute-start = (f32[1,7168]{1,0:T(1,128)S(1)}, f32[1,7168]{1,0:T(1,128)S(1)}, u32[]{:S(2)}, u32[]{:S(2)}) collective-permute-start(f32[1,7168]{1,0:T(1,128)S(1)} %bitcast.62), channel_id=1, source_target_pairs={{0,3},{1,0},{2,1},{3,2},{4,7},{5,4},{6,5},{7,6},{8,11},{9,8},{10,9... | collective-permute-start | bytes 86024 | tf_op jit(solution)/shard_map/while/body/eval_jaxpr/ppermute | solution.py:36
  103.5 5.4 %collective-permute-start.1 = (f32[1,7168]{1,0:T(1,128)S(1)}, f32[1,7168]{1,0:T(1,128)S(1)}, u32[]{:S(2)}, u32[]{:S(2)}) collective-permute-start(f32[1,7168]{1,0:T(1,128)S(1)} %bitcast.63), channel_id=1, source_target_pairs={{0,2},{1,3},{2,0},{3,1},{4,6},{5,7},{6,4},{7,5},{8,10},{9,11},{10,... | collective-permute-start | bytes 86024 | tf_op jit(solution)/shard_map/while/body/eval_jaxpr/ppermute | solution.py:36
  104.4 5.1 %collective-permute-start.2 = (f32[1,7168]{1,0:T(1,128)S(1)}, f32[1,7168]{1,0:T(1,128)S(1)}, u32[]{:S(2)}, u32[]{:S(2)}) collective-permute-start(f32[1,7168]{1,0:T(1,128)S(1)} %bitcast.64), channel_id=1, source_target_pairs={{0,1},{1,2},{2,3},{3,0},{4,5},{5,6},{6,7},{7,4},{8,9},{9,10},{10,1... | collective-permute-start | bytes 86024 | tf_op jit(solution)/shard_map/while/body/eval_jaxpr/ppermute | solution.py:36
  127.0 3.9 %collective-permute-start = (f32[1,7168]{1,0:T(1,128)S(1)}, f32[1,7168]{1,0:T(1,128)S(1)}, u32[]{:S(2)}, u32[]{:S(2)}) collective-permute-start(f32[1,7168]{1,0:T(1,128)S(1)} %bitcast.62), channel_id=1, source_target_pairs={{0,3},{1,0},{2,1},{3,2},{4,7},{5,4},{6,5},{7,6},{8,11},{9,8},{10,9... | collective-permute-start | bytes 86024 | tf_op jit(solution)/shard_map/while/body/eval_jaxpr/ppermute | solution.py:36
  128.8 5.4 %collective-permute-start.1 = (f32[1,7168]{1,0:T(1,128)S(1)}, f32[1,7168]{1,0:T(1,128)S(1)}, u32[]{:S(2)}, u32[]{:S(2)}) collective-permute-start(f32[1,7168]{1,0:T(1,128)S(1)} %bitcast.63), channel_id=1, source_target_pairs={{0,2},{1,3},{2,0},{3,1},{4,6},{5,7},{6,4},{7,5},{8,10},{9,11},{10,... | collective-permute-start | bytes 86024 | tf_op jit(solution)/shard_map/while/body/eval_jaxpr/ppermute | solution.py:36
  129.7 5.1 %collective-permute-start.2 = (f32[1,7168]{1,0:T(1,128)S(1)}, f32[1,7168]{1,0:T(1,128)S(1)}, u32[]{:S(2)}, u32[]{:S(2)}) collective-permute-start(f32[1,7168]{1,0:T(1,128)S(1)} %bitcast.64), channel_id=1, source_target_pairs={{0,1},{1,2},{2,3},{3,0},{4,5},{5,6},{6,7},{7,4},{8,9},{9,10},{10,1... | collective-permute-start | bytes 86024 | tf_op jit(solution)/shard_map/while/body/eval_jaxpr/ppermute | solution.py:36
  189.4 17.9 %copy-start.1 = (bf16[64,7168]{1,0:T(8,128)(2,1)S(1)}, bf16[64,7168]{1,0:T(8,128)(2,1)}, u32[]{:S(2)}) copy-start(bf16[64,7168]{1,0:T(8,128)(2,1)} %param.6) | copy-start | bytes 2752516

commit v3 on v2

--- a/solution.py
+++ b/solution.py
@@ -1,6 +1,8 @@
 import jax
 import jax.numpy as jnp
 from jax import lax
+from jax.experimental import pallas as pl
+from jax.experimental.pallas import tpu as pltpu
 from jax.sharding import PartitionSpec as P
 
 TOPK = 8
@@ -11,6 +13,48 @@
 
 
 EPS = 1e-06
+K_TILE = 1024
+
+
+def gated_body(rows_ref, gate_ref, up_ref, out_ref, gate_acc, up_acc):
+    step = pl.program_id(0)
+
+    @pl.when(step == 0)
+    def _():
+        gate_acc[...] = jnp.zeros_like(gate_acc)
+        up_acc[...] = jnp.zeros_like(up_acc)
+
+    rows = rows_ref[...]
+    gate_acc[...] += jnp.dot(rows, gate_ref[...], preferred_element_type=jnp.float32)
+    up_acc[...] += jnp.dot(rows, up_ref[...], preferred_element_type=jnp.float32)
+
+    @pl.when(step == pl.num_programs(0) - 1)
+    def _():
+        g = gate_acc[...]
+        out_ref[...] = (g / (1.0 + jnp.exp(-g)) * up_acc[...]).astype(out_ref.dtype)
+
+
+def gated_matmul(rows, both, ff_local):
+    m, width = rows.shape
+    steps = width // K_TILE
+    return pl.pallas_call(
+        gated_body,
+        grid=(steps,),
+        in_specs=[
+            pl.BlockSpec((m, K_TILE), lambda k: (0, k)),
+            pl.BlockSpec((K_TILE, ff_local), lambda k: (k, 0)),
+            pl.BlockSpec((K_TILE, ff_local), lambda k: (k, 1)),
+        ],
+        out_specs=pl.BlockSpec((m, ff_local), lambda k: (0, 0)),
+        out_shape=jax.ShapeDtypeStruct((m, ff_local), jnp.bfloat16),
+        scratch_shapes=[pltpu.VMEM((m, ff_local), jnp.float32), pltpu.VMEM((m, ff_local), jnp.float32)],
+        compiler_params=pltpu.CompilerParams(dimension_semantics=("arbitrary",)),
+        cost_estimate=pl.CostEstimate(
+            flops=2 * m * width * 2 * ff_local,
+            transcendentals=m * ff_local,
+            bytes_accessed=2 * (m * width + width * 2 * ff_local + m * ff_local),
+        ),
+    )(rows, both, both)
 
 
 def dispatch_rows(block_ids, tokens):
@@ -82,10 +126,9 @@
         jnp.bfloat16
     )
     both_eq = lax.optimization_barrier(jnp.concatenate([gate_eq, up_eq], axis=2))
-    act = jnp.einsum("ensd,edf->ensf", routed, both_eq, preferred_element_type=jnp.float32)
-    gate_act = act[..., :ff_local]
-    up_act = act[..., ff_local:]
-    return (jax.nn.silu(gate_act) * up_act).astype(jnp.bfloat16)
+    rows = routed.reshape(-1, width)
+    hidden = gated_matmul(rows, both_eq.reshape(width, 2 * ff_local), ff_local)
+    return hidden.reshape(routed.shape[:3] + (ff_local,))
 
 
 def solution(mesh):

time: 208 us -> 209 us (level)
  Pallas kernels: 0 us -> 16.9 us
  matrix products: 22.2 us -> 5.66 us
  starting transfers between devices: 24.1 us -> 30.6 us
  waiting for transfers between devices: 54.4 us -> 50.2 us
    pallas_call x0 -> x1, Pallas kernels: none -> 16.9 us  [gated_matmul(): pl.pallas_call(gated_body, grid=(steps,), in_specs=[pl.BlockSpec((m, K_TI...]
    dot_general x1 -> x0, matrix products: 16.5 us -> none  [shards(): jnp.einsum('ensd,edf->ensf', routed, both_eq, preferred_element_type=jnp....]
    ppermute x15, waiting for transfers between devices: 22 us -> 15 us  [hidden_sum(): lax.ppermute(values, 'hidden', [(i, (i + shift) % n) for i in range(n)])]
    ppermute x15, starting transfers between devices: 16.1 us -> 22.6 us  [hidden_sum(): lax.ppermute(values, 'hidden', [(i, (i + shift) % n) for i in range(n)])]
    all_to_all x1, waiting for transfers between devices: 32.4 us -> 35.3 us  [shards(): lax.all_to_all(outgoing, 'expert', split_axis=0, concat_axis=1, tiled=True)]
  transfers between devices with their start and end apart: 16 -> 16, of which waited for: 15 -> 15; matrix products, arithmetic and copies ran while one was open for 49% -> 48% of each run, Pallas kernels for 0% -> 0%
where the time goes in v3:
time: 209 us
  other arithmetic  103 us (49%)
  waiting for transfers between devices  50.2 us (24%)
  starting transfers between devices  30.6 us (15%)
  Pallas kernels  16.9 us (8%)
  matrix products  5.66 us (3%)
    reduce_sum x5, other arithmetic, row_terms(): return jnp.sum(values * values * cols_sq[:, None, :], axis=2)  45.5 us
    reduce_sum x5, other arithmetic, col_terms(): return jnp.sum(values * values * scale_sq[:, :, None], axis=1)  37.9 us
    all_to_all x1, waiting for transfers between devices, shards(): lax.all_to_all(outgoing, 'expert', split_axis=0, concat_axis=1, tiled=True)  35.3 us
    ppermute x15, starting transfers between devices, hidden_sum(): lax.ppermute(values, 'hidden', [(i, (i + shift) % n) for i in range(n)])  22.6 us
    pallas_call x1, Pallas kernels, gated_matmul(): pl.pallas_call(gated_body, grid=(steps,), in_specs=[pl.BlockSpec((m, K_TI...  16.9 us
    ppermute x15, waiting for transfers between devices, hidden_sum(): lax.ppermute(values, 'hidden', [(i, (i + shift) % n) for i in range(n)])  15 us
    all_to_all x1, starting transfers between devices, shards(): lax.all_to_all(outgoing, 'expert', split_axis=0, concat_axis=1, tiled=True)  8.05 us
    convert_element_type x1, other arithmetic, shards(): gate_eq = (gate_weight.astype(jnp.float32) * row_scale[:, :, None] * gate...  7.46 us
  transfers between devices with their start and end apart: 16, of which 15 were waited for; matrix products, arithmetic and copies ran while one was open for 48% of the time, Pallas kernels for 0%

profile of v3, /device:TPU:48, one launch (start us, length us, event | category | flops | bytes accessed | tf_op | source)
XLA Modules:
  0.0 208.6 jit_solution(2181152756762659690)
XLA Ops:
  3.9 5.7 %fusion = bf16[32,1,24,7168]{3,2,1,0:T(8,128)(2,1)} fusion(pred[32,24,64]{2,1,0:T(8,128)(4,1)S(1)} %and_reduce_fusion, bf16[64,7168]{1,0:T(8,128)(2,1)S(1)} %copy-done), kind=kOutput, calls=%fused_computation.13 | convolution fusion | flops 710148096 | bytes 11976704 | tf_op jit(solution)/shard_map/est,td->esd/dot_general | solution.py:72
  9.6 8.0 %all-to-all-start = ((bf16[32,1,24,7168]{3,2,1,0:T(8,128)(2,1)}), bf16[32,1,24,7168]{3,2,1,0:T(8,128)(2,1)}, u32[]{:S(2)}, u32[]{:S(2)}) async-start(bf16[32,1,24,7168]{3,2,1,0:T(8,128)(2,1)} %fusion), calls=%async_computation | async-start | bytes 22020096 | tf_op jit(solution)/shard_map/all_to_all | solution.py:103
  17.6 124.9 %while.16 = (s32[]{:T(128)}, f32[1,512]{1,0:T(1,128)S(1)}, f32[1,512]{1,0:T(1,128)S(1)}, f32[1,7168]{1,0:T(1,128)}, bf16[1,7168,512]{2,1,0:T(8,128)(2,1)}, /*index=5*/bf16[1,7168,512]{2,1,0:T(8,128)(2,1)}, s32[]{:T(128)}) while((s32[]{:T(128)}, f32[1,512]{1,0:T(1,128)S(1)}, f32[1,512]{1,0:T(1,128)S(1)}, f32[1,7168]{1,0:T(1,128)}, ...), condition=%wide.region_9.10_spmd, body=%wide.region_4.9_spmd.sunk | while | flops 58757120 | bytes 30077124 | solution.py:121
  17.7 9.1 %multiply_reduce_fusion.6 = (f32[7168]{0:T(1024)S(1)}, f32[7168]{0:T(1024)S(1)}) fusion(bf16[1,7168,512]{2,1,0:T(8,128)(2,1)} %get-tuple-element.169, f32[512]{0:T(512)S(1)} %bitcast.62, f32[512]{0:T(512)S(1)} %bitcast.63, bf16[1,7168,512]{2,1,0:T(8,128)(2,1)} %get-tuple-element.168), kind=kLoop, calls=%fused_computation.2.clone.1 | loop fusion | flops 29345792 | bytes 14741504 | tf_op jit(solution)/shard_map/while/body/eval_jaxpr/reduce_sum | solution.py:86
  26.8 1.6 collective-permute-start.2
  28.4 2.7 %collective-permute-start.1 = (f32[1,7168]{1,0:T(1,128)S(1)}, f32[1,7168]{1,0:T(1,128)S(1)}, u32[]{:S(2)}, u32[]{:S(2)}) collective-permute-start(f32[1,7168]{1,0:T(1,128)S(1)} %bitcast.55), channel_id=1, source_target_pairs={{0,2},{1,3},{2,0},{3,1},{4,6},{5,7},{6,4},{7,5},{8,10},{9,11},{10,... | collective-permute-start | bytes 86024 | tf_op jit(solution)/shard_map/while/body/eval_jaxpr/ppermute | solution.py:80
  31.1 1.4 collective-permute-start
  32.5 1.2 collective-permute-done.1
  33.7 1.2 collective-permute-done
  35.6 7.6 %multiply_reduce_fusion.7 = (f32[512]{0:T(512)S(1)}, f32[512]{0:T(512)S(1)}) fusion(bf16[1,7168,512]{2,1,0:T(8,128)(2,1)} %get-tuple-element.169, f32[7168]{0:T(1024)S(1)} %bitcast.53, bf16[1,7168,512]{2,1,0:T(8,128)(2,1)} %get-tuple-element.168), kind=kLoop, calls=%fused_computation.clone.1 | loop fusion | flops 29359104 | bytes 14712832 | tf_op jit(solution)/shard_map/while/body/eval_jaxpr/reduce_sum | solution.py:91
  43.3 9.1 %multiply_reduce_fusion.6 = (f32[7168]{0:T(1024)S(1)}, f32[7168]{0:T(1024)S(1)}) fusion(bf16[1,7168,512]{2,1,0:T(8,128)(2,1)} %get-tuple-element.169, f32[512]{0:T(512)S(1)} %bitcast.62, f32[512]{0:T(512)S(1)} %bitcast.63, bf16[1,7168,512]{2,1,0:T(8,128)(2,1)} %get-tuple-element.168), kind=kLoop, calls=%fused_computation.2.clone.1 | loop fusion | flops 29345792 | bytes 14741504 | tf_op jit(solution)/shard_map/while/body/eval_jaxpr/reduce_sum | solution.py:86
  52.8 3.8 %collective-permute-start.1 = (f32[1,7168]{1,0:T(1,128)S(1)}, f32[1,7168]{1,0:T(1,128)S(1)}, u32[]{:S(2)}, u32[]{:S(2)}) collective-permute-start(f32[1,7168]{1,0:T(1,128)S(1)} %bitcast.55), channel_id=1, source_target_pairs={{0,2},{1,3},{2,0},{3,1},{4,6},{5,7},{6,4},{7,5},{8,10},{9,11},{10,... | collective-permute-start | bytes 86024 | tf_op jit(solution)/shard_map/while/body/eval_jaxpr/ppermute | solution.py:80
  58.8 1.7 collective-permute-done
  61.2 7.6 %multiply_reduce_fusion.7 = (f32[512]{0:T(512)S(1)}, f32[512]{0:T(512)S(1)}) fusion(bf16[1,7168,512]{2,1,0:T(8,128)(2,1)} %get-tuple-element.169, f32[7168]{0:T(1024)S(1)} %bitcast.53, bf16[1,7168,512]{2,1,0:T(8,128)(2,1)} %get-tuple-element.168), kind=kLoop, calls=%fused_computation.clone.1 | loop fusion | flops 29359104 | bytes 14712832 | tf_op jit(solution)/shard_map/while/body/eval_jaxpr/reduce_sum | solution.py:91
  68.8 9.1 %multiply_reduce_fusion.6 = (f32[7168]{0:T(1024)S(1)}, f32[7168]{0:T(1024)S(1)}) fusion(bf16[1,7168,512]{2,1,0:T(8,128)(2,1)} %get-tuple-element.169, f32[512]{0:T(512)S(1)} %bitcast.62, f32[512]{0:T(512)S(1)} %bitcast.63, bf16[1,7168,512]{2,1,0:T(8,128)(2,1)} %get-tuple-element.168), kind=kLoop, calls=%fused_computation.2.clone.1 | loop fusion | flops 29345792 | bytes 14741504 | tf_op jit(solution)/shard_map/while/body/eval_jaxpr/reduce_sum | solution.py:86
  78.0 2.7 %collective-permute-start.1 = (f32[1,7168]{1,0:T(1,128)S(1)}, f32[1,7168]{1,0:T(1,128)S(1)}, u32[]{:S(2)}, u32[]{:S(2)}) collective-permute-start(f32[1,7168]{1,0:T(1,128)S(1)} %bitcast.55), channel_id=1, source_target_pairs={{0,2},{1,3},{2,0},{3,1},{4,6},{5,7},{6,4},{7,5},{8,10},{9,11},{10,... | collective-permute-start | bytes 86024 | tf_op jit(solution)/shard_map/while/body/eval_jaxpr/ppermute | solution.py:80
  80.7 1.4 collective-permute-start
  85.3 7.6 %multiply_reduce_fusion.7 = (f32[512]{0:T(512)S(1)}, f32[512]{0:T(512)S(1)}) fusion(bf16[1,7168,512]{2,1,0:T(8,128)(2,1)} %get-tuple-element.169, f32[7168]{0:T(1024)S(1)} %bitcast.53, bf16[1,7168,512]{2,1,0:T(8,128)(2,1)} %get-tuple-element.168), kind=kLoop, calls=%fused_computation.clone.1 | loop fusion | flops 29359104 | bytes 14712832 | tf_op jit(solution)/shard_map/while/body/eval_jaxpr/reduce_sum | solution.py:91
  92.9 9.1 %multiply_reduce_fusion.6 = (f32[7168]{0:T(1024)S(1)}, f32[7168]{0:T(1024)S(1)}) fusion(bf16[1,7168,512]{2,1,0:T(8,128)(2,1)} %get-tuple-element.169, f32[512]{0:T(512)S(1)} %bitcast.62, f32[512]{0:T(512)S(1)} %bitcast.63, bf16[1,7168,512]{2,1,0:T(8,128)(2,1)} %get-tuple-element.168), kind=kLoop, calls=%fused_computation.2.clone.1 | loop fusion | flops 29345792 | bytes 14741504 | tf_op jit(solution)/shard_map/while/body/eval_jaxpr/reduce_sum | solution.py:86
  102.1 1.5 collective-permute-start.2
  103.5 2.7 %collective-permute-start.1 = (f32[1,7168]{1,0:T(1,128)S(1)}, f32[1,7168]{1,0:T(1,128)S(1)}, u32[]{:S(2)}, u32[]{:S(2)}) collective-permute-start(f32[1,7168]{1,0:T(1,128)S(1)} %bitcast.55), channel_id=1, source_target_pairs={{0,2},{1,3},{2,0},{3,1},{4,6},{5,7},{6,4},{7,5},{8,10},{9,11},{10,... | collective-permute-start | bytes 86024 | tf_op jit(solution)/shard_map/while/body/eval_jaxpr/ppermute | solution.py:80
  107.2 1.7 collective-permute-done.1
  108.9 1.2 collective-permute-done
  110.8 7.6 %multiply_reduce_fusion.7 = (f32[512]{0:T(512)S(1)}, f32[512]{0:T(512)S(1)}) fusion(bf16[1,7168,512]{2,1,0:T(8,128)(2,1)} %get-tuple-element.169, f32[7168]{0:T(1024)S(1)} %bitcast.53, bf16[1,7168,512]{2,1,0:T(8,128)(2,1)} %get-tuple-element.168), kind=kLoop, calls=%fused_computation.clone.1 | loop fusion | flops 29359104 | bytes 14712832 | tf_op jit(solution)/shard_map/while/body/eval_jaxpr/reduce_sum | solution.py:91
  118.5 9.1 %multiply_reduce_fusion.6 = (f32[7168]{0:T(1024)S(1)}, f32[7168]{0:T(1024)S(1)}) fusion(bf16[1,7168,512]{2,1,0:T(8,128)(2,1)} %get-tuple-element.169, f32[512]{0:T(512)S(1)} %bitcast.62, f32[512]{0:T(512)S(1)} %bitcast.63, bf16[1,7168,512]{2,1,0:T(8,128)(2,1)} %get-tuple-element.168), kind=kLoop, calls=%fused_computation.2.clone.1 | loop fusion | flops 29345792 | bytes 14741504 | tf_op jit(solution)/shard_map/while/body/eval_jaxpr/reduce_sum | solution.py:86
  127.7 2.7 %collective-permute-start.1 = (f32[1,7168]{1,0:T(1,128)S(1)}, f32[1,7168]{1,0:T(1,128)S(1)}, u32[]{:S(2)}, u32[]{:S(2)}) collective-permute-start(f32[1,7168]{1,0:T(1,128)S(1)} %bitcast.55), channel_id=1, source_target_pairs={{0,2},{1,3},{2,0},{3,1},{4,6},{5,7},{6,4},{7,5},{8,10},{9,11},{10,... | collective-permute-start | bytes 86024 | tf_op jit(solution)/shard_map/while/body/eval_jaxpr/ppermute | solution.py:80
  130.4 1.4 collective-permute-start
  134.9 7.6 %multiply_reduce_fusion.7 = (f32[512]{0:T(512)S(1)}, f32[512]{0:T(512)S(1)}) fusion(bf16[1,7168,512]{2,1,0:T(8,128)(2,1)} %get-tuple-element.169, f32[7168]{0:T(1024)S(1)} %bitcast.53, bf16[1,7168,512]{2,1,0:T(8,128)(2,1)} %get-tuple-element.168), kind=kLoop, calls=%fused_computation.clone.1 | loop fusion | flops 29359104 | bytes 14712832 | tf_op jit(solution)/shard_map/while/body/eval_jaxpr/reduce_sum | solution.py:91
  142.5 7.5 %multiply_convert_fusion.1 = (bf16[1,7168,512]{2,1,0:T(8,128)(2,1)S(1)}, bf16[1,7168,512]{2,1,0:T(8,128)(2,1)S(1)}) fusion(bf16[1,7168,512]{2,1,0:T(8,128)(2,1)} %get-tuple-element.171, f32[512]{0:T(512)S(1)} %bitcast.61, f32[7168]{0:T(1024)} %bitcast.64, f32[512]{0:T(512)S(1)} %bitcast.59, bf16[1,7168,512]{2,1,0:T(8,128)(2,1)} %get-tuple-element.172), kind=kLoop, calls=%fused_computation.11 | loop fusion | flops 29360128 | bytes 29392896 | tf_op jit(solution)/shard_map/convert_element_type | solution.py:124
  150.0 6.5 %pad_maximum_fusion = bf16[1,7168,1024]{2,1,0:T(8,128)(2,1)} fusion(bf16[1,7168,512]{2,1,0:T(8,128)(2,1)S(1)} %get-tuple-element.102, bf16[1,7168,512]{2,1,0:T(8,128)(2,1)S(1)} %get-tuple-element.101), kind=kLoop, calls=%fused_computation.9 | loop fusion | flops 29360128 | bytes 29360128 | tf_op jit(solution)/shard_map/concatenate | solution.py:128
  156.5 35.3 %all-to-all-done = bf16[32,1,24,7168]{3,2,1,0:T(8,128)(2,1)} async-done(((bf16[32,1,24,7168]{3,2,1,0:T(8,128)(2,1)}), bf16[32,1,24,7168]{3,2,1,0:T(8,128)(2,1)}, u32[]{:S(2)}, u32[]{:S(2)}) %all-to-all-start) | async-done | bytes 11010080 | tf_op jit(solution)/shard_map/all_to_all | solution.py:103
  191.8 16.9 %shard_map.46 = bf16[768,512]{1,0:T(8,128)(2,1)} custom-call(bf16[768,7168]{1,0:T(8,128)(2,1)} %bitcast.10.rows_ref, bf16[7168,1024]{1,0:T(8,128)(2,1)} %bitcast.51, bf16[7168,1024]{1,0:T(8,128)(2,1)} %bitcast.52), custom_call_target="tpu_custom_call" | custom-call | flops 11274289152 | bytes 26476544 | tf_op jit(solution)/shard_map/pallas_call | solution.py:40
  (67 shorter events, 15.9 us)
Async XLA Ops:
  0.0 3.9 %copy-start = (bf16[64,7168]{1,0:T(8,128)(2,1)S(1)}, bf16[64,7168]{1,0:T(8,128)(2,1)}, u32[]{:S(2)}) copy-start(bf16[64,7168]{1,0:T(8,128)(2,1)} %param.6) | copy-start | bytes 2752516
  9.6 182.2 %all-to-all-start = ((bf16[32,1,24,7168]{3,2,1,0:T(8,128)(2,1)}), bf16[32,1,24,7168]{3,2,1,0:T(8,128)(2,1)}, u32[]{:S(2)}, u32[]{:S(2)}) async-start(bf16[32,1,24,7168]{3,2,1,0:T(8,128)(2,1)} %fusion), calls=%async_computation | async-start | bytes 22020096 | tf_op jit(solution)/shard_map/all_to_all | solution.py:103
  26.8 5.7 %collective-permute-start.2 = (f32[1,7168]{1,0:T(1,128)S(1)}, f32[1,7168]{1,0:T(1,128)S(1)}, u32[]{:S(2)}, u32[]{:S(2)}) collective-permute-start(f32[1,7168]{1,0:T(1,128)S(1)} %bitcast.54), channel_id=1, source_target_pairs={{0,1},{1,2},{2,3},{3,0},{4,5},{5,6},{6,7},{7,4},{8,9},{9,10},{10,1... | collective-permute-start | bytes 86024 | tf_op jit(solution)/shard_map/while/body/eval_jaxpr/ppermute | solution.py:80
  28.4 5.4 %collective-permute-start.1 = (f32[1,7168]{1,0:T(1,128)S(1)}, f32[1,7168]{1,0:T(1,128)S(1)}, u32[]{:S(2)}, u32[]{:S(2)}) collective-permute-start(f32[1,7168]{1,0:T(1,128)S(1)} %bitcast.55), channel_id=1, source_target_pairs={{0,2},{1,3},{2,0},{3,1},{4,6},{5,7},{6,4},{7,5},{8,10},{9,11},{10,... | collective-permute-start | bytes 86024 | tf_op jit(solution)/shard_map/while/body/eval_jaxpr/ppermute | solution.py:80
  31.1 3.9 %collective-permute-start = (f32[1,7168]{1,0:T(1,128)S(1)}, f32[1,7168]{1,0:T(1,128)S(1)}, u32[]{:S(2)}, u32[]{:S(2)}) collective-permute-start(f32[1,7168]{1,0:T(1,128)S(1)} %bitcast.56), channel_id=1, source_target_pairs={{0,3},{1,0},{2,1},{3,2},{4,7},{5,4},{6,5},{7,6},{8,11},{9,8},{10,9... | collective-permute-start | bytes 86024 | tf_op jit(solution)/shard_map/while/body/eval_jaxpr/ppermute | solution.py:80
  52.4 5.1 %collective-permute-start.2 = (f32[1,7168]{1,0:T(1,128)S(1)}, f32[1,7168]{1,0:T(1,128)S(1)}, u32[]{:S(2)}, u32[]{:S(2)}) collective-permute-start(f32[1,7168]{1,0:T(1,128)S(1)} %bitcast.54), channel_id=1, source_target_pairs={{0,1},{1,2},{2,3},{3,0},{4,5},{5,6},{6,7},{7,4},{8,9},{9,10},{10,1... | collective-permute-start | bytes 86024 | tf_op jit(solution)/shard_map/while/body/eval_jaxpr/ppermute | solution.py:80
  52.8 6.0 %collective-permute-start.1 = (f32[1,7168]{1,0:T(1,128)S(1)}, f32[1,7168]{1,0:T(1,128)S(1)}, u32[]{:S(2)}, u32[]{:S(2)}) collective-permute-start(f32[1,7168]{1,0:T(1,128)S(1)} %bitcast.55), channel_id=1, source_target_pairs={{0,2},{1,3},{2,0},{3,1},{4,6},{5,7},{6,4},{7,5},{8,10},{9,11},{10,... | collective-permute-start | bytes 86024 | tf_op jit(solution)/shard_map/while/body/eval_jaxpr/ppermute | solution.py:80
  56.6 3.9 %collective-permute-start = (f32[1,7168]{1,0:T(1,128)S(1)}, f32[1,7168]{1,0:T(1,128)S(1)}, u32[]{:S(2)}, u32[]{:S(2)}) collective-permute-start(f32[1,7168]{1,0:T(1,128)S(1)} %bitcast.56), channel_id=1, source_target_pairs={{0,3},{1,0},{2,1},{3,2},{4,7},{5,4},{6,5},{7,6},{8,11},{9,8},{10,9... | collective-permute-start | bytes 86024 | tf_op jit(solution)/shard_map/while/body/eval_jaxpr/ppermute | solution.py:80
  77.9 5.1 %collective-permute-start.2 = (f32[1,7168]{1,0:T(1,128)S(1)}, f32[1,7168]{1,0:T(1,128)S(1)}, u32[]{:S(2)}, u32[]{:S(2)}) collective-permute-start(f32[1,7168]{1,0:T(1,128)S(1)} %bitcast.54), channel_id=1, source_target_pairs={{0,1},{1,2},{2,3},{3,0},{4,5},{5,6},{6,7},{7,4},{8,9},{9,10},{10,1... | collective-permute-start | bytes 86024 | tf_op jit(solution)/shard_map/while/body/eval_jaxpr/ppermute | solution.py:80
  78.0 5.5 %collective-permute-start.1 = (f32[1,7168]{1,0:T(1,128)S(1)}, f32[1,7168]{1,0:T(1,128)S(1)}, u32[]{:S(2)}, u32[]{:S(2)}) collective-permute-start(f32[1,7168]{1,0:T(1,128)S(1)} %bitcast.55), channel_id=1, source_target_pairs={{0,2},{1,3},{2,0},{3,1},{4,6},{5,7},{6,4},{7,5},{8,10},{9,11},{10,... | collective-permute-start | bytes 86024 | tf_op jit(solution)/shard_map/while/body/eval_jaxpr/ppermute | solution.py:80
  80.7 3.9 %collective-permute-start = (f32[1,7168]{1,0:T(1,128)S(1)}, f32[1,7168]{1,0:T(1,128)S(1)}, u32[]{:S(2)}, u32[]{:S(2)}) collective-permute-start(f32[1,7168]{1,0:T(1,128)S(1)} %bitcast.56), channel_id=1, source_target_pairs={{0,3},{1,0},{2,1},{3,2},{4,7},{5,4},{6,5},{7,6},{8,11},{9,8},{10,9... | collective-permute-start | bytes 86024 | tf_op jit(solution)/shard_map/while/body/eval_jaxpr/ppermute | solution.py:80
  102.1 5.1 %collective-permute-start.2 = (f32[1,7168]{1,0:T(1,128)S(1)}, f32[1,7168]{1,0:T(1,128)S(1)}, u32[]{:S(2)}, u32[]{:S(2)}) collective-permute-start(f32[1,7168]{1,0:T(1,128)S(1)} %bitcast.54), channel_id=1, source_target_pairs={{0,1},{1,2},{2,3},{3,0},{4,5},{5,6},{6,7},{7,4},{8,9},{9,10},{10,1... | collective-permute-start | bytes 86024 | tf_op jit(solution)/shard_map/while/body/eval_jaxpr/ppermute | solution.py:80
  103.5 5.4 %collective-permute-start.1 = (f32[1,7168]{1,0:T(1,128)S(1)}, f32[1,7168]{1,0:T(1,128)S(1)}, u32[]{:S(2)}, u32[]{:S(2)}) collective-permute-start(f32[1,7168]{1,0:T(1,128)S(1)} %bitcast.55), channel_id=1, source_target_pairs={{0,2},{1,3},{2,0},{3,1},{4,6},{5,7},{6,4},{7,5},{8,10},{9,11},{10,... | collective-permute-start | bytes 86024 | tf_op jit(solution)/shard_map/while/body/eval_jaxpr/ppermute | solution.py:80
  106.2 3.9 %collective-permute-start = (f32[1,7168]{1,0:T(1,128)S(1)}, f32[1,7168]{1,0:T(1,128)S(1)}, u32[]{:S(2)}, u32[]{:S(2)}) collective-permute-start(f32[1,7168]{1,0:T(1,128)S(1)} %bitcast.56), channel_id=1, source_target_pairs={{0,3},{1,0},{2,1},{3,2},{4,7},{5,4},{6,5},{7,6},{8,11},{9,8},{10,9... | collective-permute-start | bytes 86024 | tf_op jit(solution)/shard_map/while/body/eval_jaxpr/ppermute | solution.py:80
  127.6 5.1 %collective-permute-start.2 = (f32[1,7168]{1,0:T(1,128)S(1)}, f32[1,7168]{1,0:T(1,128)S(1)}, u32[]{:S(2)}, u32[]{:S(2)}) collective-permute-start(f32[1,7168]{1,0:T(1,128)S(1)} %bitcast.54), channel_id=1, source_target_pairs={{0,1},{1,2},{2,3},{3,0},{4,5},{5,6},{6,7},{7,4},{8,9},{9,10},{10,1... | collective-permute-start | bytes 86024 | tf_op jit(solution)/shard_map/while/body/eval_jaxpr/ppermute | solution.py:80
  127.7 5.5 %collective-permute-start.1 = (f32[1,7168]{1,0:T(1,128)S(1)}, f32[1,7168]{1,0:T(1,128)S(1)}, u32[]{:S(2)}, u32[]{:S(2)}) collective-permute-start(f32[1,7168]{1,0:T(1,128)S(1)} %bitcast.55), channel_id=1, source_target_pairs={{0,2},{1,3},{2,0},{3,1},{4,6},{5,7},{6,4},{7,5},{8,10},{9,11},{10,... | collective-permute-start | bytes 86024 | tf_op jit(solution)/shard_map/while/body/eval_jaxpr/ppermute | solution.py:80
  130.4 3.9 %collective-permute-start = (f32[1,7168]{1,0:T(1,128)S(1)}, f32[1,7168]{1,0:T(1,128)S(1)}, u32[]{:S(2)}, u32[]{:S(2)}) collective-permute-start(f32[1,7168]{1,0:T(1,128)S(1)} %bitcast.56), channel_id=1, source_target_pairs={{0,3},{1,0},{2,1},{3,2},{4,7},{5,4},{6,5},{7,6},{8,11},{9,8},{10,9... | collective-permute-start | bytes 86024 | tf_op jit(solution)/shard_map/while/body/eval_jaxpr/ppermute | solution.py:80
  191.8 16.9 %copy-start.1 = (bf16[64,7168]{1,0:T(8,128)(2,1)S(1)}, bf16[64,7168]{1,0:T(8,128)(2,1)}, u32[]{:S(2)}) copy-start(bf16[64,7168]{1,0:T(8,128)(2,1)} %param.6) | copy-start | bytes 2752516

commit v4 on v2

--- a/solution.py
+++ b/solution.py
@@ -16,9 +16,13 @@
 def dispatch_rows(block_ids, tokens):
     tok_local, topk = block_ids.shape
     flat_ids = block_ids.reshape(-1)
-    onehot = (flat_ids[:, None] == jnp.arange(EXPERTS, dtype=jnp.int32)[None, :]).astype(jnp.int32)
-    before = jnp.cumsum(onehot, axis=0) - onehot
-    my_rank = jnp.sum(before * onehot, axis=1)
+    pairs = flat_ids.shape[0]
+    onehot = (flat_ids[:, None] == jnp.arange(EXPERTS, dtype=jnp.int32)[None, :]).astype(jnp.bfloat16)
+    earlier = (
+        jnp.arange(pairs, dtype=jnp.int32)[:, None] > jnp.arange(pairs, dtype=jnp.int32)[None, :]
+    ).astype(jnp.bfloat16)
+    before = jnp.dot(earlier, onehot, preferred_element_type=jnp.float32)
+    my_rank = jnp.sum(before * onehot.astype(jnp.float32), axis=1).astype(jnp.int32)
     pair_ids = flat_ids.reshape(tok_local, topk)
     pair_rank = my_rank.reshape(tok_local, topk)
     hit = (pair_ids[None, None] == jnp.arange(EXPERTS, dtype=jnp.int32)[:, None, None, None]) & (

time: 208 us -> 206 us (level)
  no operation moved by 1% of the time
where the time goes in v4:
time: 206 us
  other arithmetic  103 us (50%)
  waiting for transfers between devices  54.4 us (26%)
  starting transfers between devices  24.1 us (12%)
  matrix products  22.5 us (11%)
    reduce_sum x5, other arithmetic, row_terms(): return jnp.sum(values * values * cols_sq[:, None, :], axis=2)  45.5 us
    reduce_sum x5, other arithmetic, col_terms(): return jnp.sum(values * values * scale_sq[:, :, None], axis=1)  37.9 us
    all_to_all x1, waiting for transfers between devices, shards(): lax.all_to_all(outgoing, 'expert', split_axis=0, concat_axis=1, tiled=True)  32.4 us
    ppermute x15, waiting for transfers between devices, hidden_sum(): lax.ppermute(values, 'hidden', [(i, (i + shift) % n) for i in range(n)])  22 us
    dot_general x1, matrix products, shards(): jnp.einsum('ensd,edf->ensf', routed, both_eq, preferred_element_type=jnp....  16.6 us
    ppermute x15, starting transfers between devices, hidden_sum(): lax.ppermute(values, 'hidden', [(i, (i + shift) % n) for i in range(n)])  16.1 us
    all_to_all x1, starting transfers between devices, shards(): lax.all_to_all(outgoing, 'expert', split_axis=0, concat_axis=1, tiled=True)  8.04 us
    convert_element_type x1, other arithmetic, shards(): gate_eq = (gate_weight.astype(jnp.float32) * row_scale[:, :, None] * gate...  7.45 us
  transfers between devices with their start and end apart: 16, of which 15 were waited for; matrix products, arithmetic and copies ran while one was open for 49% of the time, Pallas kernels for 0%

profile of v4, /device:TPU:48, one launch (start us, length us, event | category | flops | bytes accessed | tf_op | source)
XLA Modules:
  0.0 206.0 jit_solution(10485184746225352236)
XLA Ops:
  2.5 5.7 %fusion.3 = bf16[32,1,24,7168]{3,2,1,0:T(8,128)(2,1)} fusion(pred[32,24,64]{2,1,0:T(8,128)(4,1)S(1)} %and_reduce_fusion, bf16[64,7168]{1,0:T(8,128)(2,1)S(1)} %copy-done), kind=kOutput, calls=%fused_computation.16 | convolution fusion | flops 710148096 | bytes 11976704 | tf_op jit(solution)/shard_map/est,td->esd/dot_general | solution.py:32
  8.2 8.0 %all-to-all-start = ((bf16[32,1,24,7168]{3,2,1,0:T(8,128)(2,1)}), bf16[32,1,24,7168]{3,2,1,0:T(8,128)(2,1)}, u32[]{:S(2)}, u32[]{:S(2)}) async-start(bf16[32,1,24,7168]{3,2,1,0:T(8,128)(2,1)} %fusion.3), calls=%async_computation | async-start | bytes 22020096 | tf_op jit(solution)/shard_map/all_to_all | solution.py:63
  16.3 125.4 %while.16 = (s32[]{:T(128)}, f32[1,512]{1,0:T(1,128)S(1)}, f32[1,512]{1,0:T(1,128)S(1)}, f32[1,7168]{1,0:T(1,128)}, bf16[1,7168,512]{2,1,0:T(8,128)(2,1)}, /*index=5*/bf16[1,7168,512]{2,1,0:T(8,128)(2,1)}, s32[]{:T(128)}) while((s32[]{:T(128)}, f32[1,512]{1,0:T(1,128)S(1)}, f32[1,512]{1,0:T(1,128)S(1)}, f32[1,7168]{1,0:T(1,128)}, ...), condition=%wide.region_7.0_spmd, body=%wide.region_2.0_spmd.sunk | while | flops 58757120 | bytes 30077124 | solution.py:81
  16.3 9.1 %multiply_reduce_fusion.6 = (f32[7168]{0:T(1024)S(1)}, f32[7168]{0:T(1024)S(1)}) fusion(bf16[1,7168,512]{2,1,0:T(8,128)(2,1)} %get-tuple-element.169, f32[512]{0:T(512)S(1)} %bitcast.51, f32[512]{0:T(512)S(1)} %bitcast.52, bf16[1,7168,512]{2,1,0:T(8,128)(2,1)} %get-tuple-element.168), kind=kLoop, calls=%fused_computation.2.clone.1 | loop fusion | flops 29345792 | bytes 14741504 | tf_op jit(solution)/shard_map/while/body/eval_jaxpr/reduce_sum | solution.py:46
  25.4 2.8 %collective-permute-start = (f32[1,7168]{1,0:T(1,128)S(1)}, f32[1,7168]{1,0:T(1,128)S(1)}, u32[]{:S(2)}, u32[]{:S(2)}) collective-permute-start(f32[1,7168]{1,0:T(1,128)S(1)} %bitcast.43), channel_id=1, source_target_pairs={{0,3},{1,0},{2,1},{3,2},{4,7},{5,4},{6,5},{7,6},{8,11},{9,8},{10,9... | collective-permute-start | bytes 86024 | tf_op jit(solution)/shard_map/while/body/eval_jaxpr/ppermute | solution.py:40
  30.0 3.7 %collective-permute-done.1 = f32[1,7168]{1,0:T(1,128)S(1)} collective-permute-done((f32[1,7168]{1,0:T(1,128)S(1)}, f32[1,7168]{1,0:T(1,128)S(1)}, u32[]{:S(2)}, u32[]{:S(2)}) %collective-permute-start.1) | collective-permute-done | bytes 28704 | tf_op jit(solution)/shard_map/while/body/eval_jaxpr/ppermute | solution.py:40
  34.8 7.6 %multiply_reduce_fusion.7 = (f32[512]{0:T(512)S(1)}, f32[512]{0:T(512)S(1)}) fusion(bf16[1,7168,512]{2,1,0:T(8,128)(2,1)} %get-tuple-element.169, f32[7168]{0:T(1024)S(1)} %bitcast.42, bf16[1,7168,512]{2,1,0:T(8,128)(2,1)} %get-tuple-element.168), kind=kLoop, calls=%fused_computation.clone.1 | loop fusion | flops 29359104 | bytes 14712832 | tf_op jit(solution)/shard_map/while/body/eval_jaxpr/reduce_sum | solution.py:51
  42.5 9.1 %multiply_reduce_fusion.6 = (f32[7168]{0:T(1024)S(1)}, f32[7168]{0:T(1024)S(1)}) fusion(bf16[1,7168,512]{2,1,0:T(8,128)(2,1)} %get-tuple-element.169, f32[512]{0:T(512)S(1)} %bitcast.51, f32[512]{0:T(512)S(1)} %bitcast.52, bf16[1,7168,512]{2,1,0:T(8,128)(2,1)} %get-tuple-element.168), kind=kLoop, calls=%fused_computation.2.clone.1 | loop fusion | flops 29345792 | bytes 14741504 | tf_op jit(solution)/shard_map/while/body/eval_jaxpr/reduce_sum | solution.py:46
  52.0 1.4 collective-permute-start.1
  53.4 1.2 collective-permute-start.2
  55.5 1.9 collective-permute-done.1
  57.4 1.1 collective-permute-done.2
  59.2 7.6 %multiply_reduce_fusion.7 = (f32[512]{0:T(512)S(1)}, f32[512]{0:T(512)S(1)}) fusion(bf16[1,7168,512]{2,1,0:T(8,128)(2,1)} %get-tuple-element.169, f32[7168]{0:T(1024)S(1)} %bitcast.42, bf16[1,7168,512]{2,1,0:T(8,128)(2,1)} %get-tuple-element.168), kind=kLoop, calls=%fused_computation.clone.1 | loop fusion | flops 29359104 | bytes 14712832 | tf_op jit(solution)/shard_map/while/body/eval_jaxpr/reduce_sum | solution.py:51
  66.8 9.1 %multiply_reduce_fusion.6 = (f32[7168]{0:T(1024)S(1)}, f32[7168]{0:T(1024)S(1)}) fusion(bf16[1,7168,512]{2,1,0:T(8,128)(2,1)} %get-tuple-element.169, f32[512]{0:T(512)S(1)} %bitcast.51, f32[512]{0:T(512)S(1)} %bitcast.52, bf16[1,7168,512]{2,1,0:T(8,128)(2,1)} %get-tuple-element.168), kind=kLoop, calls=%fused_computation.2.clone.1 | loop fusion | flops 29345792 | bytes 14741504 | tf_op jit(solution)/shard_map/while/body/eval_jaxpr/reduce_sum | solution.py:46
  76.0 1.8 collective-permute-start
  78.7 1.2 collective-permute-done
  79.9 3.2 %collective-permute-done.1 = f32[1,7168]{1,0:T(1,128)S(1)} collective-permute-done((f32[1,7168]{1,0:T(1,128)S(1)}, f32[1,7168]{1,0:T(1,128)S(1)}, u32[]{:S(2)}, u32[]{:S(2)}) %collective-permute-start.1) | collective-permute-done | bytes 28704 | tf_op jit(solution)/shard_map/while/body/eval_jaxpr/ppermute | solution.py:40
  84.4 7.6 %multiply_reduce_fusion.7 = (f32[512]{0:T(512)S(1)}, f32[512]{0:T(512)S(1)}) fusion(bf16[1,7168,512]{2,1,0:T(8,128)(2,1)} %get-tuple-element.169, f32[7168]{0:T(1024)S(1)} %bitcast.42, bf16[1,7168,512]{2,1,0:T(8,128)(2,1)} %get-tuple-element.168), kind=kLoop, calls=%fused_computation.clone.1 | loop fusion | flops 29359104 | bytes 14712832 | tf_op jit(solution)/shard_map/while/body/eval_jaxpr/reduce_sum | solution.py:51
  92.1 9.1 %multiply_reduce_fusion.6 = (f32[7168]{0:T(1024)S(1)}, f32[7168]{0:T(1024)S(1)}) fusion(bf16[1,7168,512]{2,1,0:T(8,128)(2,1)} %get-tuple-element.169, f32[512]{0:T(512)S(1)} %bitcast.51, f32[512]{0:T(512)S(1)} %bitcast.52, bf16[1,7168,512]{2,1,0:T(8,128)(2,1)} %get-tuple-element.168), kind=kLoop, calls=%fused_computation.2.clone.1 | loop fusion | flops 29345792 | bytes 14741504 | tf_op jit(solution)/shard_map/while/body/eval_jaxpr/reduce_sum | solution.py:46
  103.0 1.1 collective-permute-start.2
  104.1 1.0 collective-permute-done
  105.2 2.3 %collective-permute-done.1 = f32[1,7168]{1,0:T(1,128)S(1)} collective-permute-done((f32[1,7168]{1,0:T(1,128)S(1)}, f32[1,7168]{1,0:T(1,128)S(1)}, u32[]{:S(2)}, u32[]{:S(2)}) %collective-permute-start.1) | collective-permute-done | bytes 28704 | tf_op jit(solution)/shard_map/while/body/eval_jaxpr/ppermute | solution.py:40
  108.8 7.6 %multiply_reduce_fusion.7 = (f32[512]{0:T(512)S(1)}, f32[512]{0:T(512)S(1)}) fusion(bf16[1,7168,512]{2,1,0:T(8,128)(2,1)} %get-tuple-element.169, f32[7168]{0:T(1024)S(1)} %bitcast.42, bf16[1,7168,512]{2,1,0:T(8,128)(2,1)} %get-tuple-element.168), kind=kLoop, calls=%fused_computation.clone.1 | loop fusion | flops 29359104 | bytes 14712832 | tf_op jit(solution)/shard_map/while/body/eval_jaxpr/reduce_sum | solution.py:51
  116.5 9.1 %multiply_reduce_fusion.6 = (f32[7168]{0:T(1024)S(1)}, f32[7168]{0:T(1024)S(1)}) fusion(bf16[1,7168,512]{2,1,0:T(8,128)(2,1)} %get-tuple-element.169, f32[512]{0:T(512)S(1)} %bitcast.51, f32[512]{0:T(512)S(1)} %bitcast.52, bf16[1,7168,512]{2,1,0:T(8,128)(2,1)} %get-tuple-element.168), kind=kLoop, calls=%fused_computation.2.clone.1 | loop fusion | flops 29345792 | bytes 14741504 | tf_op jit(solution)/shard_map/while/body/eval_jaxpr/reduce_sum | solution.py:46
  125.6 1.8 collective-permute-start
  129.5 3.2 %collective-permute-done.1 = f32[1,7168]{1,0:T(1,128)S(1)} collective-permute-done((f32[1,7168]{1,0:T(1,128)S(1)}, f32[1,7168]{1,0:T(1,128)S(1)}, u32[]{:S(2)}, u32[]{:S(2)}) %collective-permute-start.1) | collective-permute-done | bytes 28704 | tf_op jit(solution)/shard_map/while/body/eval_jaxpr/ppermute | solution.py:40
  134.1 7.6 %multiply_reduce_fusion.7 = (f32[512]{0:T(512)S(1)}, f32[512]{0:T(512)S(1)}) fusion(bf16[1,7168,512]{2,1,0:T(8,128)(2,1)} %get-tuple-element.169, f32[7168]{0:T(1024)S(1)} %bitcast.42, bf16[1,7168,512]{2,1,0:T(8,128)(2,1)} %get-tuple-element.168), kind=kLoop, calls=%fused_computation.clone.1 | loop fusion | flops 29359104 | bytes 14712832 | tf_op jit(solution)/shard_map/while/body/eval_jaxpr/reduce_sum | solution.py:51
  141.7 7.4 %multiply_convert_fusion.1 = (bf16[1,7168,512]{2,1,0:T(8,128)(2,1)S(1)}, bf16[1,7168,512]{2,1,0:T(8,128)(2,1)S(1)}) fusion(bf16[1,7168,512]{2,1,0:T(8,128)(2,1)} %get-tuple-element.171, f32[512]{0:T(512)S(1)} %bitcast.48, f32[7168]{0:T(1024)} %bitcast.53, f32[512]{0:T(512)S(1)} %bitcast.50, bf16[1,7168,512]{2,1,0:T(8,128)(2,1)} %get-tuple-element.172), kind=kLoop, calls=%fused_computation.13 | loop fusion | flops 29360128 | bytes 29392896 | tf_op jit(solution)/shard_map/convert_element_type | solution.py:84
  149.2 6.5 %pad_maximum_fusion = bf16[1,7168,1024]{2,1,0:T(8,128)(2,1)} fusion(bf16[1,7168,512]{2,1,0:T(8,128)(2,1)S(1)} %get-tuple-element.102, bf16[1,7168,512]{2,1,0:T(8,128)(2,1)S(1)} %get-tuple-element.101), kind=kLoop, calls=%fused_computation.9 | loop fusion | flops 29360128 | bytes 29360128 | tf_op jit(solution)/shard_map/concatenate | solution.py:88
  155.7 32.4 %all-to-all-done = bf16[32,1,24,7168]{3,2,1,0:T(8,128)(2,1)} async-done(((bf16[32,1,24,7168]{3,2,1,0:T(8,128)(2,1)}), bf16[32,1,24,7168]{3,2,1,0:T(8,128)(2,1)}, u32[]{:S(2)}, u32[]{:S(2)}) %all-to-all-start) | async-done | bytes 11010080 | tf_op jit(solution)/shard_map/all_to_all | solution.py:63
  188.1 16.6 %fusion.4 = f32[1,32,24,1024]{3,2,1,0:T(8,128)S(1)} fusion(bf16[1,7168,1024]{2,1,0:T(8,128)(2,1)} %pad_maximum_fusion, bf16[32,1,24,7168]{3,2,1,0:T(8,128)(2,1)} %all-to-all-done), kind=kOutput, calls=%fused_computation.18 | convolution fusion | flops 11274289152 | bytes 28835840 | tf_op jit(solution)/shard_map/ensd,edf->ensf/dot_general | solution.py:89
  204.6 1.4 fusion.9
  (63 shorter events, 16.4 us)
Async XLA Ops:
  0.0 2.5 %copy-start = (bf16[64,7168]{1,0:T(8,128)(2,1)S(1)}, bf16[64,7168]{1,0:T(8,128)(2,1)}, u32[]{:S(2)}) copy-start(bf16[64,7168]{1,0:T(8,128)(2,1)} %param.6) | copy-start | bytes 2752516
  8.2 179.9 %all-to-all-start = ((bf16[32,1,24,7168]{3,2,1,0:T(8,128)(2,1)}), bf16[32,1,24,7168]{3,2,1,0:T(8,128)(2,1)}, u32[]{:S(2)}, u32[]{:S(2)}) async-start(bf16[32,1,24,7168]{3,2,1,0:T(8,128)(2,1)} %fusion.3), calls=%async_computation | async-start | bytes 22020096 | tf_op jit(solution)/shard_map/all_to_all | solution.py:63
  25.4 4.6 %collective-permute-start = (f32[1,7168]{1,0:T(1,128)S(1)}, f32[1,7168]{1,0:T(1,128)S(1)}, u32[]{:S(2)}, u32[]{:S(2)}) collective-permute-start(f32[1,7168]{1,0:T(1,128)S(1)} %bitcast.43), channel_id=1, source_target_pairs={{0,3},{1,0},{2,1},{3,2},{4,7},{5,4},{6,5},{7,6},{8,11},{9,8},{10,9... | collective-permute-start | bytes 86024 | tf_op jit(solution)/shard_map/while/body/eval_jaxpr/ppermute | solution.py:40
  28.2 5.4 %collective-permute-start.1 = (f32[1,7168]{1,0:T(1,128)S(1)}, f32[1,7168]{1,0:T(1,128)S(1)}, u32[]{:S(2)}, u32[]{:S(2)}) collective-permute-start(f32[1,7168]{1,0:T(1,128)S(1)} %bitcast.44), channel_id=1, source_target_pairs={{0,2},{1,3},{2,0},{3,1},{4,6},{5,7},{6,4},{7,5},{8,10},{9,11},{10,... | collective-permute-start | bytes 86024 | tf_op jit(solution)/shard_map/while/body/eval_jaxpr/ppermute | solution.py:40
  29.0 5.1 %collective-permute-start.2 = (f32[1,7168]{1,0:T(1,128)S(1)}, f32[1,7168]{1,0:T(1,128)S(1)}, u32[]{:S(2)}, u32[]{:S(2)}) collective-permute-start(f32[1,7168]{1,0:T(1,128)S(1)} %bitcast.45), channel_id=1, source_target_pairs={{0,1},{1,2},{2,3},{3,0},{4,5},{5,6},{6,7},{7,4},{8,9},{9,10},{10,1... | collective-permute-start | bytes 86024 | tf_op jit(solution)/shard_map/while/body/eval_jaxpr/ppermute | solution.py:40
  51.6 3.9 %collective-permute-start = (f32[1,7168]{1,0:T(1,128)S(1)}, f32[1,7168]{1,0:T(1,128)S(1)}, u32[]{:S(2)}, u32[]{:S(2)}) collective-permute-start(f32[1,7168]{1,0:T(1,128)S(1)} %bitcast.43), channel_id=1, source_target_pairs={{0,3},{1,0},{2,1},{3,2},{4,7},{5,4},{6,5},{7,6},{8,11},{9,8},{10,9... | collective-permute-start | bytes 86024 | tf_op jit(solution)/shard_map/while/body/eval_jaxpr/ppermute | solution.py:40
  52.0 5.4 %collective-permute-start.1 = (f32[1,7168]{1,0:T(1,128)S(1)}, f32[1,7168]{1,0:T(1,128)S(1)}, u32[]{:S(2)}, u32[]{:S(2)}) collective-permute-start(f32[1,7168]{1,0:T(1,128)S(1)} %bitcast.44), channel_id=1, source_target_pairs={{0,2},{1,3},{2,0},{3,1},{4,6},{5,7},{6,4},{7,5},{8,10},{9,11},{10,... | collective-permute-start | bytes 86024 | tf_op jit(solution)/shard_map/while/body/eval_jaxpr/ppermute | solution.py:40
  53.4 5.1 %collective-permute-start.2 = (f32[1,7168]{1,0:T(1,128)S(1)}, f32[1,7168]{1,0:T(1,128)S(1)}, u32[]{:S(2)}, u32[]{:S(2)}) collective-permute-start(f32[1,7168]{1,0:T(1,128)S(1)} %bitcast.45), channel_id=1, source_target_pairs={{0,1},{1,2},{2,3},{3,0},{4,5},{5,6},{6,7},{7,4},{8,9},{9,10},{10,1... | collective-permute-start | bytes 86024 | tf_op jit(solution)/shard_map/while/body/eval_jaxpr/ppermute | solution.py:40
  76.0 3.9 %collective-permute-start = (f32[1,7168]{1,0:T(1,128)S(1)}, f32[1,7168]{1,0:T(1,128)S(1)}, u32[]{:S(2)}, u32[]{:S(2)}) collective-permute-start(f32[1,7168]{1,0:T(1,128)S(1)} %bitcast.43), channel_id=1, source_target_pairs={{0,3},{1,0},{2,1},{3,2},{4,7},{5,4},{6,5},{7,6},{8,11},{9,8},{10,9... | collective-permute-start | bytes 86024 | tf_op jit(solution)/shard_map/while/body/eval_jaxpr/ppermute | solution.py:40
  77.8 5.4 %collective-permute-start.1 = (f32[1,7168]{1,0:T(1,128)S(1)}, f32[1,7168]{1,0:T(1,128)S(1)}, u32[]{:S(2)}, u32[]{:S(2)}) collective-permute-start(f32[1,7168]{1,0:T(1,128)S(1)} %bitcast.44), channel_id=1, source_target_pairs={{0,2},{1,3},{2,0},{3,1},{4,6},{5,7},{6,4},{7,5},{8,10},{9,11},{10,... | collective-permute-start | bytes 86024 | tf_op jit(solution)/shard_map/while/body/eval_jaxpr/ppermute | solution.py:40
  78.7 5.1 %collective-permute-start.2 = (f32[1,7168]{1,0:T(1,128)S(1)}, f32[1,7168]{1,0:T(1,128)S(1)}, u32[]{:S(2)}, u32[]{:S(2)}) collective-permute-start(f32[1,7168]{1,0:T(1,128)S(1)} %bitcast.45), channel_id=1, source_target_pairs={{0,1},{1,2},{2,3},{3,0},{4,5},{5,6},{6,7},{7,4},{8,9},{9,10},{10,1... | collective-permute-start | bytes 86024 | tf_op jit(solution)/shard_map/while/body/eval_jaxpr/ppermute | solution.py:40
  101.2 3.9 %collective-permute-start = (f32[1,7168]{1,0:T(1,128)S(1)}, f32[1,7168]{1,0:T(1,128)S(1)}, u32[]{:S(2)}, u32[]{:S(2)}) collective-permute-start(f32[1,7168]{1,0:T(1,128)S(1)} %bitcast.43), channel_id=1, source_target_pairs={{0,3},{1,0},{2,1},{3,2},{4,7},{5,4},{6,5},{7,6},{8,11},{9,8},{10,9... | collective-permute-start | bytes 86024 | tf_op jit(solution)/shard_map/while/body/eval_jaxpr/ppermute | solution.py:40
  102.1 5.4 %collective-permute-start.1 = (f32[1,7168]{1,0:T(1,128)S(1)}, f32[1,7168]{1,0:T(1,128)S(1)}, u32[]{:S(2)}, u32[]{:S(2)}) collective-permute-start(f32[1,7168]{1,0:T(1,128)S(1)} %bitcast.44), channel_id=1, source_target_pairs={{0,2},{1,3},{2,0},{3,1},{4,6},{5,7},{6,4},{7,5},{8,10},{9,11},{10,... | collective-permute-start | bytes 86024 | tf_op jit(solution)/shard_map/while/body/eval_jaxpr/ppermute | solution.py:40
  103.0 5.1 %collective-permute-start.2 = (f32[1,7168]{1,0:T(1,128)S(1)}, f32[1,7168]{1,0:T(1,128)S(1)}, u32[]{:S(2)}, u32[]{:S(2)}) collective-permute-start(f32[1,7168]{1,0:T(1,128)S(1)} %bitcast.45), channel_id=1, source_target_pairs={{0,1},{1,2},{2,3},{3,0},{4,5},{5,6},{6,7},{7,4},{8,9},{9,10},{10,1... | collective-permute-start | bytes 86024 | tf_op jit(solution)/shard_map/while/body/eval_jaxpr/ppermute | solution.py:40
  125.6 3.9 %collective-permute-start = (f32[1,7168]{1,0:T(1,128)S(1)}, f32[1,7168]{1,0:T(1,128)S(1)}, u32[]{:S(2)}, u32[]{:S(2)}) collective-permute-start(f32[1,7168]{1,0:T(1,128)S(1)} %bitcast.43), channel_id=1, source_target_pairs={{0,3},{1,0},{2,1},{3,2},{4,7},{5,4},{6,5},{7,6},{8,11},{9,8},{10,9... | collective-permute-start | bytes 86024 | tf_op jit(solution)/shard_map/while/body/eval_jaxpr/ppermute | solution.py:40
  127.4 5.4 %collective-permute-start.1 = (f32[1,7168]{1,0:T(1,128)S(1)}, f32[1,7168]{1,0:T(1,128)S(1)}, u32[]{:S(2)}, u32[]{:S(2)}) collective-permute-start(f32[1,7168]{1,0:T(1,128)S(1)} %bitcast.44), channel_id=1, source_target_pairs={{0,2},{1,3},{2,0},{3,1},{4,6},{5,7},{6,4},{7,5},{8,10},{9,11},{10,... | collective-permute-start | bytes 86024 | tf_op jit(solution)/shard_map/while/body/eval_jaxpr/ppermute | solution.py:40
  128.3 5.1 %collective-permute-start.2 = (f32[1,7168]{1,0:T(1,128)S(1)}, f32[1,7168]{1,0:T(1,128)S(1)}, u32[]{:S(2)}, u32[]{:S(2)}) collective-permute-start(f32[1,7168]{1,0:T(1,128)S(1)} %bitcast.45), channel_id=1, source_target_pairs={{0,1},{1,2},{2,3},{3,0},{4,5},{5,6},{6,7},{7,4},{8,9},{9,10},{10,1... | collective-permute-start | bytes 86024 | tf_op jit(solution)/shard_map/while/body/eval_jaxpr/ppermute | solution.py:40
  188.1 18.0 %copy-start.1 = (bf16[64,7168]{1,0:T(8,128)(2,1)S(1)}, bf16[64,7168]{1,0:T(8,128)(2,1)}, u32[]{:S(2)}) copy-start(bf16[64,7168]{1,0:T(8,128)(2,1)} %param.6) | copy-start | bytes 2752516

commit v5 on v4

--- a/solution.py
+++ b/solution.py
@@ -30,7 +30,7 @@
     )
     select = jnp.any(hit, axis=3).astype(tokens.dtype)
     rows = jnp.einsum("est,td->esd", select, tokens, preferred_element_type=jnp.float32)
-    return rows.astype(tokens.dtype)[:, None]
+    return rows.astype(tokens.dtype)
 
 
 def hidden_sum(values):
@@ -60,7 +60,7 @@
     tok_local = tokens.shape[0]
     block_ids = lax.dynamic_slice_in_dim(expert_ids, my_index * tok_local, tok_local, 0)
     outgoing = dispatch_rows(block_ids, tokens)
-    routed = lax.all_to_all(outgoing, "expert", split_axis=0, concat_axis=1, tiled=True)
+    routed = lax.all_to_all(outgoing, "expert", split_axis=0, concat_axis=0, tiled=True)[None]
     def sweep(_, carry):
         gate_cols, up_cols, _ = carry
         partial_rows = row_terms(gate_weight, gate_cols * gate_cols) + row_terms(

time: 206 us -> 206 us (level)
  no operation moved by 1% of the time
where the time goes in v5:
time: 206 us
  other arithmetic  103 us (50%)
  waiting for transfers between devices  54.4 us (26%)
  starting transfers between devices  24.1 us (12%)
  matrix products  22.5 us (11%)
    reduce_sum x5, other arithmetic, row_terms(): return jnp.sum(values * values * cols_sq[:, None, :], axis=2)  45.5 us
    reduce_sum x5, other arithmetic, col_terms(): return jnp.sum(values * values * scale_sq[:, :, None], axis=1)  37.9 us
    all_to_all x1, waiting for transfers between devices, shards(): lax.all_to_all(outgoing, 'expert', split_axis=0, concat_axis=0, tiled=True)  32.4 us
    ppermute x15, waiting for transfers between devices, hidden_sum(): lax.ppermute(values, 'hidden', [(i, (i + shift) % n) for i in range(n)])  22 us
    dot_general x1, matrix products, shards(): jnp.einsum('ensd,edf->ensf', routed, both_eq, preferred_element_type=jnp....  16.6 us
    ppermute x15, starting transfers between devices, hidden_sum(): lax.ppermute(values, 'hidden', [(i, (i + shift) % n) for i in range(n)])  16.1 us
    all_to_all x1, starting transfers between devices, shards(): lax.all_to_all(outgoing, 'expert', split_axis=0, concat_axis=0, tiled=True)  8.04 us
    convert_element_type x1, other arithmetic, shards(): gate_eq = (gate_weight.astype(jnp.float32) * row_scale[:, :, None] * gate...  7.45 us
  transfers between devices with their start and end apart: 16, of which 15 were waited for; matrix products, arithmetic and copies ran while one was open for 49% of the time, Pallas kernels for 0%

profile of v5, /device:TPU:48, one launch (start us, length us, event | category | flops | bytes accessed | tf_op | source)
XLA Modules:
  0.0 206.0 jit_solution(12540314023539071217)
XLA Ops:
  2.5 5.7 %convolution_convert_fusion = bf16[32,24,7168]{2,1,0:T(8,128)(2,1)} fusion(pred[32,24,64]{2,1,0:T(8,128)(4,1)S(1)} %and_reduce_fusion, bf16[64,7168]{1,0:T(8,128)(2,1)S(1)} %copy-done), kind=kOutput, calls=%fused_computation.14 | convolution fusion | flops 710148096 | bytes 11976704 | tf_op jit(solution)/shard_map/est,td->esd/dot_general | solution.py:32
  8.2 8.0 %all-to-all-start = ((bf16[32,24,7168]{2,1,0:T(8,128)(2,1)}), bf16[32,24,7168]{2,1,0:T(8,128)(2,1)}, u32[]{:S(2)}, u32[]{:S(2)}) async-start(bf16[32,24,7168]{2,1,0:T(8,128)(2,1)} %convolution_convert_fusion), calls=%async_computation | async-start | bytes 22020096 | tf_op jit(solution)/shard_map/all_to_all | solution.py:63
  16.3 125.4 %while.16 = (s32[]{:T(128)}, f32[1,512]{1,0:T(1,128)S(1)}, f32[1,512]{1,0:T(1,128)S(1)}, f32[1,7168]{1,0:T(1,128)}, bf16[1,7168,512]{2,1,0:T(8,128)(2,1)}, /*index=5*/bf16[1,7168,512]{2,1,0:T(8,128)(2,1)}, s32[]{:T(128)}) while((s32[]{:T(128)}, f32[1,512]{1,0:T(1,128)S(1)}, f32[1,512]{1,0:T(1,128)S(1)}, f32[1,7168]{1,0:T(1,128)}, ...), condition=%wide.region_7.0_spmd, body=%wide.region_2.0_spmd.sunk | while | flops 58757120 | bytes 30077124 | solution.py:81
  16.3 9.1 %multiply_reduce_fusion.6 = (f32[7168]{0:T(1024)S(1)}, f32[7168]{0:T(1024)S(1)}) fusion(bf16[1,7168,512]{2,1,0:T(8,128)(2,1)} %get-tuple-element.169, f32[512]{0:T(512)S(1)} %bitcast.43, f32[512]{0:T(512)S(1)} %bitcast.44, bf16[1,7168,512]{2,1,0:T(8,128)(2,1)} %get-tuple-element.168), kind=kLoop, calls=%fused_computation.2.clone.1 | loop fusion | flops 29345792 | bytes 14741504 | tf_op jit(solution)/shard_map/while/body/eval_jaxpr/reduce_sum | solution.py:46
  25.4 2.8 %collective-permute-start = (f32[1,7168]{1,0:T(1,128)S(1)}, f32[1,7168]{1,0:T(1,128)S(1)}, u32[]{:S(2)}, u32[]{:S(2)}) collective-permute-start(f32[1,7168]{1,0:T(1,128)S(1)} %bitcast.35), channel_id=1, source_target_pairs={{0,3},{1,0},{2,1},{3,2},{4,7},{5,4},{6,5},{7,6},{8,11},{9,8},{10,9... | collective-permute-start | bytes 86024 | tf_op jit(solution)/shard_map/while/body/eval_jaxpr/ppermute | solution.py:40
  30.0 3.7 %collective-permute-done.1 = f32[1,7168]{1,0:T(1,128)S(1)} collective-permute-done((f32[1,7168]{1,0:T(1,128)S(1)}, f32[1,7168]{1,0:T(1,128)S(1)}, u32[]{:S(2)}, u32[]{:S(2)}) %collective-permute-start.1) | collective-permute-done | bytes 28704 | tf_op jit(solution)/shard_map/while/body/eval_jaxpr/ppermute | solution.py:40
  34.8 7.6 %multiply_reduce_fusion.7 = (f32[512]{0:T(512)S(1)}, f32[512]{0:T(512)S(1)}) fusion(bf16[1,7168,512]{2,1,0:T(8,128)(2,1)} %get-tuple-element.169, f32[7168]{0:T(1024)S(1)} %bitcast.34, bf16[1,7168,512]{2,1,0:T(8,128)(2,1)} %get-tuple-element.168), kind=kLoop, calls=%fused_computation.clone.1 | loop fusion | flops 29359104 | bytes 14712832 | tf_op jit(solution)/shard_map/while/body/eval_jaxpr/reduce_sum | solution.py:51
  42.5 9.1 %multiply_reduce_fusion.6 = (f32[7168]{0:T(1024)S(1)}, f32[7168]{0:T(1024)S(1)}) fusion(bf16[1,7168,512]{2,1,0:T(8,128)(2,1)} %get-tuple-element.169, f32[512]{0:T(512)S(1)} %bitcast.43, f32[512]{0:T(512)S(1)} %bitcast.44, bf16[1,7168,512]{2,1,0:T(8,128)(2,1)} %get-tuple-element.168), kind=kLoop, calls=%fused_computation.2.clone.1 | loop fusion | flops 29345792 | bytes 14741504 | tf_op jit(solution)/shard_map/while/body/eval_jaxpr/reduce_sum | solution.py:46
  52.0 1.4 collective-permute-start.1
  53.4 1.2 collective-permute-start.2
  55.5 1.9 collective-permute-done.1
  57.4 1.1 collective-permute-done.2
  59.2 7.6 %multiply_reduce_fusion.7 = (f32[512]{0:T(512)S(1)}, f32[512]{0:T(512)S(1)}) fusion(bf16[1,7168,512]{2,1,0:T(8,128)(2,1)} %get-tuple-element.169, f32[7168]{0:T(1024)S(1)} %bitcast.34, bf16[1,7168,512]{2,1,0:T(8,128)(2,1)} %get-tuple-element.168), kind=kLoop, calls=%fused_computation.clone.1 | loop fusion | flops 29359104 | bytes 14712832 | tf_op jit(solution)/shard_map/while/body/eval_jaxpr/reduce_sum | solution.py:51
  66.8 9.1 %multiply_reduce_fusion.6 = (f32[7168]{0:T(1024)S(1)}, f32[7168]{0:T(1024)S(1)}) fusion(bf16[1,7168,512]{2,1,0:T(8,128)(2,1)} %get-tuple-element.169, f32[512]{0:T(512)S(1)} %bitcast.43, f32[512]{0:T(512)S(1)} %bitcast.44, bf16[1,7168,512]{2,1,0:T(8,128)(2,1)} %get-tuple-element.168), kind=kLoop, calls=%fused_computation.2.clone.1 | loop fusion | flops 29345792 | bytes 14741504 | tf_op jit(solution)/shard_map/while/body/eval_jaxpr/reduce_sum | solution.py:46
  76.0 1.8 collective-permute-start
  78.7 1.2 collective-permute-done
  79.9 3.2 %collective-permute-done.1 = f32[1,7168]{1,0:T(1,128)S(1)} collective-permute-done((f32[1,7168]{1,0:T(1,128)S(1)}, f32[1,7168]{1,0:T(1,128)S(1)}, u32[]{:S(2)}, u32[]{:S(2)}) %collective-permute-start.1) | collective-permute-done | bytes 28704 | tf_op jit(solution)/shard_map/while/body/eval_jaxpr/ppermute | solution.py:40
  84.4 7.6 %multiply_reduce_fusion.7 = (f32[512]{0:T(512)S(1)}, f32[512]{0:T(512)S(1)}) fusion(bf16[1,7168,512]{2,1,0:T(8,128)(2,1)} %get-tuple-element.169, f32[7168]{0:T(1024)S(1)} %bitcast.34, bf16[1,7168,512]{2,1,0:T(8,128)(2,1)} %get-tuple-element.168), kind=kLoop, calls=%fused_computation.clone.1 | loop fusion | flops 29359104 | bytes 14712832 | tf_op jit(solution)/shard_map/while/body/eval_jaxpr/reduce_sum | solution.py:51
  92.1 9.1 %multiply_reduce_fusion.6 = (f32[7168]{0:T(1024)S(1)}, f32[7168]{0:T(1024)S(1)}) fusion(bf16[1,7168,512]{2,1,0:T(8,128)(2,1)} %get-tuple-element.169, f32[512]{0:T(512)S(1)} %bitcast.43, f32[512]{0:T(512)S(1)} %bitcast.44, bf16[1,7168,512]{2,1,0:T(8,128)(2,1)} %get-tuple-element.168), kind=kLoop, calls=%fused_computation.2.clone.1 | loop fusion | flops 29345792 | bytes 14741504 | tf_op jit(solution)/shard_map/while/body/eval_jaxpr/reduce_sum | solution.py:46
  103.0 1.1 collective-permute-start.2
  104.1 1.0 collective-permute-done
  105.2 2.3 %collective-permute-done.1 = f32[1,7168]{1,0:T(1,128)S(1)} collective-permute-done((f32[1,7168]{1,0:T(1,128)S(1)}, f32[1,7168]{1,0:T(1,128)S(1)}, u32[]{:S(2)}, u32[]{:S(2)}) %collective-permute-start.1) | collective-permute-done | bytes 28704 | tf_op jit(solution)/shard_map/while/body/eval_jaxpr/ppermute | solution.py:40
  108.8 7.6 %multiply_reduce_fusion.7 = (f32[512]{0:T(512)S(1)}, f32[512]{0:T(512)S(1)}) fusion(bf16[1,7168,512]{2,1,0:T(8,128)(2,1)} %get-tuple-element.169, f32[7168]{0:T(1024)S(1)} %bitcast.34, bf16[1,7168,512]{2,1,0:T(8,128)(2,1)} %get-tuple-element.168), kind=kLoop, calls=%fused_computation.clone.1 | loop fusion | flops 29359104 | bytes 14712832 | tf_op jit(solution)/shard_map/while/body/eval_jaxpr/reduce_sum | solution.py:51
  116.5 9.1 %multiply_reduce_fusion.6 = (f32[7168]{0:T(1024)S(1)}, f32[7168]{0:T(1024)S(1)}) fusion(bf16[1,7168,512]{2,1,0:T(8,128)(2,1)} %get-tuple-element.169, f32[512]{0:T(512)S(1)} %bitcast.43, f32[512]{0:T(512)S(1)} %bitcast.44, bf16[1,7168,512]{2,1,0:T(8,128)(2,1)} %get-tuple-element.168), kind=kLoop, calls=%fused_computation.2.clone.1 | loop fusion | flops 29345792 | bytes 14741504 | tf_op jit(solution)/shard_map/while/body/eval_jaxpr/reduce_sum | solution.py:46
  125.6 1.8 collective-permute-start
  129.5 3.2 %collective-permute-done.1 = f32[1,7168]{1,0:T(1,128)S(1)} collective-permute-done((f32[1,7168]{1,0:T(1,128)S(1)}, f32[1,7168]{1,0:T(1,128)S(1)}, u32[]{:S(2)}, u32[]{:S(2)}) %collective-permute-start.1) | collective-permute-done | bytes 28704 | tf_op jit(solution)/shard_map/while/body/eval_jaxpr/ppermute | solution.py:40
  134.1 7.6 %multiply_reduce_fusion.7 = (f32[512]{0:T(512)S(1)}, f32[512]{0:T(512)S(1)}) fusion(bf16[1,7168,512]{2,1,0:T(8,128)(2,1)} %get-tuple-element.169, f32[7168]{0:T(1024)S(1)} %bitcast.34, bf16[1,7168,512]{2,1,0:T(8,128)(2,1)} %get-tuple-element.168), kind=kLoop, calls=%fused_computation.clone.1 | loop fusion | flops 29359104 | bytes 14712832 | tf_op jit(solution)/shard_map/while/body/eval_jaxpr/reduce_sum | solution.py:51
  141.7 7.4 %multiply_convert_fusion.1 = (bf16[1,7168,512]{2,1,0:T(8,128)(2,1)S(1)}, bf16[1,7168,512]{2,1,0:T(8,128)(2,1)S(1)}) fusion(bf16[1,7168,512]{2,1,0:T(8,128)(2,1)} %get-tuple-element.171, f32[512]{0:T(512)S(1)} %bitcast.40, f32[7168]{0:T(1024)} %bitcast.45, f32[512]{0:T(512)S(1)} %bitcast.42, bf16[1,7168,512]{2,1,0:T(8,128)(2,1)} %get-tuple-element.172), kind=kLoop, calls=%fused_computation.13 | loop fusion | flops 29360128 | bytes 29392896 | tf_op jit(solution)/shard_map/convert_element_type | solution.py:84
  149.2 6.5 %pad_maximum_fusion = bf16[1,7168,1024]{2,1,0:T(8,128)(2,1)} fusion(bf16[1,7168,512]{2,1,0:T(8,128)(2,1)S(1)} %get-tuple-element.102, bf16[1,7168,512]{2,1,0:T(8,128)(2,1)S(1)} %get-tuple-element.101), kind=kLoop, calls=%fused_computation.9 | loop fusion | flops 29360128 | bytes 29360128 | tf_op jit(solution)/shard_map/concatenate | solution.py:88
  155.7 32.4 %all-to-all-done = bf16[32,24,7168]{2,1,0:T(8,128)(2,1)} async-done(((bf16[32,24,7168]{2,1,0:T(8,128)(2,1)}), bf16[32,24,7168]{2,1,0:T(8,128)(2,1)}, u32[]{:S(2)}, u32[]{:S(2)}) %all-to-all-start) | async-done | bytes 11010080 | tf_op jit(solution)/shard_map/all_to_all | solution.py:63
  188.1 16.6 %fusion.2 = f32[1,32,24,1024]{3,2,1,0:T(8,128)S(1)} fusion(bf16[32,24,7168]{2,1,0:T(8,128)(2,1)} %all-to-all-done, bf16[1,7168,1024]{2,1,0:T(8,128)(2,1)} %pad_maximum_fusion), kind=kOutput, calls=%fused_computation.16 | convolution fusion | flops 11274289152 | bytes 28835840 | tf_op jit(solution)/shard_map/ensd,edf->ensf/dot_general | solution.py:89
  204.6 1.4 fusion.5
  (63 shorter events, 16.4 us)
Async XLA Ops:
  0.0 2.5 %copy-start = (bf16[64,7168]{1,0:T(8,128)(2,1)S(1)}, bf16[64,7168]{1,0:T(8,128)(2,1)}, u32[]{:S(2)}) copy-start(bf16[64,7168]{1,0:T(8,128)(2,1)} %param.6) | copy-start | bytes 2752516
  8.2 179.9 %all-to-all-start = ((bf16[32,24,7168]{2,1,0:T(8,128)(2,1)}), bf16[32,24,7168]{2,1,0:T(8,128)(2,1)}, u32[]{:S(2)}, u32[]{:S(2)}) async-start(bf16[32,24,7168]{2,1,0:T(8,128)(2,1)} %convolution_convert_fusion), calls=%async_computation | async-start | bytes 22020096 | tf_op jit(solution)/shard_map/all_to_all | solution.py:63
  25.4 4.6 %collective-permute-start = (f32[1,7168]{1,0:T(1,128)S(1)}, f32[1,7168]{1,0:T(1,128)S(1)}, u32[]{:S(2)}, u32[]{:S(2)}) collective-permute-start(f32[1,7168]{1,0:T(1,128)S(1)} %bitcast.35), channel_id=1, source_target_pairs={{0,3},{1,0},{2,1},{3,2},{4,7},{5,4},{6,5},{7,6},{8,11},{9,8},{10,9... | collective-permute-start | bytes 86024 | tf_op jit(solution)/shard_map/while/body/eval_jaxpr/ppermute | solution.py:40
  28.2 5.4 %collective-permute-start.1 = (f32[1,7168]{1,0:T(1,128)S(1)}, f32[1,7168]{1,0:T(1,128)S(1)}, u32[]{:S(2)}, u32[]{:S(2)}) collective-permute-start(f32[1,7168]{1,0:T(1,128)S(1)} %bitcast.36), channel_id=1, source_target_pairs={{0,2},{1,3},{2,0},{3,1},{4,6},{5,7},{6,4},{7,5},{8,10},{9,11},{10,... | collective-permute-start | bytes 86024 | tf_op jit(solution)/shard_map/while/body/eval_jaxpr/ppermute | solution.py:40
  29.0 5.1 %collective-permute-start.2 = (f32[1,7168]{1,0:T(1,128)S(1)}, f32[1,7168]{1,0:T(1,128)S(1)}, u32[]{:S(2)}, u32[]{:S(2)}) collective-permute-start(f32[1,7168]{1,0:T(1,128)S(1)} %bitcast.37), channel_id=1, source_target_pairs={{0,1},{1,2},{2,3},{3,0},{4,5},{5,6},{6,7},{7,4},{8,9},{9,10},{10,1... | collective-permute-start | bytes 86024 | tf_op jit(solution)/shard_map/while/body/eval_jaxpr/ppermute | solution.py:40
  51.6 3.9 %collective-permute-start = (f32[1,7168]{1,0:T(1,128)S(1)}, f32[1,7168]{1,0:T(1,128)S(1)}, u32[]{:S(2)}, u32[]{:S(2)}) collective-permute-start(f32[1,7168]{1,0:T(1,128)S(1)} %bitcast.35), channel_id=1, source_target_pairs={{0,3},{1,0},{2,1},{3,2},{4,7},{5,4},{6,5},{7,6},{8,11},{9,8},{10,9... | collective-permute-start | bytes 86024 | tf_op jit(solution)/shard_map/while/body/eval_jaxpr/ppermute | solution.py:40
  52.0 5.4 %collective-permute-start.1 = (f32[1,7168]{1,0:T(1,128)S(1)}, f32[1,7168]{1,0:T(1,128)S(1)}, u32[]{:S(2)}, u32[]{:S(2)}) collective-permute-start(f32[1,7168]{1,0:T(1,128)S(1)} %bitcast.36), channel_id=1, source_target_pairs={{0,2},{1,3},{2,0},{3,1},{4,6},{5,7},{6,4},{7,5},{8,10},{9,11},{10,... | collective-permute-start | bytes 86024 | tf_op jit(solution)/shard_map/while/body/eval_jaxpr/ppermute | solution.py:40
  53.4 5.1 %collective-permute-start.2 = (f32[1,7168]{1,0:T(1,128)S(1)}, f32[1,7168]{1,0:T(1,128)S(1)}, u32[]{:S(2)}, u32[]{:S(2)}) collective-permute-start(f32[1,7168]{1,0:T(1,128)S(1)} %bitcast.37), channel_id=1, source_target_pairs={{0,1},{1,2},{2,3},{3,0},{4,5},{5,6},{6,7},{7,4},{8,9},{9,10},{10,1... | collective-permute-start | bytes 86024 | tf_op jit(solution)/shard_map/while/body/eval_jaxpr/ppermute | solution.py:40
  76.0 3.9 %collective-permute-start = (f32[1,7168]{1,0:T(1,128)S(1)}, f32[1,7168]{1,0:T(1,128)S(1)}, u32[]{:S(2)}, u32[]{:S(2)}) collective-permute-start(f32[1,7168]{1,0:T(1,128)S(1)} %bitcast.35), channel_id=1, source_target_pairs={{0,3},{1,0},{2,1},{3,2},{4,7},{5,4},{6,5},{7,6},{8,11},{9,8},{10,9... | collective-permute-start | bytes 86024 | tf_op jit(solution)/shard_map/while/body/eval_jaxpr/ppermute | solution.py:40
  77.8 5.4 %collective-permute-start.1 = (f32[1,7168]{1,0:T(1,128)S(1)}, f32[1,7168]{1,0:T(1,128)S(1)}, u32[]{:S(2)}, u32[]{:S(2)}) collective-permute-start(f32[1,7168]{1,0:T(1,128)S(1)} %bitcast.36), channel_id=1, source_target_pairs={{0,2},{1,3},{2,0},{3,1},{4,6},{5,7},{6,4},{7,5},{8,10},{9,11},{10,... | collective-permute-start | bytes 86024 | tf_op jit(solution)/shard_map/while/body/eval_jaxpr/ppermute | solution.py:40
  78.7 5.1 %collective-permute-start.2 = (f32[1,7168]{1,0:T(1,128)S(1)}, f32[1,7168]{1,0:T(1,128)S(1)}, u32[]{:S(2)}, u32[]{:S(2)}) collective-permute-start(f32[1,7168]{1,0:T(1,128)S(1)} %bitcast.37), channel_id=1, source_target_pairs={{0,1},{1,2},{2,3},{3,0},{4,5},{5,6},{6,7},{7,4},{8,9},{9,10},{10,1... | collective-permute-start | bytes 86024 | tf_op jit(solution)/shard_map/while/body/eval_jaxpr/ppermute | solution.py:40
  101.2 3.9 %collective-permute-start = (f32[1,7168]{1,0:T(1,128)S(1)}, f32[1,7168]{1,0:T(1,128)S(1)}, u32[]{:S(2)}, u32[]{:S(2)}) collective-permute-start(f32[1,7168]{1,0:T(1,128)S(1)} %bitcast.35), channel_id=1, source_target_pairs={{0,3},{1,0},{2,1},{3,2},{4,7},{5,4},{6,5},{7,6},{8,11},{9,8},{10,9... | collective-permute-start | bytes 86024 | tf_op jit(solution)/shard_map/while/body/eval_jaxpr/ppermute | solution.py:40
  102.1 5.4 %collective-permute-start.1 = (f32[1,7168]{1,0:T(1,128)S(1)}, f32[1,7168]{1,0:T(1,128)S(1)}, u32[]{:S(2)}, u32[]{:S(2)}) collective-permute-start(f32[1,7168]{1,0:T(1,128)S(1)} %bitcast.36), channel_id=1, source_target_pairs={{0,2},{1,3},{2,0},{3,1},{4,6},{5,7},{6,4},{7,5},{8,10},{9,11},{10,... | collective-permute-start | bytes 86024 | tf_op jit(solution)/shard_map/while/body/eval_jaxpr/ppermute | solution.py:40
  103.0 5.1 %collective-permute-start.2 = (f32[1,7168]{1,0:T(1,128)S(1)}, f32[1,7168]{1,0:T(1,128)S(1)}, u32[]{:S(2)}, u32[]{:S(2)}) collective-permute-start(f32[1,7168]{1,0:T(1,128)S(1)} %bitcast.37), channel_id=1, source_target_pairs={{0,1},{1,2},{2,3},{3,0},{4,5},{5,6},{6,7},{7,4},{8,9},{9,10},{10,1... | collective-permute-start | bytes 86024 | tf_op jit(solution)/shard_map/while/body/eval_jaxpr/ppermute | solution.py:40
  125.6 3.9 %collective-permute-start = (f32[1,7168]{1,0:T(1,128)S(1)}, f32[1,7168]{1,0:T(1,128)S(1)}, u32[]{:S(2)}, u32[]{:S(2)}) collective-permute-start(f32[1,7168]{1,0:T(1,128)S(1)} %bitcast.35), channel_id=1, source_target_pairs={{0,3},{1,0},{2,1},{3,2},{4,7},{5,4},{6,5},{7,6},{8,11},{9,8},{10,9... | collective-permute-start | bytes 86024 | tf_op jit(solution)/shard_map/while/body/eval_jaxpr/ppermute | solution.py:40
  127.4 5.4 %collective-permute-start.1 = (f32[1,7168]{1,0:T(1,128)S(1)}, f32[1,7168]{1,0:T(1,128)S(1)}, u32[]{:S(2)}, u32[]{:S(2)}) collective-permute-start(f32[1,7168]{1,0:T(1,128)S(1)} %bitcast.36), channel_id=1, source_target_pairs={{0,2},{1,3},{2,0},{3,1},{4,6},{5,7},{6,4},{7,5},{8,10},{9,11},{10,... | collective-permute-start | bytes 86024 | tf_op jit(solution)/shard_map/while/body/eval_jaxpr/ppermute | solution.py:40
  128.3 5.1 %collective-permute-start.2 = (f32[1,7168]{1,0:T(1,128)S(1)}, f32[1,7168]{1,0:T(1,128)S(1)}, u32[]{:S(2)}, u32[]{:S(2)}) collective-permute-start(f32[1,7168]{1,0:T(1,128)S(1)} %bitcast.37), channel_id=1, source_target_pairs={{0,1},{1,2},{2,3},{3,0},{4,5},{5,6},{6,7},{7,4},{8,9},{9,10},{10,1... | collective-permute-start | bytes 86024 | tf_op jit(solution)/shard_map/while/body/eval_jaxpr/ppermute | solution.py:40
  188.1 18.0 %copy-start.1 = (bf16[64,7168]{1,0:T(8,128)(2,1)S(1)}, bf16[64,7168]{1,0:T(8,128)(2,1)}, u32[]{:S(2)}) copy-start(bf16[64,7168]{1,0:T(8,128)(2,1)} %param.6) | copy-start | bytes 2752516

commit v6 on v5

--- a/solution.py
+++ b/solution.py
@@ -85,10 +85,9 @@
     up_eq = (up_weight.astype(jnp.float32) * row_scale[:, :, None] * up_cols[:, None, :]).astype(
         jnp.bfloat16
     )
-    both_eq = lax.optimization_barrier(jnp.concatenate([gate_eq, up_eq], axis=2))
-    act = jnp.einsum("ensd,edf->ensf", routed, both_eq, preferred_element_type=jnp.float32)
-    gate_act = act[..., :ff_local]
-    up_act = act[..., ff_local:]
+    gate_eq, up_eq = lax.optimization_barrier((gate_eq, up_eq))
+    gate_act = jnp.einsum("ensd,edf->ensf", routed, gate_eq, preferred_element_type=jnp.float32)
+    up_act = jnp.einsum("ensd,edf->ensf", routed, up_eq, preferred_element_type=jnp.float32)
     return (jax.nn.silu(gate_act) * up_act).astype(jnp.bfloat16)
 
 

time: 206 us -> 211 us (1.024)
  starting transfers between devices: 24.1 us -> 30.6 us
  matrix products: 22.5 us -> 26.3 us
  other arithmetic: 103 us -> 99.7 us
    ppermute x15, waiting for transfers between devices: 22 us -> 15 us  [hidden_sum(): lax.ppermute(values, 'hidden', [(i, (i + shift) % n) for i in range(n)])]
    concatenate x1 -> x0, other arithmetic: 6.5 us -> none  [shards(): jnp.concatenate([gate_eq, up_eq], axis=2)]
    ppermute x15, starting transfers between devices: 16.1 us -> 22.6 us  [hidden_sum(): lax.ppermute(values, 'hidden', [(i, (i + shift) % n) for i in range(n)])]
    all_to_all x1, waiting for transfers between devices: 32.4 us -> 37.6 us  [shards(): lax.all_to_all(outgoing, 'expert', split_axis=0, concat_axis=0, tiled=True)]
    dot_general x1 -> x2, matrix products: 16.6 us -> 20.4 us  [the longest x1 10.9 us: shards(): jnp.einsum('ensd,edf->ensf', routed, gate_eq, preferred_element_type=jnp....]
    convert_element_type x2 -> x1, other arithmetic: 8.84 us -> 11.7 us  [shards(): (up_weight.astype(jnp.float32) * row_scale[:, :, None] * up_cols[:, None,...]
  transfers between devices with their start and end apart: 16 -> 16, of which waited for: 15 -> 15; matrix products, arithmetic and copies ran while one was open for 49% -> 47% of each run, Pallas kernels for 0% -> 0%
where the time goes in v6:
time: 211 us
  other arithmetic  99.7 us (47%)
  waiting for transfers between devices  52.6 us (25%)
  starting transfers between devices  30.6 us (15%)
  matrix products  26.3 us (12%)
    reduce_sum x5, other arithmetic, row_terms(): return jnp.sum(values * values * cols_sq[:, None, :], axis=2)  45.5 us
    reduce_sum x5, other arithmetic, col_terms(): return jnp.sum(values * values * scale_sq[:, :, None], axis=1)  37.9 us
    all_to_all x1, waiting for transfers between devices, shards(): lax.all_to_all(outgoing, 'expert', split_axis=0, concat_axis=0, tiled=True)  37.6 us
    ppermute x15, starting transfers between devices, hidden_sum(): lax.ppermute(values, 'hidden', [(i, (i + shift) % n) for i in range(n)])  22.6 us
    ppermute x15, waiting for transfers between devices, hidden_sum(): lax.ppermute(values, 'hidden', [(i, (i + shift) % n) for i in range(n)])  15 us
    convert_element_type x1, other arithmetic, shards(): (up_weight.astype(jnp.float32) * row_scale[:, :, None] * up_cols[:, None,...  11.7 us
    dot_general x1, matrix products, shards(): jnp.einsum('ensd,edf->ensf', routed, gate_eq, preferred_element_type=jnp....  10.9 us
    dot_general x1, matrix products, shards(): jnp.einsum('ensd,edf->ensf', routed, up_eq, preferred_element_type=jnp.fl...  9.44 us
  transfers between devices with their start and end apart: 16, of which 15 were waited for; matrix products, arithmetic and copies ran while one was open for 47% of the time, Pallas kernels for 0%

profile of v6, /device:TPU:48, one launch (start us, length us, event | category | flops | bytes accessed | tf_op | source)
XLA Modules:
  0.0 210.7 jit_solution(16542534189593201384)
XLA Ops:
  2.5 5.6 %convolution_convert_fusion = bf16[32,24,7168]{2,1,0:T(8,128)(2,1)} fusion(pred[32,24,64]{2,1,0:T(8,128)(4,1)S(1)} %and_reduce_fusion, bf16[64,7168]{1,0:T(8,128)(2,1)S(1)} %copy-done), kind=kOutput, calls=%fused_computation.11 | convolution fusion | flops 710148096 | bytes 11976704 | tf_op jit(solution)/shard_map/est,td->esd/dot_general | solution.py:32
  8.1 8.0 %all-to-all-start = ((bf16[32,24,7168]{2,1,0:T(8,128)(2,1)}), bf16[32,24,7168]{2,1,0:T(8,128)(2,1)}, u32[]{:S(2)}, u32[]{:S(2)}) async-start(bf16[32,24,7168]{2,1,0:T(8,128)(2,1)} %convolution_convert_fusion), calls=%async_computation | async-start | bytes 22020096 | tf_op jit(solution)/shard_map/all_to_all | solution.py:63
  16.2 124.8 %while.16 = (s32[]{:T(128)}, f32[1,512]{1,0:T(1,128)S(1)}, f32[1,512]{1,0:T(1,128)S(1)}, f32[1,7168]{1,0:T(1,128)}, bf16[1,7168,512]{2,1,0:T(8,128)(2,1)}, /*index=5*/bf16[1,7168,512]{2,1,0:T(8,128)(2,1)}, s32[]{:T(128)}) while((s32[]{:T(128)}, f32[1,512]{1,0:T(1,128)S(1)}, f32[1,512]{1,0:T(1,128)S(1)}, f32[1,7168]{1,0:T(1,128)}, ...), condition=%wide.region_7.0_spmd, body=%wide.region_2.0_spmd.sunk | while | flops 58757120 | bytes 30077124 | solution.py:81
  16.3 9.1 %multiply_reduce_fusion.6 = (f32[7168]{0:T(1024)S(1)}, f32[7168]{0:T(1024)S(1)}) fusion(bf16[1,7168,512]{2,1,0:T(8,128)(2,1)} %get-tuple-element.173, f32[512]{0:T(512)S(1)} %bitcast.50, f32[512]{0:T(512)S(1)} %bitcast.51, bf16[1,7168,512]{2,1,0:T(8,128)(2,1)} %get-tuple-element.172), kind=kLoop, calls=%fused_computation.2.clone.1 | loop fusion | flops 29345792 | bytes 14741504 | tf_op jit(solution)/shard_map/while/body/eval_jaxpr/reduce_sum | solution.py:46
  25.4 1.6 collective-permute-start.2
  26.9 2.7 %collective-permute-start.1 = (f32[1,7168]{1,0:T(1,128)S(1)}, f32[1,7168]{1,0:T(1,128)S(1)}, u32[]{:S(2)}, u32[]{:S(2)}) collective-permute-start(f32[1,7168]{1,0:T(1,128)S(1)} %bitcast.43), channel_id=1, source_target_pairs={{0,2},{1,3},{2,0},{3,1},{4,6},{5,7},{6,4},{7,5},{8,10},{9,11},{10,... | collective-permute-start | bytes 86024 | tf_op jit(solution)/shard_map/while/body/eval_jaxpr/ppermute | solution.py:40
  29.7 1.4 collective-permute-start
  31.1 1.2 collective-permute-done.1
  32.3 1.2 collective-permute-done
  34.2 7.6 %multiply_reduce_fusion.7 = (f32[512]{0:T(512)S(1)}, f32[512]{0:T(512)S(1)}) fusion(bf16[1,7168,512]{2,1,0:T(8,128)(2,1)} %get-tuple-element.173, f32[7168]{0:T(1024)S(1)} %bitcast.41, bf16[1,7168,512]{2,1,0:T(8,128)(2,1)} %get-tuple-element.172), kind=kLoop, calls=%fused_computation.clone.1 | loop fusion | flops 29359104 | bytes 14712832 | tf_op jit(solution)/shard_map/while/body/eval_jaxpr/reduce_sum | solution.py:51
  41.9 9.1 %multiply_reduce_fusion.6 = (f32[7168]{0:T(1024)S(1)}, f32[7168]{0:T(1024)S(1)}) fusion(bf16[1,7168,512]{2,1,0:T(8,128)(2,1)} %get-tuple-element.173, f32[512]{0:T(512)S(1)} %bitcast.50, f32[512]{0:T(512)S(1)} %bitcast.51, bf16[1,7168,512]{2,1,0:T(8,128)(2,1)} %get-tuple-element.172), kind=kLoop, calls=%fused_computation.2.clone.1 | loop fusion | flops 29345792 | bytes 14741504 | tf_op jit(solution)/shard_map/while/body/eval_jaxpr/reduce_sum | solution.py:46
  51.3 3.8 %collective-permute-start.1 = (f32[1,7168]{1,0:T(1,128)S(1)}, f32[1,7168]{1,0:T(1,128)S(1)}, u32[]{:S(2)}, u32[]{:S(2)}) collective-permute-start(f32[1,7168]{1,0:T(1,128)S(1)} %bitcast.43), channel_id=1, source_target_pairs={{0,2},{1,3},{2,0},{3,1},{4,6},{5,7},{6,4},{7,5},{8,10},{9,11},{10,... | collective-permute-start | bytes 86024 | tf_op jit(solution)/shard_map/while/body/eval_jaxpr/ppermute | solution.py:40
  57.3 1.7 collective-permute-done
  59.7 7.6 %multiply_reduce_fusion.7 = (f32[512]{0:T(512)S(1)}, f32[512]{0:T(512)S(1)}) fusion(bf16[1,7168,512]{2,1,0:T(8,128)(2,1)} %get-tuple-element.173, f32[7168]{0:T(1024)S(1)} %bitcast.41, bf16[1,7168,512]{2,1,0:T(8,128)(2,1)} %get-tuple-element.172), kind=kLoop, calls=%fused_computation.clone.1 | loop fusion | flops 29359104 | bytes 14712832 | tf_op jit(solution)/shard_map/while/body/eval_jaxpr/reduce_sum | solution.py:51
  67.4 9.1 %multiply_reduce_fusion.6 = (f32[7168]{0:T(1024)S(1)}, f32[7168]{0:T(1024)S(1)}) fusion(bf16[1,7168,512]{2,1,0:T(8,128)(2,1)} %get-tuple-element.173, f32[512]{0:T(512)S(1)} %bitcast.50, f32[512]{0:T(512)S(1)} %bitcast.51, bf16[1,7168,512]{2,1,0:T(8,128)(2,1)} %get-tuple-element.172), kind=kLoop, calls=%fused_computation.2.clone.1 | loop fusion | flops 29345792 | bytes 14741504 | tf_op jit(solution)/shard_map/while/body/eval_jaxpr/reduce_sum | solution.py:46
  76.6 2.7 %collective-permute-start.1 = (f32[1,7168]{1,0:T(1,128)S(1)}, f32[1,7168]{1,0:T(1,128)S(1)}, u32[]{:S(2)}, u32[]{:S(2)}) collective-permute-start(f32[1,7168]{1,0:T(1,128)S(1)} %bitcast.43), channel_id=1, source_target_pairs={{0,2},{1,3},{2,0},{3,1},{4,6},{5,7},{6,4},{7,5},{8,10},{9,11},{10,... | collective-permute-start | bytes 86024 | tf_op jit(solution)/shard_map/while/body/eval_jaxpr/ppermute | solution.py:40
  79.3 1.4 collective-permute-start
  83.8 7.6 %multiply_reduce_fusion.7 = (f32[512]{0:T(512)S(1)}, f32[512]{0:T(512)S(1)}) fusion(bf16[1,7168,512]{2,1,0:T(8,128)(2,1)} %get-tuple-element.173, f32[7168]{0:T(1024)S(1)} %bitcast.41, bf16[1,7168,512]{2,1,0:T(8,128)(2,1)} %get-tuple-element.172), kind=kLoop, calls=%fused_computation.clone.1 | loop fusion | flops 29359104 | bytes 14712832 | tf_op jit(solution)/shard_map/while/body/eval_jaxpr/reduce_sum | solution.py:51
  91.5 9.1 %multiply_reduce_fusion.6 = (f32[7168]{0:T(1024)S(1)}, f32[7168]{0:T(1024)S(1)}) fusion(bf16[1,7168,512]{2,1,0:T(8,128)(2,1)} %get-tuple-element.173, f32[512]{0:T(512)S(1)} %bitcast.50, f32[512]{0:T(512)S(1)} %bitcast.51, bf16[1,7168,512]{2,1,0:T(8,128)(2,1)} %get-tuple-element.172), kind=kLoop, calls=%fused_computation.2.clone.1 | loop fusion | flops 29345792 | bytes 14741504 | tf_op jit(solution)/shard_map/while/body/eval_jaxpr/reduce_sum | solution.py:46
  100.6 1.5 collective-permute-start.2
  102.0 2.7 %collective-permute-start.1 = (f32[1,7168]{1,0:T(1,128)S(1)}, f32[1,7168]{1,0:T(1,128)S(1)}, u32[]{:S(2)}, u32[]{:S(2)}) collective-permute-start(f32[1,7168]{1,0:T(1,128)S(1)} %bitcast.43), channel_id=1, source_target_pairs={{0,2},{1,3},{2,0},{3,1},{4,6},{5,7},{6,4},{7,5},{8,10},{9,11},{10,... | collective-permute-start | bytes 86024 | tf_op jit(solution)/shard_map/while/body/eval_jaxpr/ppermute | solution.py:40
  105.7 1.7 collective-permute-done.1
  107.4 1.2 collective-permute-done
  109.3 7.6 %multiply_reduce_fusion.7 = (f32[512]{0:T(512)S(1)}, f32[512]{0:T(512)S(1)}) fusion(bf16[1,7168,512]{2,1,0:T(8,128)(2,1)} %get-tuple-element.173, f32[7168]{0:T(1024)S(1)} %bitcast.41, bf16[1,7168,512]{2,1,0:T(8,128)(2,1)} %get-tuple-element.172), kind=kLoop, calls=%fused_computation.clone.1 | loop fusion | flops 29359104 | bytes 14712832 | tf_op jit(solution)/shard_map/while/body/eval_jaxpr/reduce_sum | solution.py:51
  117.0 9.1 %multiply_reduce_fusion.6 = (f32[7168]{0:T(1024)S(1)}, f32[7168]{0:T(1024)S(1)}) fusion(bf16[1,7168,512]{2,1,0:T(8,128)(2,1)} %get-tuple-element.173, f32[512]{0:T(512)S(1)} %bitcast.50, f32[512]{0:T(512)S(1)} %bitcast.51, bf16[1,7168,512]{2,1,0:T(8,128)(2,1)} %get-tuple-element.172), kind=kLoop, calls=%fused_computation.2.clone.1 | loop fusion | flops 29345792 | bytes 14741504 | tf_op jit(solution)/shard_map/while/body/eval_jaxpr/reduce_sum | solution.py:46
  126.2 2.7 %collective-permute-start.1 = (f32[1,7168]{1,0:T(1,128)S(1)}, f32[1,7168]{1,0:T(1,128)S(1)}, u32[]{:S(2)}, u32[]{:S(2)}) collective-permute-start(f32[1,7168]{1,0:T(1,128)S(1)} %bitcast.43), channel_id=1, source_target_pairs={{0,2},{1,3},{2,0},{3,1},{4,6},{5,7},{6,4},{7,5},{8,10},{9,11},{10,... | collective-permute-start | bytes 86024 | tf_op jit(solution)/shard_map/while/body/eval_jaxpr/ppermute | solution.py:40
  128.9 1.4 collective-permute-start
  133.4 7.6 %multiply_reduce_fusion.7 = (f32[512]{0:T(512)S(1)}, f32[512]{0:T(512)S(1)}) fusion(bf16[1,7168,512]{2,1,0:T(8,128)(2,1)} %get-tuple-element.173, f32[7168]{0:T(1024)S(1)} %bitcast.41, bf16[1,7168,512]{2,1,0:T(8,128)(2,1)} %get-tuple-element.172), kind=kLoop, calls=%fused_computation.clone.1 | loop fusion | flops 29359104 | bytes 14712832 | tf_op jit(solution)/shard_map/while/body/eval_jaxpr/reduce_sum | solution.py:51
  141.1 11.7 %multiply_convert_fusion = (bf16[1,7168,512]{2,1,0:T(8,128)(2,1)}, bf16[1,7168,512]{2,1,0:T(8,128)(2,1)}) fusion(bf16[1,7168,512]{2,1,0:T(8,128)(2,1)} %get-tuple-element.175, f32[512]{0:T(512)S(1)} %bitcast.47, f32[7168]{0:T(1024)} %bitcast.52, f32[512]{0:T(512)S(1)} %bitcast.49, bf16[1,7168,512]{2,1,0:T(8,128)(2,1)} %get-tuple-element.176), kind=kLoop, calls=%fused_computation.9 | loop fusion | flops 29360128 | bytes 29392896 | tf_op jit(solution)/shard_map/convert_element_type | solution.py:85
  152.7 37.6 %all-to-all-done = bf16[32,24,7168]{2,1,0:T(8,128)(2,1)} async-done(((bf16[32,24,7168]{2,1,0:T(8,128)(2,1)}), bf16[32,24,7168]{2,1,0:T(8,128)(2,1)}, u32[]{:S(2)}, u32[]{:S(2)}) %all-to-all-start) | async-done | bytes 11010080 | tf_op jit(solution)/shard_map/all_to_all | solution.py:63
  190.4 10.9 %fusion.2 = f32[32,24,512]{2,1,0:T(8,128)S(1)} fusion(bf16[32,24,7168]{2,1,0:T(8,128)(2,1)} %all-to-all-done, bf16[1,7168,512]{2,1,0:T(8,128)(2,1)} %get-tuple-element.85), kind=kOutput, calls=%fused_computation.14 | convolution fusion | flops 5637144576 | bytes 19922944 | tf_op jit(solution)/shard_map/ensd,edf->ensf/dot_general | solution.py:89
  201.3 9.4 %fusion.6 = bf16[1,32,24,512]{3,2,1,0:T(8,128)(2,1)} fusion(bf16[32,24,7168]{2,1,0:T(8,128)(2,1)} %all-to-all-done, bf16[1,7168,512]{2,1,0:T(8,128)(2,1)S(1)} %copy-done.1, f32[32,24,512]{2,1,0:T(8,128)S(1)} %fusion.2), kind=kOutput, calls=%fused_computation.18 | convolution fusion | flops 5639503872 | bytes 20709376 | tf_op jit(solution)/shard_map/ensd,edf->ensf/dot_general | solution.py:90
  (62 shorter events, 14.6 us)
Async XLA Ops:
  0.0 2.5 %copy-start = (bf16[64,7168]{1,0:T(8,128)(2,1)S(1)}, bf16[64,7168]{1,0:T(8,128)(2,1)}, u32[]{:S(2)}) copy-start(bf16[64,7168]{1,0:T(8,128)(2,1)} %param.6) | copy-start | bytes 2752516
  8.1 182.2 %all-to-all-start = ((bf16[32,24,7168]{2,1,0:T(8,128)(2,1)}), bf16[32,24,7168]{2,1,0:T(8,128)(2,1)}, u32[]{:S(2)}, u32[]{:S(2)}) async-start(bf16[32,24,7168]{2,1,0:T(8,128)(2,1)} %convolution_convert_fusion), calls=%async_computation | async-start | bytes 22020096 | tf_op jit(solution)/shard_map/all_to_all | solution.py:63
  25.4 5.7 %collective-permute-start.2 = (f32[1,7168]{1,0:T(1,128)S(1)}, f32[1,7168]{1,0:T(1,128)S(1)}, u32[]{:S(2)}, u32[]{:S(2)}) collective-permute-start(f32[1,7168]{1,0:T(1,128)S(1)} %bitcast.42), channel_id=1, source_target_pairs={{0,1},{1,2},{2,3},{3,0},{4,5},{5,6},{6,7},{7,4},{8,9},{9,10},{10,1... | collective-permute-start | bytes 86024 | tf_op jit(solution)/shard_map/while/body/eval_jaxpr/ppermute | solution.py:40
  26.9 5.4 %collective-permute-start.1 = (f32[1,7168]{1,0:T(1,128)S(1)}, f32[1,7168]{1,0:T(1,128)S(1)}, u32[]{:S(2)}, u32[]{:S(2)}) collective-permute-start(f32[1,7168]{1,0:T(1,128)S(1)} %bitcast.43), channel_id=1, source_target_pairs={{0,2},{1,3},{2,0},{3,1},{4,6},{5,7},{6,4},{7,5},{8,10},{9,11},{10,... | collective-permute-start | bytes 86024 | tf_op jit(solution)/shard_map/while/body/eval_jaxpr/ppermute | solution.py:40
  29.7 3.9 %collective-permute-start = (f32[1,7168]{1,0:T(1,128)S(1)}, f32[1,7168]{1,0:T(1,128)S(1)}, u32[]{:S(2)}, u32[]{:S(2)}) collective-permute-start(f32[1,7168]{1,0:T(1,128)S(1)} %bitcast.44), channel_id=1, source_target_pairs={{0,3},{1,0},{2,1},{3,2},{4,7},{5,4},{6,5},{7,6},{8,11},{9,8},{10,9... | collective-permute-start | bytes 86024 | tf_op jit(solution)/shard_map/while/body/eval_jaxpr/ppermute | solution.py:40
  51.0 5.1 %collective-permute-start.2 = (f32[1,7168]{1,0:T(1,128)S(1)}, f32[1,7168]{1,0:T(1,128)S(1)}, u32[]{:S(2)}, u32[]{:S(2)}) collective-permute-start(f32[1,7168]{1,0:T(1,128)S(1)} %bitcast.42), channel_id=1, source_target_pairs={{0,1},{1,2},{2,3},{3,0},{4,5},{5,6},{6,7},{7,4},{8,9},{9,10},{10,1... | collective-permute-start | bytes 86024 | tf_op jit(solution)/shard_map/while/body/eval_jaxpr/ppermute | solution.py:40
  51.3 6.0 %collective-permute-start.1 = (f32[1,7168]{1,0:T(1,128)S(1)}, f32[1,7168]{1,0:T(1,128)S(1)}, u32[]{:S(2)}, u32[]{:S(2)}) collective-permute-start(f32[1,7168]{1,0:T(1,128)S(1)} %bitcast.43), channel_id=1, source_target_pairs={{0,2},{1,3},{2,0},{3,1},{4,6},{5,7},{6,4},{7,5},{8,10},{9,11},{10,... | collective-permute-start | bytes 86024 | tf_op jit(solution)/shard_map/while/body/eval_jaxpr/ppermute | solution.py:40
  55.2 3.9 %collective-permute-start = (f32[1,7168]{1,0:T(1,128)S(1)}, f32[1,7168]{1,0:T(1,128)S(1)}, u32[]{:S(2)}, u32[]{:S(2)}) collective-permute-start(f32[1,7168]{1,0:T(1,128)S(1)} %bitcast.44), channel_id=1, source_target_pairs={{0,3},{1,0},{2,1},{3,2},{4,7},{5,4},{6,5},{7,6},{8,11},{9,8},{10,9... | collective-permute-start | bytes 86024 | tf_op jit(solution)/shard_map/while/body/eval_jaxpr/ppermute | solution.py:40
  76.5 5.1 %collective-permute-start.2 = (f32[1,7168]{1,0:T(1,128)S(1)}, f32[1,7168]{1,0:T(1,128)S(1)}, u32[]{:S(2)}, u32[]{:S(2)}) collective-permute-start(f32[1,7168]{1,0:T(1,128)S(1)} %bitcast.42), channel_id=1, source_target_pairs={{0,1},{1,2},{2,3},{3,0},{4,5},{5,6},{6,7},{7,4},{8,9},{9,10},{10,1... | collective-permute-start | bytes 86024 | tf_op jit(solution)/shard_map/while/body/eval_jaxpr/ppermute | solution.py:40
  76.6 5.5 %collective-permute-start.1 = (f32[1,7168]{1,0:T(1,128)S(1)}, f32[1,7168]{1,0:T(1,128)S(1)}, u32[]{:S(2)}, u32[]{:S(2)}) collective-permute-start(f32[1,7168]{1,0:T(1,128)S(1)} %bitcast.43), channel_id=1, source_target_pairs={{0,2},{1,3},{2,0},{3,1},{4,6},{5,7},{6,4},{7,5},{8,10},{9,11},{10,... | collective-permute-start | bytes 86024 | tf_op jit(solution)/shard_map/while/body/eval_jaxpr/ppermute | solution.py:40
  79.3 3.9 %collective-permute-start = (f32[1,7168]{1,0:T(1,128)S(1)}, f32[1,7168]{1,0:T(1,128)S(1)}, u32[]{:S(2)}, u32[]{:S(2)}) collective-permute-start(f32[1,7168]{1,0:T(1,128)S(1)} %bitcast.44), channel_id=1, source_target_pairs={{0,3},{1,0},{2,1},{3,2},{4,7},{5,4},{6,5},{7,6},{8,11},{9,8},{10,9... | collective-permute-start | bytes 86024 | tf_op jit(solution)/shard_map/while/body/eval_jaxpr/ppermute | solution.py:40
  100.6 5.1 %collective-permute-start.2 = (f32[1,7168]{1,0:T(1,128)S(1)}, f32[1,7168]{1,0:T(1,128)S(1)}, u32[]{:S(2)}, u32[]{:S(2)}) collective-permute-start(f32[1,7168]{1,0:T(1,128)S(1)} %bitcast.42), channel_id=1, source_target_pairs={{0,1},{1,2},{2,3},{3,0},{4,5},{5,6},{6,7},{7,4},{8,9},{9,10},{10,1... | collective-permute-start | bytes 86024 | tf_op jit(solution)/shard_map/while/body/eval_jaxpr/ppermute | solution.py:40
  102.0 5.4 %collective-permute-start.1 = (f32[1,7168]{1,0:T(1,128)S(1)}, f32[1,7168]{1,0:T(1,128)S(1)}, u32[]{:S(2)}, u32[]{:S(2)}) collective-permute-start(f32[1,7168]{1,0:T(1,128)S(1)} %bitcast.43), channel_id=1, source_target_pairs={{0,2},{1,3},{2,0},{3,1},{4,6},{5,7},{6,4},{7,5},{8,10},{9,11},{10,... | collective-permute-start | bytes 86024 | tf_op jit(solution)/shard_map/while/body/eval_jaxpr/ppermute | solution.py:40
  104.8 3.9 %collective-permute-start = (f32[1,7168]{1,0:T(1,128)S(1)}, f32[1,7168]{1,0:T(1,128)S(1)}, u32[]{:S(2)}, u32[]{:S(2)}) collective-permute-start(f32[1,7168]{1,0:T(1,128)S(1)} %bitcast.44), channel_id=1, source_target_pairs={{0,3},{1,0},{2,1},{3,2},{4,7},{5,4},{6,5},{7,6},{8,11},{9,8},{10,9... | collective-permute-start | bytes 86024 | tf_op jit(solution)/shard_map/while/body/eval_jaxpr/ppermute | solution.py:40
  126.1 5.1 %collective-permute-start.2 = (f32[1,7168]{1,0:T(1,128)S(1)}, f32[1,7168]{1,0:T(1,128)S(1)}, u32[]{:S(2)}, u32[]{:S(2)}) collective-permute-start(f32[1,7168]{1,0:T(1,128)S(1)} %bitcast.42), channel_id=1, source_target_pairs={{0,1},{1,2},{2,3},{3,0},{4,5},{5,6},{6,7},{7,4},{8,9},{9,10},{10,1... | collective-permute-start | bytes 86024 | tf_op jit(solution)/shard_map/while/body/eval_jaxpr/ppermute | solution.py:40
  126.2 5.5 %collective-permute-start.1 = (f32[1,7168]{1,0:T(1,128)S(1)}, f32[1,7168]{1,0:T(1,128)S(1)}, u32[]{:S(2)}, u32[]{:S(2)}) collective-permute-start(f32[1,7168]{1,0:T(1,128)S(1)} %bitcast.43), channel_id=1, source_target_pairs={{0,2},{1,3},{2,0},{3,1},{4,6},{5,7},{6,4},{7,5},{8,10},{9,11},{10,... | collective-permute-start | bytes 86024 | tf_op jit(solution)/shard_map/while/body/eval_jaxpr/ppermute | solution.py:40
  128.9 3.9 %collective-permute-start = (f32[1,7168]{1,0:T(1,128)S(1)}, f32[1,7168]{1,0:T(1,128)S(1)}, u32[]{:S(2)}, u32[]{:S(2)}) collective-permute-start(f32[1,7168]{1,0:T(1,128)S(1)} %bitcast.44), channel_id=1, source_target_pairs={{0,3},{1,0},{2,1},{3,2},{4,7},{5,4},{6,5},{7,6},{8,11},{9,8},{10,9... | collective-permute-start | bytes 86024 | tf_op jit(solution)/shard_map/while/body/eval_jaxpr/ppermute | solution.py:40
  190.4 10.9 %copy-start.1 = (bf16[1,7168,512]{2,1,0:T(8,128)(2,1)S(1)}, bf16[1,7168,512]{2,1,0:T(8,128)(2,1)}, u32[]{:S(2)}) copy-start(bf16[1,7168,512]{2,1,0:T(8,128)(2,1)} %get-tuple-element.86) | copy-start | bytes 22020100

commit v7 on v5

--- a/solution.py
+++ b/solution.py
@@ -23,12 +23,12 @@
     ).astype(jnp.bfloat16)
     before = jnp.dot(earlier, onehot, preferred_element_type=jnp.float32)
     my_rank = jnp.sum(before * onehot.astype(jnp.float32), axis=1).astype(jnp.int32)
-    pair_ids = flat_ids.reshape(tok_local, topk)
-    pair_rank = my_rank.reshape(tok_local, topk)
+    pair_ids = flat_ids.reshape(tok_local, topk).T
+    pair_rank = my_rank.reshape(tok_local, topk).T
     hit = (pair_ids[None, None] == jnp.arange(EXPERTS, dtype=jnp.int32)[:, None, None, None]) & (
         pair_rank[None, None] == jnp.arange(CAP, dtype=jnp.int32)[None, :, None, None]
     )
-    select = jnp.any(hit, axis=3).astype(tokens.dtype)
+    select = jnp.any(hit, axis=2).astype(tokens.dtype)
     rows = jnp.einsum("est,td->esd", select, tokens, preferred_element_type=jnp.float32)
     return rows.astype(tokens.dtype)
 

time: 206 us -> 207 us (level)
  no operation moved by 1% of the time
where the time goes in v7:
time: 207 us
  other arithmetic  103 us (50%)
  waiting for transfers between devices  54.4 us (26%)
  starting transfers between devices  24.1 us (12%)
  matrix products  22.5 us (11%)
    reduce_sum x5, other arithmetic, row_terms(): return jnp.sum(values * values * cols_sq[:, None, :], axis=2)  45.5 us
    reduce_sum x5, other arithmetic, col_terms(): return jnp.sum(values * values * scale_sq[:, :, None], axis=1)  37.9 us
    all_to_all x1, waiting for transfers between devices, shards(): lax.all_to_all(outgoing, 'expert', split_axis=0, concat_axis=0, tiled=True)  32.4 us
    ppermute x15, waiting for transfers between devices, hidden_sum(): lax.ppermute(values, 'hidden', [(i, (i + shift) % n) for i in range(n)])  22 us
    dot_general x1, matrix products, shards(): jnp.einsum('ensd,edf->ensf', routed, both_eq, preferred_element_type=jnp....  16.5 us
    ppermute x15, starting transfers between devices, hidden_sum(): lax.ppermute(values, 'hidden', [(i, (i + shift) % n) for i in range(n)])  16.1 us
    all_to_all x1, starting transfers between devices, shards(): lax.all_to_all(outgoing, 'expert', split_axis=0, concat_axis=0, tiled=True)  8.04 us
    convert_element_type x1, other arithmetic, shards(): gate_eq = (gate_weight.astype(jnp.float32) * row_scale[:, :, None] * gate...  7.45 us
  transfers between devices with their start and end apart: 16, of which 15 were waited for; matrix products, arithmetic and copies ran while one was open for 49% of the time, Pallas kernels for 0%

profile of v7, /device:TPU:48, one launch (start us, length us, event | category | flops | bytes accessed | tf_op | source)
XLA Modules:
  0.0 206.8 jit_solution(9575235135156163182)
XLA Ops:
  3.3 5.7 %convolution_convert_fusion = bf16[32,24,7168]{2,1,0:T(8,128)(2,1)} fusion(pred[32,24,64]{2,1,0:T(8,128)(4,1)S(1)} %and_reduce_fusion, bf16[64,7168]{1,0:T(8,128)(2,1)S(1)} %copy-done), kind=kOutput, calls=%fused_computation.14 | convolution fusion | flops 710148096 | bytes 11976704 | tf_op jit(solution)/shard_map/est,td->esd/dot_general | solution.py:32
  8.9 8.0 %all-to-all-start = ((bf16[32,24,7168]{2,1,0:T(8,128)(2,1)}), bf16[32,24,7168]{2,1,0:T(8,128)(2,1)}, u32[]{:S(2)}, u32[]{:S(2)}) async-start(bf16[32,24,7168]{2,1,0:T(8,128)(2,1)} %convolution_convert_fusion), calls=%async_computation | async-start | bytes 22020096 | tf_op jit(solution)/shard_map/all_to_all | solution.py:63
  17.0 125.4 %while.16 = (s32[]{:T(128)}, f32[1,512]{1,0:T(1,128)S(1)}, f32[1,512]{1,0:T(1,128)S(1)}, f32[1,7168]{1,0:T(1,128)}, bf16[1,7168,512]{2,1,0:T(8,128)(2,1)}, /*index=5*/bf16[1,7168,512]{2,1,0:T(8,128)(2,1)}, s32[]{:T(128)}) while((s32[]{:T(128)}, f32[1,512]{1,0:T(1,128)S(1)}, f32[1,512]{1,0:T(1,128)S(1)}, f32[1,7168]{1,0:T(1,128)}, ...), condition=%wide.region_7.0_spmd, body=%wide.region_2.0_spmd.sunk | while | flops 58757120 | bytes 30077124 | solution.py:81
  17.1 9.1 %multiply_reduce_fusion.6 = (f32[7168]{0:T(1024)S(1)}, f32[7168]{0:T(1024)S(1)}) fusion(bf16[1,7168,512]{2,1,0:T(8,128)(2,1)} %get-tuple-element.169, f32[512]{0:T(512)S(1)} %bitcast.46, f32[512]{0:T(512)S(1)} %bitcast.47, bf16[1,7168,512]{2,1,0:T(8,128)(2,1)} %get-tuple-element.168), kind=kLoop, calls=%fused_computation.2.clone.1 | loop fusion | flops 29345792 | bytes 14741504 | tf_op jit(solution)/shard_map/while/body/eval_jaxpr/reduce_sum | solution.py:46
  26.2 2.8 %collective-permute-start = (f32[1,7168]{1,0:T(1,128)S(1)}, f32[1,7168]{1,0:T(1,128)S(1)}, u32[]{:S(2)}, u32[]{:S(2)}) collective-permute-start(f32[1,7168]{1,0:T(1,128)S(1)} %bitcast.38), channel_id=1, source_target_pairs={{0,3},{1,0},{2,1},{3,2},{4,7},{5,4},{6,5},{7,6},{8,11},{9,8},{10,9... | collective-permute-start | bytes 86024 | tf_op jit(solution)/shard_map/while/body/eval_jaxpr/ppermute | solution.py:40
  30.7 3.7 %collective-permute-done.1 = f32[1,7168]{1,0:T(1,128)S(1)} collective-permute-done((f32[1,7168]{1,0:T(1,128)S(1)}, f32[1,7168]{1,0:T(1,128)S(1)}, u32[]{:S(2)}, u32[]{:S(2)}) %collective-permute-start.1) | collective-permute-done | bytes 28704 | tf_op jit(solution)/shard_map/while/body/eval_jaxpr/ppermute | solution.py:40
  35.6 7.6 %multiply_reduce_fusion.7 = (f32[512]{0:T(512)S(1)}, f32[512]{0:T(512)S(1)}) fusion(bf16[1,7168,512]{2,1,0:T(8,128)(2,1)} %get-tuple-element.169, f32[7168]{0:T(1024)S(1)} %bitcast.37, bf16[1,7168,512]{2,1,0:T(8,128)(2,1)} %get-tuple-element.168), kind=kLoop, calls=%fused_computation.clone.1 | loop fusion | flops 29359104 | bytes 14712832 | tf_op jit(solution)/shard_map/while/body/eval_jaxpr/reduce_sum | solution.py:51
  43.2 9.1 %multiply_reduce_fusion.6 = (f32[7168]{0:T(1024)S(1)}, f32[7168]{0:T(1024)S(1)}) fusion(bf16[1,7168,512]{2,1,0:T(8,128)(2,1)} %get-tuple-element.169, f32[512]{0:T(512)S(1)} %bitcast.46, f32[512]{0:T(512)S(1)} %bitcast.47, bf16[1,7168,512]{2,1,0:T(8,128)(2,1)} %get-tuple-element.168), kind=kLoop, calls=%fused_computation.2.clone.1 | loop fusion | flops 29345792 | bytes 14741504 | tf_op jit(solution)/shard_map/while/body/eval_jaxpr/reduce_sum | solution.py:46
  52.8 1.4 collective-permute-start.1
  54.2 1.2 collective-permute-start.2
  56.3 1.9 collective-permute-done.1
  58.2 1.1 collective-permute-done.2
  59.9 7.6 %multiply_reduce_fusion.7 = (f32[512]{0:T(512)S(1)}, f32[512]{0:T(512)S(1)}) fusion(bf16[1,7168,512]{2,1,0:T(8,128)(2,1)} %get-tuple-element.169, f32[7168]{0:T(1024)S(1)} %bitcast.37, bf16[1,7168,512]{2,1,0:T(8,128)(2,1)} %get-tuple-element.168), kind=kLoop, calls=%fused_computation.clone.1 | loop fusion | flops 29359104 | bytes 14712832 | tf_op jit(solution)/shard_map/while/body/eval_jaxpr/reduce_sum | solution.py:51
  67.6 9.1 %multiply_reduce_fusion.6 = (f32[7168]{0:T(1024)S(1)}, f32[7168]{0:T(1024)S(1)}) fusion(bf16[1,7168,512]{2,1,0:T(8,128)(2,1)} %get-tuple-element.169, f32[512]{0:T(512)S(1)} %bitcast.46, f32[512]{0:T(512)S(1)} %bitcast.47, bf16[1,7168,512]{2,1,0:T(8,128)(2,1)} %get-tuple-element.168), kind=kLoop, calls=%fused_computation.2.clone.1 | loop fusion | flops 29345792 | bytes 14741504 | tf_op jit(solution)/shard_map/while/body/eval_jaxpr/reduce_sum | solution.py:46
  76.7 1.8 collective-permute-start
  79.5 1.2 collective-permute-done
  80.7 3.2 %collective-permute-done.1 = f32[1,7168]{1,0:T(1,128)S(1)} collective-permute-done((f32[1,7168]{1,0:T(1,128)S(1)}, f32[1,7168]{1,0:T(1,128)S(1)}, u32[]{:S(2)}, u32[]{:S(2)}) %collective-permute-start.1) | collective-permute-done | bytes 28704 | tf_op jit(solution)/shard_map/while/body/eval_jaxpr/ppermute | solution.py:40
  85.2 7.6 %multiply_reduce_fusion.7 = (f32[512]{0:T(512)S(1)}, f32[512]{0:T(512)S(1)}) fusion(bf16[1,7168,512]{2,1,0:T(8,128)(2,1)} %get-tuple-element.169, f32[7168]{0:T(1024)S(1)} %bitcast.37, bf16[1,7168,512]{2,1,0:T(8,128)(2,1)} %get-tuple-element.168), kind=kLoop, calls=%fused_computation.clone.1 | loop fusion | flops 29359104 | bytes 14712832 | tf_op jit(solution)/shard_map/while/body/eval_jaxpr/reduce_sum | solution.py:51
  92.9 9.1 %multiply_reduce_fusion.6 = (f32[7168]{0:T(1024)S(1)}, f32[7168]{0:T(1024)S(1)}) fusion(bf16[1,7168,512]{2,1,0:T(8,128)(2,1)} %get-tuple-element.169, f32[512]{0:T(512)S(1)} %bitcast.46, f32[512]{0:T(512)S(1)} %bitcast.47, bf16[1,7168,512]{2,1,0:T(8,128)(2,1)} %get-tuple-element.168), kind=kLoop, calls=%fused_computation.2.clone.1 | loop fusion | flops 29345792 | bytes 14741504 | tf_op jit(solution)/shard_map/while/body/eval_jaxpr/reduce_sum | solution.py:46
  103.8 1.1 collective-permute-start.2
  104.9 1.0 collective-permute-done
  105.9 2.3 %collective-permute-done.1 = f32[1,7168]{1,0:T(1,128)S(1)} collective-permute-done((f32[1,7168]{1,0:T(1,128)S(1)}, f32[1,7168]{1,0:T(1,128)S(1)}, u32[]{:S(2)}, u32[]{:S(2)}) %collective-permute-start.1) | collective-permute-done | bytes 28704 | tf_op jit(solution)/shard_map/while/body/eval_jaxpr/ppermute | solution.py:40
  109.6 7.6 %multiply_reduce_fusion.7 = (f32[512]{0:T(512)S(1)}, f32[512]{0:T(512)S(1)}) fusion(bf16[1,7168,512]{2,1,0:T(8,128)(2,1)} %get-tuple-element.169, f32[7168]{0:T(1024)S(1)} %bitcast.37, bf16[1,7168,512]{2,1,0:T(8,128)(2,1)} %get-tuple-element.168), kind=kLoop, calls=%fused_computation.clone.1 | loop fusion | flops 29359104 | bytes 14712832 | tf_op jit(solution)/shard_map/while/body/eval_jaxpr/reduce_sum | solution.py:51
  117.2 9.1 %multiply_reduce_fusion.6 = (f32[7168]{0:T(1024)S(1)}, f32[7168]{0:T(1024)S(1)}) fusion(bf16[1,7168,512]{2,1,0:T(8,128)(2,1)} %get-tuple-element.169, f32[512]{0:T(512)S(1)} %bitcast.46, f32[512]{0:T(512)S(1)} %bitcast.47, bf16[1,7168,512]{2,1,0:T(8,128)(2,1)} %get-tuple-element.168), kind=kLoop, calls=%fused_computation.2.clone.1 | loop fusion | flops 29345792 | bytes 14741504 | tf_op jit(solution)/shard_map/while/body/eval_jaxpr/reduce_sum | solution.py:46
  126.3 1.8 collective-permute-start
  130.3 3.2 %collective-permute-done.1 = f32[1,7168]{1,0:T(1,128)S(1)} collective-permute-done((f32[1,7168]{1,0:T(1,128)S(1)}, f32[1,7168]{1,0:T(1,128)S(1)}, u32[]{:S(2)}, u32[]{:S(2)}) %collective-permute-start.1) | collective-permute-done | bytes 28704 | tf_op jit(solution)/shard_map/while/body/eval_jaxpr/ppermute | solution.py:40
  134.8 7.6 %multiply_reduce_fusion.7 = (f32[512]{0:T(512)S(1)}, f32[512]{0:T(512)S(1)}) fusion(bf16[1,7168,512]{2,1,0:T(8,128)(2,1)} %get-tuple-element.169, f32[7168]{0:T(1024)S(1)} %bitcast.37, bf16[1,7168,512]{2,1,0:T(8,128)(2,1)} %get-tuple-element.168), kind=kLoop, calls=%fused_computation.clone.1 | loop fusion | flops 29359104 | bytes 14712832 | tf_op jit(solution)/shard_map/while/body/eval_jaxpr/reduce_sum | solution.py:51
  142.5 7.4 %multiply_convert_fusion.1 = (bf16[1,7168,512]{2,1,0:T(8,128)(2,1)S(1)}, bf16[1,7168,512]{2,1,0:T(8,128)(2,1)S(1)}) fusion(bf16[1,7168,512]{2,1,0:T(8,128)(2,1)} %get-tuple-element.171, f32[512]{0:T(512)S(1)} %bitcast.43, f32[7168]{0:T(1024)} %bitcast.49, f32[512]{0:T(512)S(1)} %bitcast.45, bf16[1,7168,512]{2,1,0:T(8,128)(2,1)} %get-tuple-element.172), kind=kLoop, calls=%fused_computation.13 | loop fusion | flops 29360128 | bytes 29392896 | tf_op jit(solution)/shard_map/convert_element_type | solution.py:84
  149.9 6.5 %pad_maximum_fusion = bf16[1,7168,1024]{2,1,0:T(8,128)(2,1)} fusion(bf16[1,7168,512]{2,1,0:T(8,128)(2,1)S(1)} %get-tuple-element.102, bf16[1,7168,512]{2,1,0:T(8,128)(2,1)S(1)} %get-tuple-element.101), kind=kLoop, calls=%fused_computation.9 | loop fusion | flops 29360128 | bytes 29360128 | tf_op jit(solution)/shard_map/concatenate | solution.py:88
  156.4 32.4 %all-to-all-done = bf16[32,24,7168]{2,1,0:T(8,128)(2,1)} async-done(((bf16[32,24,7168]{2,1,0:T(8,128)(2,1)}), bf16[32,24,7168]{2,1,0:T(8,128)(2,1)}, u32[]{:S(2)}, u32[]{:S(2)}) %all-to-all-start) | async-done | bytes 11010080 | tf_op jit(solution)/shard_map/all_to_all | solution.py:63
  188.8 16.5 %fusion.2 = f32[1,32,24,1024]{3,2,1,0:T(8,128)S(1)} fusion(bf16[32,24,7168]{2,1,0:T(8,128)(2,1)} %all-to-all-done, bf16[1,7168,1024]{2,1,0:T(8,128)(2,1)} %pad_maximum_fusion), kind=kOutput, calls=%fused_computation.16 | convolution fusion | flops 11274289152 | bytes 28835840 | tf_op jit(solution)/shard_map/ensd,edf->ensf/dot_general | solution.py:89
  205.4 1.4 fusion.5
  (64 shorter events, 17.1 us)
Async XLA Ops:
  0.0 3.3 %copy-start = (bf16[64,7168]{1,0:T(8,128)(2,1)S(1)}, bf16[64,7168]{1,0:T(8,128)(2,1)}, u32[]{:S(2)}) copy-start(bf16[64,7168]{1,0:T(8,128)(2,1)} %param.6) | copy-start | bytes 2752516
  8.9 179.9 %all-to-all-start = ((bf16[32,24,7168]{2,1,0:T(8,128)(2,1)}), bf16[32,24,7168]{2,1,0:T(8,128)(2,1)}, u32[]{:S(2)}, u32[]{:S(2)}) async-start(bf16[32,24,7168]{2,1,0:T(8,128)(2,1)} %convolution_convert_fusion), calls=%async_computation | async-start | bytes 22020096 | tf_op jit(solution)/shard_map/all_to_all | solution.py:63
  26.2 4.5 %collective-permute-start = (f32[1,7168]{1,0:T(1,128)S(1)}, f32[1,7168]{1,0:T(1,128)S(1)}, u32[]{:S(2)}, u32[]{:S(2)}) collective-permute-start(f32[1,7168]{1,0:T(1,128)S(1)} %bitcast.38), channel_id=1, source_target_pairs={{0,3},{1,0},{2,1},{3,2},{4,7},{5,4},{6,5},{7,6},{8,11},{9,8},{10,9... | collective-permute-start | bytes 86024 | tf_op jit(solution)/shard_map/while/body/eval_jaxpr/ppermute | solution.py:40
  29.0 5.4 %collective-permute-start.1 = (f32[1,7168]{1,0:T(1,128)S(1)}, f32[1,7168]{1,0:T(1,128)S(1)}, u32[]{:S(2)}, u32[]{:S(2)}) collective-permute-start(f32[1,7168]{1,0:T(1,128)S(1)} %bitcast.39), channel_id=1, source_target_pairs={{0,2},{1,3},{2,0},{3,1},{4,6},{5,7},{6,4},{7,5},{8,10},{9,11},{10,... | collective-permute-start | bytes 86024 | tf_op jit(solution)/shard_map/while/body/eval_jaxpr/ppermute | solution.py:40
  29.8 5.1 %collective-permute-start.2 = (f32[1,7168]{1,0:T(1,128)S(1)}, f32[1,7168]{1,0:T(1,128)S(1)}, u32[]{:S(2)}, u32[]{:S(2)}) collective-permute-start(f32[1,7168]{1,0:T(1,128)S(1)} %bitcast.40), channel_id=1, source_target_pairs={{0,1},{1,2},{2,3},{3,0},{4,5},{5,6},{6,7},{7,4},{8,9},{9,10},{10,1... | collective-permute-start | bytes 86024 | tf_op jit(solution)/shard_map/while/body/eval_jaxpr/ppermute | solution.py:40
  52.4 3.9 %collective-permute-start = (f32[1,7168]{1,0:T(1,128)S(1)}, f32[1,7168]{1,0:T(1,128)S(1)}, u32[]{:S(2)}, u32[]{:S(2)}) collective-permute-start(f32[1,7168]{1,0:T(1,128)S(1)} %bitcast.38), channel_id=1, source_target_pairs={{0,3},{1,0},{2,1},{3,2},{4,7},{5,4},{6,5},{7,6},{8,11},{9,8},{10,9... | collective-permute-start | bytes 86024 | tf_op jit(solution)/shard_map/while/body/eval_jaxpr/ppermute | solution.py:40
  52.8 5.4 %collective-permute-start.1 = (f32[1,7168]{1,0:T(1,128)S(1)}, f32[1,7168]{1,0:T(1,128)S(1)}, u32[]{:S(2)}, u32[]{:S(2)}) collective-permute-start(f32[1,7168]{1,0:T(1,128)S(1)} %bitcast.39), channel_id=1, source_target_pairs={{0,2},{1,3},{2,0},{3,1},{4,6},{5,7},{6,4},{7,5},{8,10},{9,11},{10,... | collective-permute-start | bytes 86024 | tf_op jit(solution)/shard_map/while/body/eval_jaxpr/ppermute | solution.py:40
  54.2 5.1 %collective-permute-start.2 = (f32[1,7168]{1,0:T(1,128)S(1)}, f32[1,7168]{1,0:T(1,128)S(1)}, u32[]{:S(2)}, u32[]{:S(2)}) collective-permute-start(f32[1,7168]{1,0:T(1,128)S(1)} %bitcast.40), channel_id=1, source_target_pairs={{0,1},{1,2},{2,3},{3,0},{4,5},{5,6},{6,7},{7,4},{8,9},{9,10},{10,1... | collective-permute-start | bytes 86024 | tf_op jit(solution)/shard_map/while/body/eval_jaxpr/ppermute | solution.py:40
  76.7 3.9 %collective-permute-start = (f32[1,7168]{1,0:T(1,128)S(1)}, f32[1,7168]{1,0:T(1,128)S(1)}, u32[]{:S(2)}, u32[]{:S(2)}) collective-permute-start(f32[1,7168]{1,0:T(1,128)S(1)} %bitcast.38), channel_id=1, source_target_pairs={{0,3},{1,0},{2,1},{3,2},{4,7},{5,4},{6,5},{7,6},{8,11},{9,8},{10,9... | collective-permute-start | bytes 86024 | tf_op jit(solution)/shard_map/while/body/eval_jaxpr/ppermute | solution.py:40
  78.5 5.4 %collective-permute-start.1 = (f32[1,7168]{1,0:T(1,128)S(1)}, f32[1,7168]{1,0:T(1,128)S(1)}, u32[]{:S(2)}, u32[]{:S(2)}) collective-permute-start(f32[1,7168]{1,0:T(1,128)S(1)} %bitcast.39), channel_id=1, source_target_pairs={{0,2},{1,3},{2,0},{3,1},{4,6},{5,7},{6,4},{7,5},{8,10},{9,11},{10,... | collective-permute-start | bytes 86024 | tf_op jit(solution)/shard_map/while/body/eval_jaxpr/ppermute | solution.py:40
  79.4 5.1 %collective-permute-start.2 = (f32[1,7168]{1,0:T(1,128)S(1)}, f32[1,7168]{1,0:T(1,128)S(1)}, u32[]{:S(2)}, u32[]{:S(2)}) collective-permute-start(f32[1,7168]{1,0:T(1,128)S(1)} %bitcast.40), channel_id=1, source_target_pairs={{0,1},{1,2},{2,3},{3,0},{4,5},{5,6},{6,7},{7,4},{8,9},{9,10},{10,1... | collective-permute-start | bytes 86024 | tf_op jit(solution)/shard_map/while/body/eval_jaxpr/ppermute | solution.py:40
  102.0 3.9 %collective-permute-start = (f32[1,7168]{1,0:T(1,128)S(1)}, f32[1,7168]{1,0:T(1,128)S(1)}, u32[]{:S(2)}, u32[]{:S(2)}) collective-permute-start(f32[1,7168]{1,0:T(1,128)S(1)} %bitcast.38), channel_id=1, source_target_pairs={{0,3},{1,0},{2,1},{3,2},{4,7},{5,4},{6,5},{7,6},{8,11},{9,8},{10,9... | collective-permute-start | bytes 86024 | tf_op jit(solution)/shard_map/while/body/eval_jaxpr/ppermute | solution.py:40
  102.9 5.4 %collective-permute-start.1 = (f32[1,7168]{1,0:T(1,128)S(1)}, f32[1,7168]{1,0:T(1,128)S(1)}, u32[]{:S(2)}, u32[]{:S(2)}) collective-permute-start(f32[1,7168]{1,0:T(1,128)S(1)} %bitcast.39), channel_id=1, source_target_pairs={{0,2},{1,3},{2,0},{3,1},{4,6},{5,7},{6,4},{7,5},{8,10},{9,11},{10,... | collective-permute-start | bytes 86024 | tf_op jit(solution)/shard_map/while/body/eval_jaxpr/ppermute | solution.py:40
  103.8 5.1 %collective-permute-start.2 = (f32[1,7168]{1,0:T(1,128)S(1)}, f32[1,7168]{1,0:T(1,128)S(1)}, u32[]{:S(2)}, u32[]{:S(2)}) collective-permute-start(f32[1,7168]{1,0:T(1,128)S(1)} %bitcast.40), channel_id=1, source_target_pairs={{0,1},{1,2},{2,3},{3,0},{4,5},{5,6},{6,7},{7,4},{8,9},{9,10},{10,1... | collective-permute-start | bytes 86024 | tf_op jit(solution)/shard_map/while/body/eval_jaxpr/ppermute | solution.py:40
  126.3 3.9 %collective-permute-start = (f32[1,7168]{1,0:T(1,128)S(1)}, f32[1,7168]{1,0:T(1,128)S(1)}, u32[]{:S(2)}, u32[]{:S(2)}) collective-permute-start(f32[1,7168]{1,0:T(1,128)S(1)} %bitcast.38), channel_id=1, source_target_pairs={{0,3},{1,0},{2,1},{3,2},{4,7},{5,4},{6,5},{7,6},{8,11},{9,8},{10,9... | collective-permute-start | bytes 86024 | tf_op jit(solution)/shard_map/while/body/eval_jaxpr/ppermute | solution.py:40
  128.2 5.4 %collective-permute-start.1 = (f32[1,7168]{1,0:T(1,128)S(1)}, f32[1,7168]{1,0:T(1,128)S(1)}, u32[]{:S(2)}, u32[]{:S(2)}) collective-permute-start(f32[1,7168]{1,0:T(1,128)S(1)} %bitcast.39), channel_id=1, source_target_pairs={{0,2},{1,3},{2,0},{3,1},{4,6},{5,7},{6,4},{7,5},{8,10},{9,11},{10,... | collective-permute-start | bytes 86024 | tf_op jit(solution)/shard_map/while/body/eval_jaxpr/ppermute | solution.py:40
  129.1 5.1 %collective-permute-start.2 = (f32[1,7168]{1,0:T(1,128)S(1)}, f32[1,7168]{1,0:T(1,128)S(1)}, u32[]{:S(2)}, u32[]{:S(2)}) collective-permute-start(f32[1,7168]{1,0:T(1,128)S(1)} %bitcast.40), channel_id=1, source_target_pairs={{0,1},{1,2},{2,3},{3,0},{4,5},{5,6},{6,7},{7,4},{8,9},{9,10},{10,1... | collective-permute-start | bytes 86024 | tf_op jit(solution)/shard_map/while/body/eval_jaxpr/ppermute | solution.py:40
  188.8 17.9 %copy-start.1 = (bf16[64,7168]{1,0:T(8,128)(2,1)S(1)}, bf16[64,7168]{1,0:T(8,128)(2,1)}, u32[]{:S(2)}) copy-start(bf16[64,7168]{1,0:T(8,128)(2,1)} %param.6) | copy-start | bytes 2752516

commit v8 on v5

--- a/solution.py
+++ b/solution.py
@@ -58,7 +58,7 @@
     ff_total = ff_local * lax.axis_size("hidden")
     my_index = lax.axis_index("expert")
     tok_local = tokens.shape[0]
-    block_ids = lax.dynamic_slice_in_dim(expert_ids, my_index * tok_local, tok_local, 0)
+    block_ids = expert_ids.reshape(-1, tok_local, expert_ids.shape[1])[my_index]
     outgoing = dispatch_rows(block_ids, tokens)
     routed = lax.all_to_all(outgoing, "expert", split_axis=0, concat_axis=0, tiled=True)[None]
     def sweep(_, carry):

time: 206 us -> 206 us (level)
  no operation moved by 1% of the time
where the time goes in v8:
time: 206 us
  other arithmetic  103 us (50%)
  waiting for transfers between devices  54.4 us (26%)
  starting transfers between devices  24.1 us (12%)
  matrix products  22.5 us (11%)
    reduce_sum x5, other arithmetic, row_terms(): return jnp.sum(values * values * cols_sq[:, None, :], axis=2)  45.5 us
    reduce_sum x5, other arithmetic, col_terms(): return jnp.sum(values * values * scale_sq[:, :, None], axis=1)  37.9 us
    all_to_all x1, waiting for transfers between devices, shards(): lax.all_to_all(outgoing, 'expert', split_axis=0, concat_axis=0, tiled=True)  32.4 us
    ppermute x15, waiting for transfers between devices, hidden_sum(): lax.ppermute(values, 'hidden', [(i, (i + shift) % n) for i in range(n)])  22 us
    dot_general x1, matrix products, shards(): jnp.einsum('ensd,edf->ensf', routed, both_eq, preferred_element_type=jnp....  16.6 us
    ppermute x15, starting transfers between devices, hidden_sum(): lax.ppermute(values, 'hidden', [(i, (i + shift) % n) for i in range(n)])  16.1 us
    all_to_all x1, starting transfers between devices, shards(): lax.all_to_all(outgoing, 'expert', split_axis=0, concat_axis=0, tiled=True)  8.03 us
    convert_element_type x1, other arithmetic, shards(): gate_eq = (gate_weight.astype(jnp.float32) * row_scale[:, :, None] * gate...  7.45 us
  transfers between devices with their start and end apart: 16, of which 15 were waited for; matrix products, arithmetic and copies ran while one was open for 49% of the time, Pallas kernels for 0%

profile of v8, /device:TPU:48, one launch (start us, length us, event | category | flops | bytes accessed | tf_op | source)
XLA Modules:
  0.0 206.2 jit_solution(9830663822656071508)
XLA Ops:
  2.7 5.7 %convolution_convert_fusion = bf16[32,24,7168]{2,1,0:T(8,128)(2,1)} fusion(pred[32,24,64]{2,1,0:T(8,128)(4,1)S(1)} %and_reduce_fusion, bf16[64,7168]{1,0:T(8,128)(2,1)S(1)} %copy-done), kind=kOutput, calls=%fused_computation.14 | convolution fusion | flops 710148096 | bytes 11976704 | tf_op jit(solution)/shard_map/est,td->esd/dot_general | solution.py:32
  8.4 8.0 %all-to-all-start = ((bf16[32,24,7168]{2,1,0:T(8,128)(2,1)}), bf16[32,24,7168]{2,1,0:T(8,128)(2,1)}, u32[]{:S(2)}, u32[]{:S(2)}) async-start(bf16[32,24,7168]{2,1,0:T(8,128)(2,1)} %convolution_convert_fusion), calls=%async_computation | async-start | bytes 22020096 | tf_op jit(solution)/shard_map/all_to_all | solution.py:63
  16.5 125.4 %while.16 = (s32[]{:T(128)}, f32[1,512]{1,0:T(1,128)S(1)}, f32[1,512]{1,0:T(1,128)S(1)}, f32[1,7168]{1,0:T(1,128)}, bf16[1,7168,512]{2,1,0:T(8,128)(2,1)}, /*index=5*/bf16[1,7168,512]{2,1,0:T(8,128)(2,1)}, s32[]{:T(128)}) while((s32[]{:T(128)}, f32[1,512]{1,0:T(1,128)S(1)}, f32[1,512]{1,0:T(1,128)S(1)}, f32[1,7168]{1,0:T(1,128)}, ...), condition=%wide.region_7.0_spmd, body=%wide.region_2.0_spmd.sunk | while | flops 58757120 | bytes 30077124 | solution.py:81
  16.5 9.1 %multiply_reduce_fusion.6 = (f32[7168]{0:T(1024)S(1)}, f32[7168]{0:T(1024)S(1)}) fusion(bf16[1,7168,512]{2,1,0:T(8,128)(2,1)} %get-tuple-element.169, f32[512]{0:T(512)S(1)} %bitcast.46, f32[512]{0:T(512)S(1)} %bitcast.47, bf16[1,7168,512]{2,1,0:T(8,128)(2,1)} %get-tuple-element.168), kind=kLoop, calls=%fused_computation.2.clone.1 | loop fusion | flops 29345792 | bytes 14741504 | tf_op jit(solution)/shard_map/while/body/eval_jaxpr/reduce_sum | solution.py:46
  25.6 2.8 %collective-permute-start = (f32[1,7168]{1,0:T(1,128)S(1)}, f32[1,7168]{1,0:T(1,128)S(1)}, u32[]{:S(2)}, u32[]{:S(2)}) collective-permute-start(f32[1,7168]{1,0:T(1,128)S(1)} %bitcast.38), channel_id=1, source_target_pairs={{0,3},{1,0},{2,1},{3,2},{4,7},{5,4},{6,5},{7,6},{8,11},{9,8},{10,9... | collective-permute-start | bytes 86024 | tf_op jit(solution)/shard_map/while/body/eval_jaxpr/ppermute | solution.py:40
  30.2 3.7 %collective-permute-done.1 = f32[1,7168]{1,0:T(1,128)S(1)} collective-permute-done((f32[1,7168]{1,0:T(1,128)S(1)}, f32[1,7168]{1,0:T(1,128)S(1)}, u32[]{:S(2)}, u32[]{:S(2)}) %collective-permute-start.1) | collective-permute-done | bytes 28704 | tf_op jit(solution)/shard_map/while/body/eval_jaxpr/ppermute | solution.py:40
  35.0 7.6 %multiply_reduce_fusion.7 = (f32[512]{0:T(512)S(1)}, f32[512]{0:T(512)S(1)}) fusion(bf16[1,7168,512]{2,1,0:T(8,128)(2,1)} %get-tuple-element.169, f32[7168]{0:T(1024)S(1)} %bitcast.37, bf16[1,7168,512]{2,1,0:T(8,128)(2,1)} %get-tuple-element.168), kind=kLoop, calls=%fused_computation.clone.1 | loop fusion | flops 29359104 | bytes 14712832 | tf_op jit(solution)/shard_map/while/body/eval_jaxpr/reduce_sum | solution.py:51
  42.7 9.1 %multiply_reduce_fusion.6 = (f32[7168]{0:T(1024)S(1)}, f32[7168]{0:T(1024)S(1)}) fusion(bf16[1,7168,512]{2,1,0:T(8,128)(2,1)} %get-tuple-element.169, f32[512]{0:T(512)S(1)} %bitcast.46, f32[512]{0:T(512)S(1)} %bitcast.47, bf16[1,7168,512]{2,1,0:T(8,128)(2,1)} %get-tuple-element.168), kind=kLoop, calls=%fused_computation.2.clone.1 | loop fusion | flops 29345792 | bytes 14741504 | tf_op jit(solution)/shard_map/while/body/eval_jaxpr/reduce_sum | solution.py:46
  52.2 1.4 collective-permute-start.1
  53.6 1.2 collective-permute-start.2
  55.7 1.9 collective-permute-done.1
  57.6 1.1 collective-permute-done.2
  59.4 7.6 %multiply_reduce_fusion.7 = (f32[512]{0:T(512)S(1)}, f32[512]{0:T(512)S(1)}) fusion(bf16[1,7168,512]{2,1,0:T(8,128)(2,1)} %get-tuple-element.169, f32[7168]{0:T(1024)S(1)} %bitcast.37, bf16[1,7168,512]{2,1,0:T(8,128)(2,1)} %get-tuple-element.168), kind=kLoop, calls=%fused_computation.clone.1 | loop fusion | flops 29359104 | bytes 14712832 | tf_op jit(solution)/shard_map/while/body/eval_jaxpr/reduce_sum | solution.py:51
  67.0 9.1 %multiply_reduce_fusion.6 = (f32[7168]{0:T(1024)S(1)}, f32[7168]{0:T(1024)S(1)}) fusion(bf16[1,7168,512]{2,1,0:T(8,128)(2,1)} %get-tuple-element.169, f32[512]{0:T(512)S(1)} %bitcast.46, f32[512]{0:T(512)S(1)} %bitcast.47, bf16[1,7168,512]{2,1,0:T(8,128)(2,1)} %get-tuple-element.168), kind=kLoop, calls=%fused_computation.2.clone.1 | loop fusion | flops 29345792 | bytes 14741504 | tf_op jit(solution)/shard_map/while/body/eval_jaxpr/reduce_sum | solution.py:46
  76.2 1.8 collective-permute-start
  78.9 1.2 collective-permute-done
  80.1 3.2 %collective-permute-done.1 = f32[1,7168]{1,0:T(1,128)S(1)} collective-permute-done((f32[1,7168]{1,0:T(1,128)S(1)}, f32[1,7168]{1,0:T(1,128)S(1)}, u32[]{:S(2)}, u32[]{:S(2)}) %collective-permute-start.1) | collective-permute-done | bytes 28704 | tf_op jit(solution)/shard_map/while/body/eval_jaxpr/ppermute | solution.py:40
  84.6 7.6 %multiply_reduce_fusion.7 = (f32[512]{0:T(512)S(1)}, f32[512]{0:T(512)S(1)}) fusion(bf16[1,7168,512]{2,1,0:T(8,128)(2,1)} %get-tuple-element.169, f32[7168]{0:T(1024)S(1)} %bitcast.37, bf16[1,7168,512]{2,1,0:T(8,128)(2,1)} %get-tuple-element.168), kind=kLoop, calls=%fused_computation.clone.1 | loop fusion | flops 29359104 | bytes 14712832 | tf_op jit(solution)/shard_map/while/body/eval_jaxpr/reduce_sum | solution.py:51
  92.3 9.1 %multiply_reduce_fusion.6 = (f32[7168]{0:T(1024)S(1)}, f32[7168]{0:T(1024)S(1)}) fusion(bf16[1,7168,512]{2,1,0:T(8,128)(2,1)} %get-tuple-element.169, f32[512]{0:T(512)S(1)} %bitcast.46, f32[512]{0:T(512)S(1)} %bitcast.47, bf16[1,7168,512]{2,1,0:T(8,128)(2,1)} %get-tuple-element.168), kind=kLoop, calls=%fused_computation.2.clone.1 | loop fusion | flops 29345792 | bytes 14741504 | tf_op jit(solution)/shard_map/while/body/eval_jaxpr/reduce_sum | solution.py:46
  103.2 1.1 collective-permute-start.2
  104.3 1.0 collective-permute-done
  105.4 2.3 %collective-permute-done.1 = f32[1,7168]{1,0:T(1,128)S(1)} collective-permute-done((f32[1,7168]{1,0:T(1,128)S(1)}, f32[1,7168]{1,0:T(1,128)S(1)}, u32[]{:S(2)}, u32[]{:S(2)}) %collective-permute-start.1) | collective-permute-done | bytes 28704 | tf_op jit(solution)/shard_map/while/body/eval_jaxpr/ppermute | solution.py:40
  109.0 7.6 %multiply_reduce_fusion.7 = (f32[512]{0:T(512)S(1)}, f32[512]{0:T(512)S(1)}) fusion(bf16[1,7168,512]{2,1,0:T(8,128)(2,1)} %get-tuple-element.169, f32[7168]{0:T(1024)S(1)} %bitcast.37, bf16[1,7168,512]{2,1,0:T(8,128)(2,1)} %get-tuple-element.168), kind=kLoop, calls=%fused_computation.clone.1 | loop fusion | flops 29359104 | bytes 14712832 | tf_op jit(solution)/shard_map/while/body/eval_jaxpr/reduce_sum | solution.py:51
  116.7 9.1 %multiply_reduce_fusion.6 = (f32[7168]{0:T(1024)S(1)}, f32[7168]{0:T(1024)S(1)}) fusion(bf16[1,7168,512]{2,1,0:T(8,128)(2,1)} %get-tuple-element.169, f32[512]{0:T(512)S(1)} %bitcast.46, f32[512]{0:T(512)S(1)} %bitcast.47, bf16[1,7168,512]{2,1,0:T(8,128)(2,1)} %get-tuple-element.168), kind=kLoop, calls=%fused_computation.2.clone.1 | loop fusion | flops 29345792 | bytes 14741504 | tf_op jit(solution)/shard_map/while/body/eval_jaxpr/reduce_sum | solution.py:46
  125.8 1.8 collective-permute-start
  129.7 3.2 %collective-permute-done.1 = f32[1,7168]{1,0:T(1,128)S(1)} collective-permute-done((f32[1,7168]{1,0:T(1,128)S(1)}, f32[1,7168]{1,0:T(1,128)S(1)}, u32[]{:S(2)}, u32[]{:S(2)}) %collective-permute-start.1) | collective-permute-done | bytes 28704 | tf_op jit(solution)/shard_map/while/body/eval_jaxpr/ppermute | solution.py:40
  134.3 7.6 %multiply_reduce_fusion.7 = (f32[512]{0:T(512)S(1)}, f32[512]{0:T(512)S(1)}) fusion(bf16[1,7168,512]{2,1,0:T(8,128)(2,1)} %get-tuple-element.169, f32[7168]{0:T(1024)S(1)} %bitcast.37, bf16[1,7168,512]{2,1,0:T(8,128)(2,1)} %get-tuple-element.168), kind=kLoop, calls=%fused_computation.clone.1 | loop fusion | flops 29359104 | bytes 14712832 | tf_op jit(solution)/shard_map/while/body/eval_jaxpr/reduce_sum | solution.py:51
  141.9 7.4 %multiply_convert_fusion.1 = (bf16[1,7168,512]{2,1,0:T(8,128)(2,1)S(1)}, bf16[1,7168,512]{2,1,0:T(8,128)(2,1)S(1)}) fusion(bf16[1,7168,512]{2,1,0:T(8,128)(2,1)} %get-tuple-element.171, f32[512]{0:T(512)S(1)} %bitcast.43, f32[7168]{0:T(1024)} %bitcast.49, f32[512]{0:T(512)S(1)} %bitcast.45, bf16[1,7168,512]{2,1,0:T(8,128)(2,1)} %get-tuple-element.172), kind=kLoop, calls=%fused_computation.13 | loop fusion | flops 29360128 | bytes 29392896 | tf_op jit(solution)/shard_map/convert_element_type | solution.py:84
  149.3 6.5 %pad_maximum_fusion = bf16[1,7168,1024]{2,1,0:T(8,128)(2,1)} fusion(bf16[1,7168,512]{2,1,0:T(8,128)(2,1)S(1)} %get-tuple-element.102, bf16[1,7168,512]{2,1,0:T(8,128)(2,1)S(1)} %get-tuple-element.101), kind=kLoop, calls=%fused_computation.9 | loop fusion | flops 29360128 | bytes 29360128 | tf_op jit(solution)/shard_map/concatenate | solution.py:88
  155.9 32.4 %all-to-all-done = bf16[32,24,7168]{2,1,0:T(8,128)(2,1)} async-done(((bf16[32,24,7168]{2,1,0:T(8,128)(2,1)}), bf16[32,24,7168]{2,1,0:T(8,128)(2,1)}, u32[]{:S(2)}, u32[]{:S(2)}) %all-to-all-start) | async-done | bytes 11010080 | tf_op jit(solution)/shard_map/all_to_all | solution.py:63
  188.3 16.6 %fusion.2 = f32[1,32,24,1024]{3,2,1,0:T(8,128)S(1)} fusion(bf16[32,24,7168]{2,1,0:T(8,128)(2,1)} %all-to-all-done, bf16[1,7168,1024]{2,1,0:T(8,128)(2,1)} %pad_maximum_fusion), kind=kOutput, calls=%fused_computation.16 | convolution fusion | flops 11274289152 | bytes 28835840 | tf_op jit(solution)/shard_map/ensd,edf->ensf/dot_general | solution.py:89
  204.8 1.4 fusion.5
  (64 shorter events, 16.6 us)
Async XLA Ops:
  0.0 2.7 %copy-start = (bf16[64,7168]{1,0:T(8,128)(2,1)S(1)}, bf16[64,7168]{1,0:T(8,128)(2,1)}, u32[]{:S(2)}) copy-start(bf16[64,7168]{1,0:T(8,128)(2,1)} %param.6) | copy-start | bytes 2752516
  8.4 179.9 %all-to-all-start = ((bf16[32,24,7168]{2,1,0:T(8,128)(2,1)}), bf16[32,24,7168]{2,1,0:T(8,128)(2,1)}, u32[]{:S(2)}, u32[]{:S(2)}) async-start(bf16[32,24,7168]{2,1,0:T(8,128)(2,1)} %convolution_convert_fusion), calls=%async_computation | async-start | bytes 22020096 | tf_op jit(solution)/shard_map/all_to_all | solution.py:63
  25.6 4.6 %collective-permute-start = (f32[1,7168]{1,0:T(1,128)S(1)}, f32[1,7168]{1,0:T(1,128)S(1)}, u32[]{:S(2)}, u32[]{:S(2)}) collective-permute-start(f32[1,7168]{1,0:T(1,128)S(1)} %bitcast.38), channel_id=1, source_target_pairs={{0,3},{1,0},{2,1},{3,2},{4,7},{5,4},{6,5},{7,6},{8,11},{9,8},{10,9... | collective-permute-start | bytes 86024 | tf_op jit(solution)/shard_map/while/body/eval_jaxpr/ppermute | solution.py:40
  28.4 5.4 %collective-permute-start.1 = (f32[1,7168]{1,0:T(1,128)S(1)}, f32[1,7168]{1,0:T(1,128)S(1)}, u32[]{:S(2)}, u32[]{:S(2)}) collective-permute-start(f32[1,7168]{1,0:T(1,128)S(1)} %bitcast.39), channel_id=1, source_target_pairs={{0,2},{1,3},{2,0},{3,1},{4,6},{5,7},{6,4},{7,5},{8,10},{9,11},{10,... | collective-permute-start | bytes 86024 | tf_op jit(solution)/shard_map/while/body/eval_jaxpr/ppermute | solution.py:40
  29.2 5.1 %collective-permute-start.2 = (f32[1,7168]{1,0:T(1,128)S(1)}, f32[1,7168]{1,0:T(1,128)S(1)}, u32[]{:S(2)}, u32[]{:S(2)}) collective-permute-start(f32[1,7168]{1,0:T(1,128)S(1)} %bitcast.40), channel_id=1, source_target_pairs={{0,1},{1,2},{2,3},{3,0},{4,5},{5,6},{6,7},{7,4},{8,9},{9,10},{10,1... | collective-permute-start | bytes 86024 | tf_op jit(solution)/shard_map/while/body/eval_jaxpr/ppermute | solution.py:40
  51.8 3.9 %collective-permute-start = (f32[1,7168]{1,0:T(1,128)S(1)}, f32[1,7168]{1,0:T(1,128)S(1)}, u32[]{:S(2)}, u32[]{:S(2)}) collective-permute-start(f32[1,7168]{1,0:T(1,128)S(1)} %bitcast.38), channel_id=1, source_target_pairs={{0,3},{1,0},{2,1},{3,2},{4,7},{5,4},{6,5},{7,6},{8,11},{9,8},{10,9... | collective-permute-start | bytes 86024 | tf_op jit(solution)/shard_map/while/body/eval_jaxpr/ppermute | solution.py:40
  52.2 5.4 %collective-permute-start.1 = (f32[1,7168]{1,0:T(1,128)S(1)}, f32[1,7168]{1,0:T(1,128)S(1)}, u32[]{:S(2)}, u32[]{:S(2)}) collective-permute-start(f32[1,7168]{1,0:T(1,128)S(1)} %bitcast.39), channel_id=1, source_target_pairs={{0,2},{1,3},{2,0},{3,1},{4,6},{5,7},{6,4},{7,5},{8,10},{9,11},{10,... | collective-permute-start | bytes 86024 | tf_op jit(solution)/shard_map/while/body/eval_jaxpr/ppermute | solution.py:40
  53.6 5.1 %collective-permute-start.2 = (f32[1,7168]{1,0:T(1,128)S(1)}, f32[1,7168]{1,0:T(1,128)S(1)}, u32[]{:S(2)}, u32[]{:S(2)}) collective-permute-start(f32[1,7168]{1,0:T(1,128)S(1)} %bitcast.40), channel_id=1, source_target_pairs={{0,1},{1,2},{2,3},{3,0},{4,5},{5,6},{6,7},{7,4},{8,9},{9,10},{10,1... | collective-permute-start | bytes 86024 | tf_op jit(solution)/shard_map/while/body/eval_jaxpr/ppermute | solution.py:40
  76.2 3.9 %collective-permute-start = (f32[1,7168]{1,0:T(1,128)S(1)}, f32[1,7168]{1,0:T(1,128)S(1)}, u32[]{:S(2)}, u32[]{:S(2)}) collective-permute-start(f32[1,7168]{1,0:T(1,128)S(1)} %bitcast.38), channel_id=1, source_target_pairs={{0,3},{1,0},{2,1},{3,2},{4,7},{5,4},{6,5},{7,6},{8,11},{9,8},{10,9... | collective-permute-start | bytes 86024 | tf_op jit(solution)/shard_map/while/body/eval_jaxpr/ppermute | solution.py:40
  78.0 5.4 %collective-permute-start.1 = (f32[1,7168]{1,0:T(1,128)S(1)}, f32[1,7168]{1,0:T(1,128)S(1)}, u32[]{:S(2)}, u32[]{:S(2)}) collective-permute-start(f32[1,7168]{1,0:T(1,128)S(1)} %bitcast.39), channel_id=1, source_target_pairs={{0,2},{1,3},{2,0},{3,1},{4,6},{5,7},{6,4},{7,5},{8,10},{9,11},{10,... | collective-permute-start | bytes 86024 | tf_op jit(solution)/shard_map/while/body/eval_jaxpr/ppermute | solution.py:40
  78.9 5.1 %collective-permute-start.2 = (f32[1,7168]{1,0:T(1,128)S(1)}, f32[1,7168]{1,0:T(1,128)S(1)}, u32[]{:S(2)}, u32[]{:S(2)}) collective-permute-start(f32[1,7168]{1,0:T(1,128)S(1)} %bitcast.40), channel_id=1, source_target_pairs={{0,1},{1,2},{2,3},{3,0},{4,5},{5,6},{6,7},{7,4},{8,9},{9,10},{10,1... | collective-permute-start | bytes 86024 | tf_op jit(solution)/shard_map/while/body/eval_jaxpr/ppermute | solution.py:40
  101.4 3.9 %collective-permute-start = (f32[1,7168]{1,0:T(1,128)S(1)}, f32[1,7168]{1,0:T(1,128)S(1)}, u32[]{:S(2)}, u32[]{:S(2)}) collective-permute-start(f32[1,7168]{1,0:T(1,128)S(1)} %bitcast.38), channel_id=1, source_target_pairs={{0,3},{1,0},{2,1},{3,2},{4,7},{5,4},{6,5},{7,6},{8,11},{9,8},{10,9... | collective-permute-start | bytes 86024 | tf_op jit(solution)/shard_map/while/body/eval_jaxpr/ppermute | solution.py:40
  102.3 5.4 %collective-permute-start.1 = (f32[1,7168]{1,0:T(1,128)S(1)}, f32[1,7168]{1,0:T(1,128)S(1)}, u32[]{:S(2)}, u32[]{:S(2)}) collective-permute-start(f32[1,7168]{1,0:T(1,128)S(1)} %bitcast.39), channel_id=1, source_target_pairs={{0,2},{1,3},{2,0},{3,1},{4,6},{5,7},{6,4},{7,5},{8,10},{9,11},{10,... | collective-permute-start | bytes 86024 | tf_op jit(solution)/shard_map/while/body/eval_jaxpr/ppermute | solution.py:40
  103.2 5.1 %collective-permute-start.2 = (f32[1,7168]{1,0:T(1,128)S(1)}, f32[1,7168]{1,0:T(1,128)S(1)}, u32[]{:S(2)}, u32[]{:S(2)}) collective-permute-start(f32[1,7168]{1,0:T(1,128)S(1)} %bitcast.40), channel_id=1, source_target_pairs={{0,1},{1,2},{2,3},{3,0},{4,5},{5,6},{6,7},{7,4},{8,9},{9,10},{10,1... | collective-permute-start | bytes 86024 | tf_op jit(solution)/shard_map/while/body/eval_jaxpr/ppermute | solution.py:40
  125.8 3.9 %collective-permute-start = (f32[1,7168]{1,0:T(1,128)S(1)}, f32[1,7168]{1,0:T(1,128)S(1)}, u32[]{:S(2)}, u32[]{:S(2)}) collective-permute-start(f32[1,7168]{1,0:T(1,128)S(1)} %bitcast.38), channel_id=1, source_target_pairs={{0,3},{1,0},{2,1},{3,2},{4,7},{5,4},{6,5},{7,6},{8,11},{9,8},{10,9... | collective-permute-start | bytes 86024 | tf_op jit(solution)/shard_map/while/body/eval_jaxpr/ppermute | solution.py:40
  127.6 5.4 %collective-permute-start.1 = (f32[1,7168]{1,0:T(1,128)S(1)}, f32[1,7168]{1,0:T(1,128)S(1)}, u32[]{:S(2)}, u32[]{:S(2)}) collective-permute-start(f32[1,7168]{1,0:T(1,128)S(1)} %bitcast.39), channel_id=1, source_target_pairs={{0,2},{1,3},{2,0},{3,1},{4,6},{5,7},{6,4},{7,5},{8,10},{9,11},{10,... | collective-permute-start | bytes 86024 | tf_op jit(solution)/shard_map/while/body/eval_jaxpr/ppermute | solution.py:40
  128.5 5.1 %collective-permute-start.2 = (f32[1,7168]{1,0:T(1,128)S(1)}, f32[1,7168]{1,0:T(1,128)S(1)}, u32[]{:S(2)}, u32[]{:S(2)}) collective-permute-start(f32[1,7168]{1,0:T(1,128)S(1)} %bitcast.40), channel_id=1, source_target_pairs={{0,1},{1,2},{2,3},{3,0},{4,5},{5,6},{6,7},{7,4},{8,9},{9,10},{10,1... | collective-permute-start | bytes 86024 | tf_op jit(solution)/shard_map/while/body/eval_jaxpr/ppermute | solution.py:40
  188.2 18.0 %copy-start.1 = (bf16[64,7168]{1,0:T(8,128)(2,1)S(1)}, bf16[64,7168]{1,0:T(8,128)(2,1)}, u32[]{:S(2)}) copy-start(bf16[64,7168]{1,0:T(8,128)(2,1)} %param.6) | copy-start | bytes 2752516
